TPU v7x, 128 devices: a whole 4x4x4 slice. The times are simulated.
128 devices in a mesh: req: 2 (over core), seq: 64 (over z, y, x).
Axes of the slice: x: 4, y: 4, z: 4, core: 2. Of those that a mesh axis runs over, the one named last changes fastest.
Arguments:
- tokens: bfloat16 [4, 128, 1536], P(None, ('req', 'seq')), may hold values from -6 to 6
- lengths: int32 [128], P('req'), may hold values from 1 to 16384, as said below
- k_cache: bfloat16 [128, 4096, 256], P('req', 'seq'), may hold values from -500 to 500
- v_cache: bfloat16 [128, 4096, 256], P('req', 'seq'), may hold values from -12 to 12
- attn_gain: bfloat16 [1536], replicated, may hold values from 0.5 to 1.5
- w_qkv: bfloat16 [1536, 2048], replicated, may hold values from -0.15625 to 0.15625
- sink: float32 [12], replicated, may hold values from -1 to 3
- w_out: bfloat16 [1536, 1536], replicated, may hold values from -0.15625 to 0.15625
- moe_gain: bfloat16 [1536], replicated, may hold values from 0.5 to 1.5
- router: bfloat16 [1536, 32], replicated, may hold values from -0.15625 to 0.15625
- w_gate: bfloat16 [1536, 24576], P(None, ('req', 'seq')), may hold values from -0.15625 to 0.15625
- w_up: bfloat16 [1536, 24576], P(None, ('req', 'seq')), may hold values from -0.15625 to 0.15625
- w_down: bfloat16 [24576, 1536], P(('req', 'seq')), may hold values from -0.21875 to 0.21875
- routes: int32 [128, 4, 4], replicated, may hold values from 0 to 31, all different within a row; in each aligned block of 4 rows (0 to 3, 4 to 7, ..., all dimensions but the last counted through in order) at most 2 rows name the same one
Outputs:
- outputs: bfloat16 [4, 128, 1536], P(None, ('req', 'seq'))
Inputs may be any that keep to these rules, and one draw needn't show every extreme that they name: Each request has lengths positions before the first step; some request has all 16384 in every draw. `routes`: among the 4 tokens of one device's requests (requests 1 d .. 1 d + 1 - 1, all steps), no expert is named by more than 2 tokens, and in every draw some expert is named by exactly 2.
All inputs are finite; a program needn't handle non-finite values.
Results may differ from a plain program's by a relative error of at most 0.02.
Values may be sent and summed in bfloat16 or wider, within the bound.
No kernel may reach another device: no remote copies, remote signals or barrier semaphores. Data moves between devices by JAX's collectives and lax.ppermute only.
A program may use at most 512 MiB of HBM per device.

v0:
```python
import jax
import jax.numpy as jnp
from jax import lax
from jax.sharding import PartitionSpec as P

D = 1536
QH = 12
KVH = 2
HD = 128
E = 32
EFF = 768
TOP = 4
STEPS = 4
MOST = 2


def combined_all(value, axis, join):
    gathered = jax.tree.map(
        lambda a, kind: lax.all_gather(a.astype(kind), axis),
        value,
        (jnp.bfloat16, jnp.bfloat16, jnp.bfloat16),
    )

    def take(source):
        return jax.tree.map(
            lambda a, own: lax.dynamic_index_in_dim(a, source, 0, False).astype(own.dtype),
            gathered,
            value,
        )

    return lax.fori_loop(
        1, lax.axis_size(axis), lambda source, state: join(state, take(source)), take(0)
    )


def normalize(x, gain):
    xf = x.astype(jnp.float32)
    inv = lax.rsqrt(jnp.mean(xf * xf, axis=-1, keepdims=True) + 1e-05)
    return (xf * inv * gain.astype(jnp.float32)).astype(jnp.bfloat16)


def rotate(x, place):
    half = x.shape[-1] // 2
    index = jnp.arange(half, dtype=jnp.float32)
    inverse = jnp.exp(-jnp.log(1000000.0) * 2.0 * index / x.shape[-1])
    angle = place.astype(jnp.float32)[..., None, None] * inverse
    first = x[..., :half]
    second = x[..., half:]
    cosine = jnp.cos(angle)
    sine = jnp.sin(angle)
    return jnp.concatenate(
        [first * cosine - second * sine, second * cosine + first * sine], axis=-1
    )


def route_weights(logits, picks):
    onehot = (picks[:, :, None] == jnp.arange(E, dtype=jnp.int32)[None, None, :]).astype(
        jnp.float32
    )
    chosen = jnp.sum(onehot * logits[:, None, :], axis=-1)
    share = jax.nn.softmax(chosen, axis=-1)
    return jnp.sum(share[:, :, None] * onehot, axis=1)


def combine_parts(first, second):
    peak = jnp.maximum(first[0], second[0])
    left_scale = jnp.exp(first[0] - peak)
    right_scale = jnp.exp(second[0] - peak)
    return (
        peak,
        first[1] * left_scale + second[1] * right_scale,
        first[2] * left_scale[..., None] + second[2] * right_scale[..., None],
    )


def on_device(
    tokens,
    lengths,
    k_cache,
    v_cache,
    attn_gain,
    w_qkv,
    sink,
    w_out,
    moe_gain,
    router,
    w_gate,
    w_up,
    w_down,
    routes,
):
    seq_count = lax.axis_size("seq")
    seq_place = lax.axis_index("seq")
    device = lax.axis_index("req") * seq_count + seq_place
    devices = lax.axis_size(("req", "seq"))
    rows = tokens.shape[1]
    group_rows = lengths.shape[0]
    local_pos = k_cache.shape[1]
    window = local_pos * seq_count
    heads_per = QH // KVH
    scale = HD ** (-0.5)
    columns = w_gate.shape[1]
    expert_mine = device * columns // EFF
    own_len = lax.dynamic_slice_in_dim(lengths, seq_place * rows, rows)
    step_ids = jnp.arange(STEPS, dtype=jnp.int32)
    a = normalize(tokens, attn_gain)
    proj = jnp.einsum("srm,mn->srn", a, w_qkv, preferred_element_type=jnp.float32)
    place = own_len[None, :] + step_ids[:, None]
    query = rotate(proj[..., : QH * HD].reshape(STEPS, rows, QH, HD), place).astype(jnp.bfloat16)
    fresh_key = rotate(
        proj[..., QH * HD : (QH + KVH) * HD].reshape(STEPS, rows, KVH, HD), place
    ).astype(jnp.bfloat16)
    fresh_val = proj[..., (QH + KVH) * HD :].reshape(STEPS, rows, KVH, HD).astype(jnp.bfloat16)
    every_query = lax.all_gather(query.reshape(STEPS, rows, QH * HD), "seq", axis=1, tiled=True)
    grouped_all = every_query.reshape(STEPS, group_rows, KVH, heads_per, HD)
    cache_keys = k_cache.reshape(group_rows, local_pos, KVH, HD)
    cache_vals = v_cache.reshape(group_rows, local_pos, KVH, HD)
    scores = (
        jnp.einsum("tnkgd,nckd->tnkgc", grouped_all, cache_keys, preferred_element_type=jnp.float32)
        * scale
    )
    key_slot = seq_place * local_pos + jnp.arange(local_pos, dtype=jnp.int32)
    back = jnp.mod(lengths[None, :, None] - 1 - key_slot[None, None, :], window)
    reach = jnp.minimum(lengths[None, :, None], window - 1 - step_ids[:, None, None])
    valid = (back < reach)[:, :, None, None, :]
    peak_local = jnp.max(jnp.where(valid, scores, -1e30), axis=-1)
    weights = jnp.where(valid, jnp.exp(scores - peak_local[..., None]), 0.0)
    total_local = jnp.sum(weights, axis=-1)
    mixed_local = jnp.einsum(
        "tnkgc,nckd->tnkgd",
        weights.astype(jnp.bfloat16),
        cache_vals,
        preferred_element_type=jnp.float32,
    )
    peak_all, total_all, mixed_all = combined_all(
        (peak_local, total_local, mixed_local), "seq", combine_parts
    )
    peak = lax.dynamic_slice_in_dim(peak_all, seq_place * rows, rows, 1)
    total = lax.dynamic_slice_in_dim(total_all, seq_place * rows, rows, 1)
    mixed = lax.dynamic_slice_in_dim(mixed_all, seq_place * rows, rows, 1)
    grouped = query.reshape(STEPS, rows, KVH, heads_per, HD)
    tail_scores = (
        jnp.einsum("trkgd,srkd->trkgs", grouped, fresh_key, preferred_element_type=jnp.float32)
        * scale
    )
    tail_valid = (step_ids[None, :] <= step_ids[:, None])[:, None, None, None, :]
    sink_grid = sink.reshape(KVH, heads_per)[None, None]
    final = jnp.maximum(
        jnp.maximum(peak, jnp.max(jnp.where(tail_valid, tail_scores, -1e30), axis=-1)), sink_grid
    )
    shift = jnp.exp(peak - final)
    tail_w = jnp.where(tail_valid, jnp.exp(tail_scores - final[..., None]), 0.0)
    denom = total * shift + jnp.sum(tail_w, axis=-1) + jnp.exp(sink_grid - final)
    mixed = mixed * shift[..., None] + jnp.einsum(
        "trkgs,srkd->trkgd",
        tail_w.astype(jnp.bfloat16),
        fresh_val,
        preferred_element_type=jnp.float32,
    )
    attn = (mixed / denom[..., None]).reshape(STEPS, rows, QH * HD).astype(jnp.bfloat16)
    h = (
        tokens.astype(jnp.float32)
        + jnp.einsum("srn,nm->srm", attn, w_out, preferred_element_type=jnp.float32)
    ).astype(jnp.bfloat16)
    u = normalize(h, moe_gain)
    own_tokens = rows * STEPS
    u_tok = u.transpose(1, 0, 2).reshape(own_tokens, D)
    every_row = lax.all_gather(u_tok, ("req", "seq"), axis=0, tiled=True)
    all_picks = routes.reshape(-1, TOP)
    every_logit = jnp.dot(every_row, router, preferred_element_type=jnp.float32)
    dense_all = route_weights(every_logit, all_picks)
    weight_mine = jnp.sum(
        dense_all * (jnp.arange(E, dtype=jnp.int32) == expert_mine)[None, :].astype(jnp.float32),
        axis=-1,
    )
    mine = jnp.any(all_picks == expert_mine, axis=-1)
    slot = jnp.cumsum(mine.astype(jnp.int32)) - 1
    limit = MOST * devices
    select = (
        (slot[None, :] == jnp.arange(limit, dtype=jnp.int32)[:, None]) & mine[None, :]
    ).astype(jnp.float32)
    picked = jnp.dot(
        select.astype(jnp.bfloat16), every_row, preferred_element_type=jnp.float32
    ).astype(jnp.bfloat16)
    slot_weight = jnp.dot(select, weight_mine, precision=lax.Precision.HIGHEST)
    hidden = (
        jax.nn.relu(jnp.dot(picked, w_gate, preferred_element_type=jnp.float32))
        * jnp.dot(picked, w_up, preferred_element_type=jnp.float32)
    ).astype(jnp.bfloat16)
    produced = jnp.dot(hidden, w_down, preferred_element_type=jnp.float32) * slot_weight[:, None]
    moe = lax.psum_scatter(
        jnp.einsum("lc,lm->cm", select, produced, precision=lax.Precision.HIGHEST),
        ("req", "seq"),
        scatter_dimension=0,
        tiled=True,
    )
    moe_steps = moe.reshape(rows, STEPS, D).transpose(1, 0, 2)
    return (h.astype(jnp.float32) + moe_steps).astype(jnp.bfloat16)


def solution(mesh):
    in_specs = (
        P(None, ("req", "seq"), None),
        P("req"),
        P("req", "seq", None),
        P("req", "seq", None),
        P(),
        P(),
        P(),
        P(),
        P(),
        P(),
        P(None, ("req", "seq")),
        P(None, ("req", "seq")),
        P(("req", "seq"), None),
        P(),
    )
    out_specs = P(None, ("req", "seq"), None)
    return jax.shard_map(
        on_device, mesh=mesh, in_specs=in_specs, out_specs=out_specs, check_vma=False
    )
```

profile of v0, /device:TPU:1, one launch (start us, length us, event | category | flops | bytes accessed | tf_op | source)
XLA Modules:
  0.0 1043.7 jit_solution(8082044500679967716)
XLA Ops:
  8.2 3.9 convolution_bitcast_fusion.1
  17.0 155.1 %all_gather.20 = bf16[4,64,1536]{2,0,1:T(4,128)(2,1)S(1)} all-gather(bf16[4,1,1536]{2,0,1:T(4,128)(2,1)S(1)} %convert_element_type.198), channel_id=1, replica_groups=mesh['req'=2,'seq'=64] {'seq'}, dimensions={1}, use_global_device_ids=true | all-gather | bytes 798720 | tf_op jit(solution)/shard_map/all_gather | solution.py:114
  175.9 3.4 fusion.8
  184.5 149.0 %all-gather = bf16[256,64,2,6]{1,2,3,0:T(2,128)(2,1)S(1)} all-gather(bf16[4,64,2,6]{1,2,3,0:T(2,128)(2,1)S(1)} %copy.158), channel_id=2, replica_groups=mesh['req'=2,'seq'=64] {'seq'}, dimensions={0}, use_global_device_ids=true | all-gather | bytes 399360 | tf_op jit(solution)/shard_map/all_gather | solution.py:19
  333.5 156.4 %all-gather.1 = bf16[256,64,2,6]{1,2,3,0:T(2,128)(2,1)S(1)} all-gather(bf16[4,64,2,6]{1,2,3,0:T(2,128)(2,1)S(1)} %copy.160), channel_id=3, replica_groups=mesh['req'=2,'seq'=64] {'seq'}, dimensions={0}, use_global_device_ids=true | all-gather | bytes 399360 | tf_op jit(solution)/shard_map/all_gather | solution.py:19
  490.9 40.0 %all-gather.7.cloned.1.call-done = bf16[256,64,2,6,128]{4,3,0,2,1:T(8,128)(2,1)} async-done(((bf16[4,64,2,6,128]{4,3,0,2,1:T(8,128)(2,1)}), bf16[256,64,2,6,128]{4,3,0,2,1:T(8,128)(2,1)}) %all-gather.7.cloned.1.call-update) | async-done | bytes 50331664 | tf_op jit(solution)/shard_map/all_gather | solution.py:19
  532.5 233.8 %while.19 = (s32[]{:T(128)}, f32[4,64,2,6]{1,2,3,0:T(2,128)S(1)}, f32[4,64,2,6]{1,2,3,0:T(2,128)S(1)}, f32[4,64,2,6,128]{4,3,2,1,0:T(8,128)S(1)}, bf16[64,4,64,2...) while((s32[]{:T(128)}, f32[4,64,2,6]{1,2,3,0:T(2,128)S(1)}, ...), condition=%wide.region_4.5_spmd, body=%wide.region_3.4_spmd.sunk | while | flops 1597445 | bytes 4354199 | solution.py:31
  533.7 2.5 fusion.101
  537.4 2.5 fusion.101
  541.1 2.5 fusion.101
  544.9 2.5 fusion.101
  548.6 2.5 fusion.101
  552.3 2.5 fusion.101
  556.0 2.5 fusion.101
  559.7 2.5 fusion.101
  563.4 2.5 fusion.101
  567.1 2.5 fusion.101
  570.8 2.5 fusion.101
  619.1 2.5 fusion.101
  689.6 2.5 fusion.101
  768.0 3.2 multiply_reduce_fusion.1
  773.7 100.2 %all-gather.9.cloned.1.call-done = bf16[512,1,1536]{2,1,0:T(2,128)(2,1)} async-done(((bf16[4,1,1536]{2,1,0:T(2,128)(2,1)}), bf16[512,1,1536]{2,1,0:T(2,128)(2,1)}) %all-gather.9.cloned.1.call-update) | async-done | bytes 1572880 | tf_op jit(solution)/shard_map/all_gather | solution.py:168
  882.2 3.3 fusion.38
  885.5 150.3 %all-reduce.3.cloned.1.call-done = f32[512,1536]{1,0:T(8,128)} async-done(((f32[512,1536]{1,0:T(8,128)}), f32[512,1536]{1,0:T(8,128)}) %all-reduce.3.cloned.1.call-update) | async-done | bytes 3145744
  (355 shorter events, 230.3 us)
Async XLA Ops:
  6.5 873.4 %copy-start = (bf16[192,1536]{1,0:T(8,128)(2,1)S(1)}, bf16[192,1536]{1,0:T(8,128)(2,1)}, u32[]{:S(2)}) copy-start(bf16[192,1536]{1,0:T(8,128)(2,1)} %param.28) | copy-start | bytes 1769476
  6.5 524.3 %all-gather.7.cloned.1.call-start = ((), (), s32[]{:S(2)}) async-start(), calls=%async_computation | async-start | bytes 68157440 | tf_op jit(solution)/shard_map/all_gather | solution.py:19
  8.2 4.6 copy-start.12
  8.2 6.5 copy-start.1
  12.1 0.6 copy-start.8
  16.7 156.9 %copy-start.2 = (bf16[64,64,256]{2,1,0:T(8,128)(2,1)S(1)}, bf16[64,64,256]{2,1,0:T(8,128)(2,1)}, u32[]{:S(2)}) copy-start(bf16[64,64,256]{2,1,0:T(8,128)(2,1)} %param.19) | copy-start | bytes 6291460
  173.6 2.1 copy-start.7
  175.9 3.4 copy-start.3
  181.4 1.9 copy-start.14
  181.4 2.0 copy-start.11
  181.5 692.5 %all-gather.9.cloned.1.call-start = ((), (), s32[]{:S(2)}) async-start(), calls=%async_computation.1 | async-start | bytes 3170304 | tf_op jit(solution)/shard_map/all_gather | solution.py:168
  333.5 156.5 %copy-start.4 = (bf16[256,64,2,6]{1,2,3,0:T(2,128)(2,1)}, bf16[256,64,2,6]{1,2,3,0:T(2,128)(2,1)S(1)}, u32[]{:S(2)}) copy-start(bf16[256,64,2,6]{1,2,3,0:T(2,128)(2,1)S(1)} %all-gather) | copy-start | bytes 1179652
  489.9 0.9 copy-start.5
  532.5 235.5 %copy-start.9 = (bf16[4,1,1536]{2,0,1:T(4,128)(2,1)S(1)}, bf16[4,1,1536]{2,0,1:T(4,128)(2,1)}, u32[]{:S(2)}) copy-start(bf16[4,1,1536]{2,0,1:T(4,128)(2,1)} %param.16) | copy-start | bytes 36868
  768.0 4.2 copy-start.10
  768.0 105.9 %copy-start.13 = (bf16[1536,32]{0,1:T(8,128)(2,1)S(1)}, bf16[1536,32]{0,1:T(8,128)(2,1)}, u32[]{:S(2)}) copy-start(bf16[1536,32]{0,1:T(8,128)(2,1)} %param.25) | copy-start | bytes 294916
  772.0 263.8 %all-reduce.3.cloned.1.call-start = ((), (), s32[]{:S(2)}) async-start(), calls=%async_computation.2 | async-start | bytes 6291456
  876.4 3.1 copy-start.6
Sparse Core Ops, SparseCore 0:
  181.6 349.2 all-gather.6
  772.1 101.7 all-gather.8
  885.6 150.1 all-reduce.2
where the time goes:
time: 1050 us; the launch traced here: 1040 us
  blocking collectives  461 us (44%)
  waiting for transfers between devices  291 us (28%)
  other arithmetic  218 us (21%)
  local copies, waits for them, and re-layouts  33.8 us (3%)
  matrix products  25 us (2%)
  between operations  13.6 us (1%)
    all_gather x2, blocking collectives, combined_all(): lax.all_gather(a.astype(kind), axis)  305 us
    add x63, other arithmetic, combine_parts(): first[2] * left_scale[..., None] + second[2] * right_scale[..., None]  159 us
    all_gather x1, blocking collectives, on_device(): lax.all_gather(query.reshape(STEPS, rows, QH * HD), 'seq', axis=1, tiled=...  155 us
    unnamed x4, waiting for transfers between devices  150 us
    all_gather x1, waiting for transfers between devices, on_device(): every_row = lax.all_gather(u_tok, ('req', 'seq'), axis=0, tiled=True)  100 us
    add x63, other arithmetic, combine_parts(): first[1] * left_scale + second[1] * right_scale  49.8 us
    all_gather x1, waiting for transfers between devices, combined_all(): lax.all_gather(a.astype(kind), axis)  40 us
  transfers between devices with their start and end apart: 3, of which 3 were waited for; matrix products, arithmetic and copies ran while one was open for 0% of the time, Pallas kernels for 0%

commit v1 on v0

v1 whole, which is shorter than its diff:
```python
import jax
import jax.numpy as jnp
from jax import lax
from jax.sharding import PartitionSpec as P

D = 1536
QH = 12
KVH = 2
HD = 128
E = 32
EFF = 768
TOP = 4
STEPS = 4
MOST = 2


def normalize(x, gain):
    xf = x.astype(jnp.float32)
    inv = lax.rsqrt(jnp.mean(xf * xf, axis=-1, keepdims=True) + 1e-05)
    return (xf * inv * gain.astype(jnp.float32)).astype(jnp.bfloat16)


def rotate(x, place):
    half = x.shape[-1] // 2
    index = jnp.arange(half, dtype=jnp.float32)
    inverse = jnp.exp(-jnp.log(1000000.0) * 2.0 * index / x.shape[-1])
    angle = place.astype(jnp.float32)[..., None, None] * inverse
    first = x[..., :half]
    second = x[..., half:]
    cosine = jnp.cos(angle)
    sine = jnp.sin(angle)
    return jnp.concatenate(
        [first * cosine - second * sine, second * cosine + first * sine], axis=-1
    )


def on_device(
    tokens,
    lengths,
    k_cache,
    v_cache,
    attn_gain,
    w_qkv,
    sink,
    w_out,
    moe_gain,
    router,
    w_gate,
    w_up,
    w_down,
    routes,
):
    seq_count = lax.axis_size("seq")
    seq_place = lax.axis_index("seq")
    devices = lax.axis_size(("req", "seq"))
    device = lax.axis_index("req") * seq_count + seq_place
    group_rows = lengths.shape[0]
    local_pos = k_cache.shape[1]
    window = local_pos * seq_count
    heads_per = QH // KVH
    scale = HD ** (-0.5)
    heads_steps = STEPS * QH
    step_ids = jnp.arange(STEPS, dtype=jnp.int32)

    x = tokens[:, 0, :]
    own_len = lax.dynamic_index_in_dim(lengths, seq_place, 0, False)
    with jax.named_scope("qkv_projection"):
        a = normalize(x, attn_gain)
        proj = jnp.dot(a, w_qkv, preferred_element_type=jnp.float32)
        place = own_len + step_ids
        query = rotate(proj[:, : QH * HD].reshape(STEPS, QH, HD), place).astype(jnp.bfloat16)
        fresh_key = rotate(
            proj[:, QH * HD : (QH + KVH) * HD].reshape(STEPS, KVH, HD), place
        ).astype(jnp.bfloat16)
        fresh_val = proj[:, (QH + KVH) * HD :].reshape(STEPS, KVH, HD).astype(jnp.bfloat16)

    with jax.named_scope("query_exchange"):
        sent_q = jnp.broadcast_to(query.reshape(1, STEPS * QH * HD), (seq_count, STEPS * QH * HD))
        every_query = lax.all_to_all(sent_q, "seq", 0, 0, tiled=True)
    grouped_all = every_query.reshape(group_rows, STEPS, KVH, heads_per, HD)

    with jax.named_scope("slot_attention"):
        cache_keys = k_cache.reshape(group_rows, local_pos, KVH, HD)
        cache_vals = v_cache.reshape(group_rows, local_pos, KVH, HD)
        scores = (
            jnp.einsum("ntkgd,nckd->ntkgc", grouped_all, cache_keys, preferred_element_type=jnp.float32)
            * scale
        )
        key_slot = seq_place * local_pos + jnp.arange(local_pos, dtype=jnp.int32)
        back = jnp.mod(lengths[:, None, None] - 1 - key_slot[None, None, :], window)
        reach = jnp.minimum(lengths[:, None, None], window - 1 - step_ids[None, :, None])
        valid = (back < reach)[:, :, None, None, :]
        peak_local = jnp.max(jnp.where(valid, scores, -1e30), axis=-1)
        weights = jnp.where(valid, jnp.exp(scores - peak_local[..., None]), 0.0)
        total_local = jnp.sum(weights, axis=-1)
        mixed_local = jnp.einsum(
            "ntkgc,nckd->ntkgd",
            weights.astype(jnp.bfloat16),
            cache_vals,
            preferred_element_type=jnp.float32,
        )
        stats = jnp.concatenate(
            [
                total_local.reshape(group_rows, heads_steps),
                peak_local.reshape(group_rows, heads_steps),
                jnp.zeros((group_rows, HD - 2 * heads_steps), jnp.float32),
            ],
            axis=-1,
        )
        packed = jnp.concatenate(
            [mixed_local.reshape(group_rows, heads_steps, HD), stats[:, None, :]], axis=1
        )

    with jax.named_scope("partial_exchange"):
        parts = lax.all_to_all(packed, "seq", 0, 0, tiled=True)

    with jax.named_scope("merge_attention"):
        mixed_s = parts[:, :heads_steps, :].reshape(seq_count, STEPS, KVH, heads_per, HD)
        total_s = parts[:, heads_steps, :heads_steps].reshape(seq_count, STEPS, KVH, heads_per)
        peak_s = parts[:, heads_steps, heads_steps : 2 * heads_steps].reshape(
            seq_count, STEPS, KVH, heads_per
        )
        grouped = query.reshape(STEPS, KVH, heads_per, HD)
        tail_scores = (
            jnp.einsum("tkgd,skd->tkgs", grouped, fresh_key, preferred_element_type=jnp.float32)
            * scale
        )
        tail_valid = (step_ids[None, :] <= step_ids[:, None])[:, None, None, :]
        sink_grid = sink.reshape(KVH, heads_per)[None]
        final = jnp.maximum(
            jnp.maximum(jnp.max(peak_s, axis=0), jnp.max(jnp.where(tail_valid, tail_scores, -1e30), axis=-1)),
            sink_grid,
        )
        shift = jnp.exp(peak_s - final[None])
        tail_w = jnp.where(tail_valid, jnp.exp(tail_scores - final[..., None]), 0.0)
        denom = (
            jnp.sum(total_s * shift, axis=0)
            + jnp.sum(tail_w, axis=-1)
            + jnp.exp(sink_grid - final)
        )
        mixed = jnp.sum(mixed_s * shift[..., None], axis=0) + jnp.einsum(
            "tkgs,skd->tkgd",
            tail_w.astype(jnp.bfloat16),
            fresh_val,
            preferred_element_type=jnp.float32,
        )
        attn = (mixed / denom[..., None]).reshape(STEPS, QH * HD).astype(jnp.bfloat16)

    with jax.named_scope("attention_output"):
        h = (
            x.astype(jnp.float32) + jnp.dot(attn, w_out, preferred_element_type=jnp.float32)
        ).astype(jnp.bfloat16)
        u = normalize(h, moe_gain)

    with jax.named_scope("route"):
        picks = lax.dynamic_index_in_dim(routes, device, 0, False)
        experts = jnp.arange(E, dtype=jnp.int32)
        onehot = (picks[:, :, None] == experts[None, None, :]).astype(jnp.float32)
        logits = jnp.dot(u, router, preferred_element_type=jnp.float32)
        chosen = jnp.sum(onehot * logits[:, None, :], axis=-1)
        share = jax.nn.softmax(chosen, axis=-1)
        weight_te = jnp.sum(share[:, :, None] * onehot, axis=1)
        named = jnp.any(picks[:, :, None] == experts[None, None, :], axis=1)
        rank = jnp.cumsum(named.astype(jnp.int32), axis=0) - 1
        slots = jnp.arange(MOST, dtype=jnp.int32)
        select = (named[:, :, None] & (rank[:, :, None] == slots[None, None, :])).astype(jnp.float32)
        dispatch = jnp.einsum(
            "tej,tm->ejm", select.astype(jnp.bfloat16), u, preferred_element_type=jnp.float32
        ).astype(jnp.bfloat16)
        per_device = devices // E
        sent_u = jnp.broadcast_to(
            dispatch[:, None], (E, per_device, MOST, D)
        ).reshape(devices, MOST, D)

    with jax.named_scope("token_dispatch"):
        arrived = lax.all_to_all(sent_u, ("req", "seq"), 0, 0, tiled=True)

    with jax.named_scope("expert_quarter"):
        rows_in = arrived.reshape(devices * MOST, D)
        hidden = (
            jax.nn.relu(jnp.dot(rows_in, w_gate, preferred_element_type=jnp.float32))
            * jnp.dot(rows_in, w_up, preferred_element_type=jnp.float32)
        ).astype(jnp.bfloat16)
        produced = jnp.dot(hidden, w_down, preferred_element_type=jnp.float32).reshape(
            devices, MOST, D
        )

    with jax.named_scope("expert_return"):
        returned = lax.all_to_all(produced, ("req", "seq"), 0, 0, tiled=True)

    with jax.named_scope("expert_sum"):
        by_expert = jnp.sum(returned.reshape(E, per_device, MOST, D), axis=1)
        mix = (weight_te[:, :, None] * select).reshape(STEPS, E * MOST)
        moe = jnp.dot(
            mix, by_expert.reshape(E * MOST, D), precision=lax.Precision.HIGHEST,
            preferred_element_type=jnp.float32,
        )
        out = (h.astype(jnp.float32) + moe).astype(jnp.bfloat16)
    return out[:, None, :]


def solution(mesh):
    in_specs = (
        P(None, ("req", "seq"), None),
        P("req"),
        P("req", "seq", None),
        P("req", "seq", None),
        P(),
        P(),
        P(),
        P(),
        P(),
        P(),
        P(None, ("req", "seq")),
        P(None, ("req", "seq")),
        P(("req", "seq"), None),
        P(),
    )
    out_specs = P(None, ("req", "seq"), None)
    return jax.shard_map(
        on_device, mesh=mesh, in_specs=in_specs, out_specs=out_specs, check_vma=False
    )
```

time: 1050 us -> 160 us (0.15)
  blocking collectives: 461 us -> 22.8 us
  waiting for transfers between devices: 291 us -> 53.6 us
  other arithmetic: 218 us -> 19.2 us
  starting transfers between devices: 0.27 us -> 21.7 us
  between operations: 13.6 us -> 0.44 us
    all_gather x3 -> x0, blocking collectives: 461 us -> none  [the longest x2 305 us: combined_all(): lax.all_gather(a.astype(kind), axis)]
    add x126 -> x1, other arithmetic: 209 us -> 0.01 us  [on_device(): jnp.sum(total_s * shift, axis=0) + jnp.sum(tail_w, axis=-1)]
    unnamed x4 -> x0, waiting for transfers between devices: 150 us -> none
    all_gather x2 -> x0, waiting for transfers between devices: 140 us -> none  [the longest x1 100 us: on_device(): every_row = lax.all_gather(u_tok, ('req', 'seq'), axis=0, tiled=True)]
    all_to_all x0 -> x3, waiting for transfers between devices: none -> 53.6 us  [the longest x1 23.2 us: on_device(): parts = lax.all_to_all(packed, 'seq', 0, 0, tiled=True)]
    all_to_all x0 -> x1, blocking collectives: none -> 22.8 us  [on_device(): arrived = lax.all_to_all(sent_u, ('req', 'seq'), 0, 0, tiled=True)]
    exp x126 -> x0, local copies, waits for them, and re-layouts: 22.6 us -> none  [the longest x63 11.5 us: combine_parts(): left_scale = jnp.exp(first[0] - peak)]
    all_to_all x0 -> x3, starting transfers between devices: none -> 21.7 us  [the longest x1 12.1 us: on_device(): every_query = lax.all_to_all(sent_q, 'seq', 0, 0, tiled=True)]
  transfers between devices with their start and end apart: 3 -> 3, of which waited for: 3 -> 3; matrix products, arithmetic and copies ran while one was open for 0% -> 6% of each run, Pallas kernels for 0% -> 0%
where the time goes in v1:
time: 160 us
  waiting for transfers between devices  53.6 us (34%)
  local copies, waits for them, and re-layouts  23.3 us (15%)
  blocking collectives  22.8 us (14%)
  starting transfers between devices  21.7 us (14%)
  other arithmetic  19.2 us (12%)
  matrix products  18.5 us (12%)
    all_to_all x1, waiting for transfers between devices, on_device(): parts = lax.all_to_all(packed, 'seq', 0, 0, tiled=True)  23.2 us
    all_to_all x1, blocking collectives, on_device(): arrived = lax.all_to_all(sent_u, ('req', 'seq'), 0, 0, tiled=True)  22.8 us
    all_to_all x1, waiting for transfers between devices, on_device(): returned = lax.all_to_all(produced, ('req', 'seq'), 0, 0, tiled=True)  22.6 us
    all_to_all x1, starting transfers between devices, on_device(): every_query = lax.all_to_all(sent_q, 'seq', 0, 0, tiled=True)  12.1 us
    all_to_all x1, waiting for transfers between devices, on_device(): every_query = lax.all_to_all(sent_q, 'seq', 0, 0, tiled=True)  7.8 us
    all_to_all x1, other arithmetic, on_device(): every_query = lax.all_to_all(sent_q, 'seq', 0, 0, tiled=True)  5.76 us
    broadcast_in_dim x1, other arithmetic, on_device(): jnp.broadcast_to(query.reshape(1, STEPS * QH * HD), (seq_count, STEPS * Q...  5.35 us
    all_to_all x1, starting transfers between devices, on_device(): parts = lax.all_to_all(packed, 'seq', 0, 0, tiled=True)  5.04 us
  transfers between devices with their start and end apart: 3, of which 3 were waited for; matrix products, arithmetic and copies ran while one was open for 6% of the time, Pallas kernels for 0%

profile of v1, /device:TPU:1, one launch (start us, length us, event | category | flops | bytes accessed | tf_op | source)
XLA Modules:
  0.0 159.5 jit_solution(1468867788270816918)
XLA Ops:
  0.0 1.3 dynamic_slice.8
  3.5 3.8 %fusion.39 = f32[4,2048]{1,0:T(4,128)S(1)} fusion(bf16[1536,2048]{1,0:T(8,128)(2,1)} %param.19, bf16[4,1,1536]{2,0,1:T(4,128)(2,1)} %param.14, f32[1536]{0:T(1024)S(1)} %convert_element_type.85, f32[4]{0:T(128)S(1)} %add_rsqrt_fusion.1), kind=kOutput, calls=%fused_computation.67 | convolution fusion | flops 25190400 | bytes 6342672 | tf_op jit(solution)/shard_map/qkv_projection/dot_general | solution.py:69
  9.5 5.4 %reduce.6 = bf16[64,6144]{1,0:T(8,128)(2,1)S(1)} reduce(bf16[64,1,6144]{2,1,0:T(2,128)(2,1)S(1)} %broadcast_in_dim.49, bf16[]{:T(256)} %broadcast.272), dimensions={1}, to_apply=%broadcast_in_dim.49.reduce_sub_computation | reduce | bytes 1572866 | tf_op jit(solution)/shard_map/query_exchange/broadcast_in_dim | solution.py:78
  14.9 1.5 reshape.378
  16.4 12.1 %all-to-all-start = ((bf16[64,2,3072]{2,1,0:T(2,128)(2,1)}), bf16[64,2,3072]{2,1,0:T(2,128)(2,1)S(1)}, u32[]{:S(2)}, u32[]{:S(2)}) async-start(bf16[64,2,3072]{2,1,0:T(2,128)(2,1)} %reshape.378), calls=%async_computation | async-start | bytes 1572864 | tf_op jit(solution)/shard_map/query_exchange/all_to_all | solution.py:79
  28.6 2.6 %reshape.359 = bf16[64,64,2,128]{3,2,1,0:T(2,128)(2,1)S(1)} reshape(bf16[64,64,256]{2,1,0:T(8,128)(2,1)} %param.16) | data formatting | bytes 4194304 | tf_op jit(solution)/shard_map/slot_attention/reshape | solution.py:83
  31.1 4.0 %reshape.360 = bf16[64,64,2,128]{3,2,1,0:T(2,128)(2,1)} reshape(bf16[64,64,256]{2,1,0:T(8,128)(2,1)} %param.17) | data formatting | bytes 4194304 | tf_op jit(solution)/shard_map/slot_attention/reshape | solution.py:84
  35.5 7.8 %all-to-all-done = bf16[64,2,3072]{2,1,0:T(2,128)(2,1)S(1)} async-done(((bf16[64,2,3072]{2,1,0:T(2,128)(2,1)}), bf16[64,2,3072]{2,1,0:T(2,128)(2,1)S(1)}, u32[]{:S(2)}, u32[]{:S(2)}) %all-to-all-start) | async-done | bytes 786464 | tf_op jit(solution)/shard_map/query_exchange/all_to_all | solution.py:79
  43.3 2.0 %reshape.379 = bf16[64,1,6144]{2,1,0:T(2,128)(2,1)} reshape(bf16[64,2,3072]{2,1,0:T(2,128)(2,1)S(1)} %all-to-all-done) | data formatting | bytes 1572864
  45.2 5.8 %reduce.3 = bf16[64,6144]{1,0:T(8,128)(2,1)S(1)} reduce(bf16[64,1,6144]{2,1,0:T(2,128)(2,1)} %reshape.379, bf16[]{:T(256)} %constant.77), dimensions={1}, to_apply=%all_to_all.13.reduce_sub_computation | reduce | bytes 1572866 | tf_op jit(solution)/shard_map/query_exchange/all_to_all | solution.py:79
  51.0 2.0 %reshape.358 = bf16[64,4,2,6,128]{4,3,2,1,0:T(8,128)(2,1)} reshape(bf16[64,6144]{1,0:T(8,128)(2,1)S(1)} %reduce.3) | data formatting | bytes 1572864 | tf_op jit(solution)/shard_map/reshape | solution.py:80
  53.0 3.8 %fusion.7 = (f32[64,4,2,6]{3,1,2,0:T(4,128)S(1)}, f32[64,2,4,6,64]{4,3,2,1,0:T(8,128)}) fusion(pred[64,4,64]{2,1,0:T(4,128)(4,1)S(1)} %broadcast_compare_fusion, bf16[64,64,2,128,1]{3,2,1,0,4:T(2,128)(2,1)S(1)} %bitcast.89, bf16[64,4,2,6,128]{4,3,2,1,0:T(8,128)(2,1)} %reshape.358), kind=kOutput, calls=%fused_computation.12 | convolution fusion | flops 50918400 | bytes 3698688 | tf_op jit(solution)/shard_map/slot_attention/ntkgd,nckd->ntkgc/dot_general | solution.py:86
  57.0 2.8 %fusion.15 = f32[64,4,2,6]{3,1,2,0:T(4,128)S(1)} fusion(f32[64,2,4,6,64]{4,3,2,1,0:T(8,128)} %get-tuple-element.14, f32[64,4,2,6]{3,1,2,0:T(4,128)S(1)} %get-tuple-element.13, pred[64,4,64]{2,1,0:T(4,128)(4,1)S(1)} %broadcast_compare_fusion), kind=kLoop, calls=%fused_computation.19 | loop fusion | flops 783360 | bytes 827392 | tf_op jit(solution)/shard_map/slot_attention/reduce_sum | solution.py:95
  59.8 2.5 %fusion.12 = f32[64,4,2,6,128]{4,3,1,2,0:T(8,128)S(1)} fusion(bf16[64,64,2,128,1]{3,2,1,0,4:T(2,128)(2,1)} %bitcast.92, f32[64,2,4,6,64]{4,3,2,1,0:T(8,128)S(1)} %copy-done.1, f32[64,4,2,6]{3,1,2,0:T(4,128)S(1)} %get-tuple-element.13, pred[64,4,64]{2,1,0:T(4,128)(4,1)S(1)} %broadcast_compare_fusion), kind=kOutput, calls=%fused_computation.17 | convolution fusion | flops 51118080 | bytes 4485120 | tf_op jit(solution)/shard_map/slot_attention/ntkgc,nckd->ntkgd/dot_general | solution.py:96
  63.8 2.2 %copy.75 = f32[64,49,128]{2,1,0:T(8,128)} copy(f32[64,49,128]{2,0,1:T(8,128)S(1)} %pad_maximum_fusion) | data formatting | bytes 3211264 | tf_op jit(solution)/shard_map/slot_attention/concatenate | solution.py:110
  66.0 5.0 %all-to-all-start.1 = ((f32[64,49,128]{2,1,0:T(8,128)}), f32[64,49,128]{2,1,0:T(8,128)S(1)}, u32[]{:S(2)}, u32[]{:S(2)}) async-start(f32[64,49,128]{2,1,0:T(8,128)} %copy.75), calls=%async_computation.1 | async-start | bytes 3670016 | tf_op jit(solution)/shard_map/partial_exchange/all_to_all | solution.py:115
  72.8 23.2 %all-to-all-done.1 = f32[64,49,128]{2,1,0:T(8,128)S(1)} async-done(((f32[64,49,128]{2,1,0:T(8,128)}), f32[64,49,128]{2,1,0:T(8,128)S(1)}, u32[]{:S(2)}, u32[]{:S(2)}) %all-to-all-start.1) | async-done | bytes 1605664 | tf_op jit(solution)/shard_map/partial_exchange/all_to_all | solution.py:115
  98.1 3.2 %multiply_reduce_fusion = (f32[4]{0:T(128)S(1)}, f32[4,1536]{1,0:T(4,128)S(1)}) fusion(bf16[4,1536]{1,0:T(4,128)(2,1)S(1)} %convert_element_type.93, bf16[1536,1536]{1,0:T(8,128)(2,1)} %param.21, bf16[4,1,1536]{2,0,1:T(4,128)(2,1)S(1)} %copy-done.4), kind=kOutput, calls=%fused_computation.59 | convolution fusion | flops 18911228 | bytes 4767760 | tf_op jit(solution)/shard_map/attention_output/dot_general | solution.py:151
  102.2 22.8 %all_to_all.21 = bf16[128,2,1536]{2,1,0:T(2,128)(2,1)S(1)} all-to-all(bf16[128,2,1536]{2,1,0:T(2,128)(2,1)S(1)} %bitcast.91), channel_id=1, replica_groups=mesh['req'=2,'seq'=64] {'req','seq'}, dimensions={0} | all-to-all | bytes 1572864 | tf_op jit(solution)/shard_map/token_dispatch/all_to_all | solution.py:176
  125.7 2.2 %fusion.19 = f32[256,1536]{1,0:T(8,128)S(1)} fusion(bf16[192,1536]{1,0:T(8,128)(2,1)S(1)} %copy-done, f32[256,192]{0,1:T(8,128)S(1)} %convolution_maximum_fusion, bf16[256,1536]{1,0:T(8,128)(2,1)S(1)} %reshape.366, bf16[1536,192]{0,1:T(8,128)(2,1)} %param.25), kind=kOutput, calls=%fused_computation.27 | convolution fusion | flops 302088192 | bytes 3735552 | tf_op jit(solution)/shard_map/expert_quarter/dot_general | solution.py:184
  128.0 2.1 %reshape.367 = f32[128,2,1536]{2,1,0:T(2,128)} reshape(f32[256,1536]{1,0:T(8,128)S(1)} %fusion.19) | data formatting | bytes 3145728 | tf_op jit(solution)/shard_map/expert_quarter/reshape | solution.py:184
  130.1 4.5 %all-to-all-start.3 = ((f32[128,2,1536]{2,1,0:T(2,128)}), f32[128,2,1536]{2,1,0:T(2,128)S(1)}, u32[]{:S(2)}, u32[]{:S(2)}) async-start(f32[128,2,1536]{2,1,0:T(2,128)} %reshape.367), calls=%async_computation.3 | async-start | bytes 3145728 | tf_op jit(solution)/shard_map/expert_return/all_to_all | solution.py:189
  135.5 22.6 %all-to-all-done.3 = f32[128,2,1536]{2,1,0:T(2,128)S(1)} async-done(((f32[128,2,1536]{2,1,0:T(2,128)}), f32[128,2,1536]{2,1,0:T(2,128)S(1)}, u32[]{:S(2)}, u32[]{:S(2)}) %all-to-all-start.3) | async-done | bytes 1572896 | tf_op jit(solution)/shard_map/expert_return/all_to_all | solution.py:189
  158.6 1.0 fusion.4
  (95 shorter events, 13.1 us)
Async XLA Ops:
  0.0 125.7 %copy-start = (bf16[192,1536]{1,0:T(8,128)(2,1)S(1)}, bf16[192,1536]{1,0:T(8,128)(2,1)}, u32[]{:S(2)}) copy-start(bf16[192,1536]{1,0:T(8,128)(2,1)} %param.26) | copy-start | bytes 1769476
  7.3 0.6 copy-start.3
  14.9 13.7 %copy-start.7 = (s32[64]{0:T(128)S(1)}, s32[64]{0:T(128)}, u32[]{:S(2)}) copy-start(s32[64]{0:T(128)} %param.15) | copy-start | bytes 772
  16.4 26.9 %all-to-all-start = ((bf16[64,2,3072]{2,1,0:T(2,128)(2,1)}), bf16[64,2,3072]{2,1,0:T(2,128)(2,1)S(1)}, u32[]{:S(2)}, u32[]{:S(2)}) async-start(bf16[64,2,3072]{2,1,0:T(2,128)(2,1)} %reshape.378), calls=%async_computation | async-start | bytes 1572864 | tf_op jit(solution)/shard_map/query_exchange/all_to_all | solution.py:79
  56.8 2.9 %copy-start.1 = (f32[64,2,4,6,64]{4,3,2,1,0:T(8,128)S(1)}, f32[64,2,4,6,64]{4,3,2,1,0:T(8,128)}, u32[]{:S(2)}) copy-start(f32[64,2,4,6,64]{4,3,2,1,0:T(8,128)} %get-tuple-element.14) | copy-start | bytes 2359300
  66.0 5.1 %copy-start.9 = (f32[12]{0:T(128)S(1)}, f32[12]{0:T(128)}, u32[]{:S(2)}) copy-start(f32[12]{0:T(128)} %param.20) | copy-start | bytes 148
  66.0 6.4 %copy-start.6 = (bf16[1536]{0:T(1024)(128)(2,1)S(1)}, bf16[1536]{0:T(1024)(128)(2,1)}, u32[]{:S(2)}) copy-start(bf16[1536]{0:T(1024)(128)(2,1)} %param.22) | copy-start | bytes 9220
  66.0 6.5 %copy-start.5 = (s32[128,4,4]{0,2,1:T(4,128)S(1)}, s32[128,4,4]{0,2,1:T(4,128)}, u32[]{:S(2)}) copy-start(s32[128,4,4]{0,2,1:T(4,128)} %param.27) | copy-start | bytes 24580
  66.0 30.0 %all-to-all-start.1 = ((f32[64,49,128]{2,1,0:T(8,128)}), f32[64,49,128]{2,1,0:T(8,128)S(1)}, u32[]{:S(2)}, u32[]{:S(2)}) async-start(f32[64,49,128]{2,1,0:T(8,128)} %copy.75), calls=%async_computation.1 | async-start | bytes 3670016 | tf_op jit(solution)/shard_map/partial_exchange/all_to_all | solution.py:115
  71.0 27.1 %copy-start.4 = (bf16[4,1,1536]{2,0,1:T(4,128)(2,1)S(1)}, bf16[4,1,1536]{2,0,1:T(4,128)(2,1)}, u32[]{:S(2)}) copy-start(bf16[4,1,1536]{2,0,1:T(4,128)(2,1)} %param.14) | copy-start | bytes 36868
  101.8 23.5 %copy-start.2 = (bf16[1536,192]{0,1:T(8,128)(2,1)S(1)}, bf16[1536,192]{0,1:T(8,128)(2,1)}, u32[]{:S(2)}) copy-start(bf16[1536,192]{0,1:T(8,128)(2,1)} %param.24) | copy-start | bytes 1769476
  130.1 4.5 %copy-start.8 = (bf16[1536,32]{0,1:T(8,128)(2,1)S(1)}, bf16[1536,32]{0,1:T(8,128)(2,1)}, u32[]{:S(2)}) copy-start(bf16[1536,32]{0,1:T(8,128)(2,1)} %param.23) | copy-start | bytes 294916
  130.1 28.0 %all-to-all-start.3 = ((f32[128,2,1536]{2,1,0:T(2,128)}), f32[128,2,1536]{2,1,0:T(2,128)S(1)}, u32[]{:S(2)}, u32[]{:S(2)}) async-start(f32[128,2,1536]{2,1,0:T(2,128)} %reshape.367), calls=%async_computation.3 | async-start | bytes 3145728 | tf_op jit(solution)/shard_map/expert_return/all_to_all | solution.py:189

commit v2 on v1

--- a/solution.py
+++ b/solution.py
@@ -59,11 +59,10 @@
     window = local_pos * seq_count
     heads_per = QH // KVH
     scale = HD ** (-0.5)
-    heads_steps = STEPS * QH
     step_ids = jnp.arange(STEPS, dtype=jnp.int32)
 
     x = tokens[:, 0, :]
-    own_len = lax.dynamic_index_in_dim(lengths, seq_place, 0, False)
+    own_len = jnp.sum(jnp.where(jnp.arange(group_rows) == seq_place, lengths, 0))
     with jax.named_scope("qkv_projection"):
         a = normalize(x, attn_gain)
         proj = jnp.dot(a, w_qkv, preferred_element_type=jnp.float32)
@@ -74,59 +73,75 @@
         ).astype(jnp.bfloat16)
         fresh_val = proj[:, (QH + KVH) * HD :].reshape(STEPS, KVH, HD).astype(jnp.bfloat16)
 
+    per_head = STEPS * heads_per
+    rows_q = KVH * per_head
+    q_heads = query.reshape(STEPS, KVH, heads_per, HD).transpose(1, 0, 2, 3)
     with jax.named_scope("query_exchange"):
-        sent_q = jnp.broadcast_to(query.reshape(1, STEPS * QH * HD), (seq_count, STEPS * QH * HD))
+        sent_q = jnp.broadcast_to(q_heads.reshape(1, rows_q, HD), (seq_count, rows_q, HD))
         every_query = lax.all_to_all(sent_q, "seq", 0, 0, tiled=True)
-    grouped_all = every_query.reshape(group_rows, STEPS, KVH, heads_per, HD)
 
     with jax.named_scope("slot_attention"):
-        cache_keys = k_cache.reshape(group_rows, local_pos, KVH, HD)
-        cache_vals = v_cache.reshape(group_rows, local_pos, KVH, HD)
-        scores = (
-            jnp.einsum("ntkgd,nckd->ntkgc", grouped_all, cache_keys, preferred_element_type=jnp.float32)
-            * scale
-        )
         key_slot = seq_place * local_pos + jnp.arange(local_pos, dtype=jnp.int32)
-        back = jnp.mod(lengths[:, None, None] - 1 - key_slot[None, None, :], window)
-        reach = jnp.minimum(lengths[:, None, None], window - 1 - step_ids[None, :, None])
-        valid = (back < reach)[:, :, None, None, :]
-        peak_local = jnp.max(jnp.where(valid, scores, -1e30), axis=-1)
-        weights = jnp.where(valid, jnp.exp(scores - peak_local[..., None]), 0.0)
-        total_local = jnp.sum(weights, axis=-1)
-        mixed_local = jnp.einsum(
-            "ntkgc,nckd->ntkgd",
-            weights.astype(jnp.bfloat16),
-            cache_vals,
-            preferred_element_type=jnp.float32,
-        )
-        stats = jnp.concatenate(
+        back = jnp.mod(lengths[:, None] - 1 - key_slot[None, :], window)
+        row_step = jnp.arange(per_head, dtype=jnp.int32) // heads_per
+        reach = jnp.minimum(lengths[:, None], window - 1 - row_step[None, :])
+        valid = back[:, None, :] < reach[:, :, None]
+        mixed_heads, total_heads, hi_heads, mid_heads = [], [], [], []
+        for k in range(KVH):
+            q_k = every_query[:, k * per_head : (k + 1) * per_head, :]
+            keys_k = k_cache[:, :, k * HD : (k + 1) * HD]
+            vals_k = v_cache[:, :, k * HD : (k + 1) * HD]
+            scores = (
+                jnp.einsum("nrd,ncd->nrc", q_k, keys_k, preferred_element_type=jnp.float32)
+                * scale
+            )
+            peak = jnp.max(jnp.where(valid, scores, -1e30), axis=-1)
+            hi = peak.astype(jnp.bfloat16)
+            mid = (peak - hi.astype(jnp.float32)).astype(jnp.bfloat16)
+            shard_peak = hi.astype(jnp.float32) + mid.astype(jnp.float32)
+            weights = jnp.where(valid, jnp.exp(scores - shard_peak[..., None]), 0.0)
+            total_heads.append(jnp.sum(weights, axis=-1))
+            mixed_heads.append(
+                jnp.einsum(
+                    "nrc,ncd->nrd",
+                    weights.astype(jnp.bfloat16),
+                    vals_k,
+                    preferred_element_type=jnp.float32,
+                )
+            )
+            hi_heads.append(hi)
+            mid_heads.append(mid)
+        stats = jnp.stack(
             [
-                total_local.reshape(group_rows, heads_steps),
-                peak_local.reshape(group_rows, heads_steps),
-                jnp.zeros((group_rows, HD - 2 * heads_steps), jnp.float32),
+                jnp.concatenate(total_heads, axis=1),
+                jnp.concatenate(hi_heads, axis=1).astype(jnp.float32),
+                jnp.concatenate(mid_heads, axis=1).astype(jnp.float32),
             ],
-            axis=-1,
-        )
-        packed = jnp.concatenate(
-            [mixed_local.reshape(group_rows, heads_steps, HD), stats[:, None, :]], axis=1
-        )
+            axis=1,
+        )
+        stats = jnp.pad(stats, ((0, 0), (0, 16 - 3), (0, HD - rows_q)))
+        packed = jnp.concatenate(mixed_heads + [stats], axis=1).astype(jnp.bfloat16)
 
     with jax.named_scope("partial_exchange"):
         parts = lax.all_to_all(packed, "seq", 0, 0, tiled=True)
 
     with jax.named_scope("merge_attention"):
-        mixed_s = parts[:, :heads_steps, :].reshape(seq_count, STEPS, KVH, heads_per, HD)
-        total_s = parts[:, heads_steps, :heads_steps].reshape(seq_count, STEPS, KVH, heads_per)
-        peak_s = parts[:, heads_steps, heads_steps : 2 * heads_steps].reshape(
-            seq_count, STEPS, KVH, heads_per
-        )
-        grouped = query.reshape(STEPS, KVH, heads_per, HD)
+        mixed_s = parts[:, :rows_q, :].astype(jnp.float32).reshape(
+            seq_count, KVH, STEPS, heads_per, HD
+        )
+        total_s = parts[:, rows_q, :rows_q].astype(jnp.float32).reshape(
+            seq_count, KVH, STEPS, heads_per
+        )
+        peak_s = (
+            parts[:, rows_q + 1, :rows_q].astype(jnp.float32)
+            + parts[:, rows_q + 2, :rows_q].astype(jnp.float32)
+        ).reshape(seq_count, KVH, STEPS, heads_per)
         tail_scores = (
-            jnp.einsum("tkgd,skd->tkgs", grouped, fresh_key, preferred_element_type=jnp.float32)
+            jnp.einsum("ktgd,skd->ktgs", q_heads, fresh_key, preferred_element_type=jnp.float32)
             * scale
         )
-        tail_valid = (step_ids[None, :] <= step_ids[:, None])[:, None, None, :]
-        sink_grid = sink.reshape(KVH, heads_per)[None]
+        tail_valid = (step_ids[None, :] <= step_ids[:, None])[None, :, None, :]
+        sink_grid = sink.reshape(KVH, 1, heads_per)
         final = jnp.maximum(
             jnp.maximum(jnp.max(peak_s, axis=0), jnp.max(jnp.where(tail_valid, tail_scores, -1e30), axis=-1)),
             sink_grid,
@@ -139,12 +154,14 @@
             + jnp.exp(sink_grid - final)
         )
         mixed = jnp.sum(mixed_s * shift[..., None], axis=0) + jnp.einsum(
-            "tkgs,skd->tkgd",
+            "ktgs,skd->ktgd",
             tail_w.astype(jnp.bfloat16),
             fresh_val,
             preferred_element_type=jnp.float32,
         )
-        attn = (mixed / denom[..., None]).reshape(STEPS, QH * HD).astype(jnp.bfloat16)
+        attn = (
+            (mixed / denom[..., None]).transpose(1, 0, 2, 3).reshape(STEPS, QH * HD).astype(jnp.bfloat16)
+        )
 
     with jax.named_scope("attention_output"):
         h = (
@@ -153,7 +170,8 @@
         u = normalize(h, moe_gain)
 
     with jax.named_scope("route"):
-        picks = lax.dynamic_index_in_dim(routes, device, 0, False)
+        row_ids = jnp.arange(routes.shape[0], dtype=jnp.int32)
+        picks = jnp.sum(jnp.where((row_ids == device)[:, None, None], routes, 0), axis=0)
         experts = jnp.arange(E, dtype=jnp.int32)
         onehot = (picks[:, :, None] == experts[None, None, :]).astype(jnp.float32)
         logits = jnp.dot(u, router, preferred_element_type=jnp.float32)
@@ -181,15 +199,17 @@
             jax.nn.relu(jnp.dot(rows_in, w_gate, preferred_element_type=jnp.float32))
             * jnp.dot(rows_in, w_up, preferred_element_type=jnp.float32)
         ).astype(jnp.bfloat16)
-        produced = jnp.dot(hidden, w_down, preferred_element_type=jnp.float32).reshape(
-            devices, MOST, D
+        produced = (
+            jnp.dot(hidden, w_down, preferred_element_type=jnp.float32)
+            .astype(jnp.bfloat16)
+            .reshape(devices, MOST, D)
         )
 
     with jax.named_scope("expert_return"):
         returned = lax.all_to_all(produced, ("req", "seq"), 0, 0, tiled=True)
 
     with jax.named_scope("expert_sum"):
-        by_expert = jnp.sum(returned.reshape(E, per_device, MOST, D), axis=1)
+        by_expert = jnp.sum(returned.astype(jnp.float32).reshape(E, per_device, MOST, D), axis=1)
         mix = (weight_te[:, :, None] * select).reshape(STEPS, E * MOST)
         moe = jnp.dot(
             mix, by_expert.reshape(E * MOST, D), precision=lax.Precision.HIGHEST,

time: 160 us -> 121 us (0.76)
  local copies, waits for them, and re-layouts: 23.3 us -> 4.49 us
  other arithmetic: 19.2 us -> 8.85 us
  waiting for transfers between devices: 53.6 us -> 45.5 us
    reshape x8 -> x1, local copies, waits for them, and re-layouts: 10.8 us -> 1.17 us  [on_device(): produced = jnp.dot(hidden, w_down, preferred_element_type=jnp.float32).as...]
    all_to_all x1, waiting for transfers between devices: 23.2 us -> 15.7 us  [on_device(): parts = lax.all_to_all(packed, 'seq', 0, 0, tiled=True)]
    all_to_all x1, waiting for transfers between devices: 22.6 us -> 15.1 us  [on_device(): returned = lax.all_to_all(produced, ('req', 'seq'), 0, 0, tiled=True)]
    all_to_all x1, waiting for transfers between devices: 7.8 us -> 14.7 us  [on_device(): every_query = lax.all_to_all(sent_q, 'seq', 0, 0, tiled=True)]
    all_to_all x1 -> x0, other arithmetic: 5.76 us -> none  [on_device(): every_query = lax.all_to_all(sent_q, 'seq', 0, 0, tiled=True)]
    broadcast_in_dim x2 -> x0, other arithmetic: 5.44 us -> none  [the longest x1 5.35 us: on_device(): jnp.broadcast_to(query.reshape(1, STEPS * QH * HD), (seq_count, STEPS * Q...]
    unnamed x22 -> x32, local copies, waits for them, and re-layouts: 4.09 us -> 0.38 us
    concatenate x2, local copies, waits for them, and re-layouts: 2.27 us -> 0.2 us  [the longest x1 0.1 us: on_device(): jnp.concatenate(mid_heads, axis=1).astype(jnp.float32)]
  transfers between devices with their start and end apart: 3 -> 3, of which waited for: 3 -> 3; matrix products, arithmetic and copies ran while one was open for 6% -> 2% of each run, Pallas kernels for 0% -> 0%
where the time goes in v2:
time: 121 us; the launch traced here: 120 us
  waiting for transfers between devices  45.5 us (38%)
  blocking collectives  22.3 us (18%)
  starting transfers between devices  21.3 us (18%)
  matrix products  17.2 us (14%)
  other arithmetic  8.85 us (7%)
  local copies, waits for them, and re-layouts  4.49 us (4%)
    all_to_all x1, blocking collectives, on_device(): arrived = lax.all_to_all(sent_u, ('req', 'seq'), 0, 0, tiled=True)  22.3 us
    all_to_all x1, waiting for transfers between devices, on_device(): parts = lax.all_to_all(packed, 'seq', 0, 0, tiled=True)  15.7 us
    all_to_all x1, waiting for transfers between devices, on_device(): returned = lax.all_to_all(produced, ('req', 'seq'), 0, 0, tiled=True)  15.1 us
    all_to_all x1, waiting for transfers between devices, on_device(): every_query = lax.all_to_all(sent_q, 'seq', 0, 0, tiled=True)  14.7 us
    all_to_all x1, starting transfers between devices, on_device(): every_query = lax.all_to_all(sent_q, 'seq', 0, 0, tiled=True)  12 us
    all_to_all x1, starting transfers between devices, on_device(): parts = lax.all_to_all(packed, 'seq', 0, 0, tiled=True)  4.78 us
    all_to_all x1, starting transfers between devices, on_device(): returned = lax.all_to_all(produced, ('req', 'seq'), 0, 0, tiled=True)  4.54 us
    dot_general x2, matrix products, on_device(): jnp.einsum('nrd,ncd->nrc', q_k, keys_k, preferred_element_type=jnp.float32)  4.1 us
  transfers between devices with their start and end apart: 3, of which 3 were waited for; matrix products, arithmetic and copies ran while one was open for 2% of the time, Pallas kernels for 0%

profile of v2, /device:TPU:1, one launch (start us, length us, event | category | flops | bytes accessed | tf_op | source)
XLA Modules:
  0.0 120.2 jit_solution(4330392849721439188)
XLA Ops:
  0.0 1.4 %broadcast_add_fusion.1 = (s32[64]{0:T(128)S(1)}, s32[]{:T(128)}) fusion(s32[64]{0:T(128)} %param.15, s32[]{:T(128)S(6)} %axis_index.22), kind=kLoop, calls=%fused_computation.155 | loop fusion | flops 255 | bytes 520 | tf_op jit(solution)/shard_map/slot_attention/sub | solution.py:85
  1.4 0.6 add_convert_fusion.2
  2.0 0.7 convert_element_type.240
  2.7 0.8 fusion.45
  3.6 3.8 %fusion.50 = f32[4,2048]{1,0:T(4,128)S(1)} fusion(bf16[1536,2048]{1,0:T(8,128)(2,1)} %param.19, bf16[4,1,1536]{2,0,1:T(4,128)(2,1)} %param.14, f32[1536]{0:T(1024)S(1)} %convert_element_type.240, f32[4]{0:T(128)S(1)} %add_rsqrt_fusion.1), kind=kOutput, calls=%fused_computation.93 | convolution fusion | flops 25190400 | bytes 6342672 | tf_op jit(solution)/shard_map/qkv_projection/dot_general | solution.py:68
  7.7 1.0 broadcast_in_dim.55
  8.7 12.0 %all-to-all-start = ((bf16[64,48,128]{2,1,0:T(8,128)(2,1)}), bf16[64,48,128]{2,1,0:T(8,128)(2,1)S(1)}, u32[]{:S(2)}, u32[]{:S(2)}) async-start(bf16[64,48,128]{2,1,0:T(8,128)(2,1)} %broadcast_in_dim.55), calls=%async_computation | async-start | bytes 1572864 | tf_op jit(solution)/shard_map/query_exchange/all_to_all | solution.py:81
  20.9 14.7 %all-to-all-done = bf16[64,48,128]{2,1,0:T(8,128)(2,1)S(1)} async-done(((bf16[64,48,128]{2,1,0:T(8,128)(2,1)}), bf16[64,48,128]{2,1,0:T(8,128)(2,1)S(1)}, u32[]{:S(2)}, u32[]{:S(2)}) %all-to-all-start) | async-done | bytes 786464 | tf_op jit(solution)/shard_map/query_exchange/all_to_all | solution.py:81
  35.6 2.0 %fusion.13 = (f32[64,24]{1,0:T(8,128)S(1)}, f32[64,24,64]{2,1,0:T(8,128)S(1)}) fusion(s32[64,24]{1,0:T(8,128)S(1)} %broadcast_minimum_fusion, s32[64,64]{1,0:T(8,128)S(1)} %add_select_fusion, bf16[64,64,256]{2,1,0:T(8,128)(2,1)} %param.16, bf16[64,48,128]{2,1,0:T(8,128)(2,1)S(1)} %all-to-all-done), kind=kOutput, calls=%fused_computation.32 | convolution fusion | flops 25557504 | bytes 1906688 | tf_op jit(solution)/shard_map/slot_attention/nrd,ncd->nrc/dot_general | solution.py:95
  37.7 2.1 %fusion.15 = (bf16[64,24]{1,0:T(8,128)(2,1)S(1)}, f32[64,24]{1,0:T(8,128)S(1)}, f32[64,24,64]{2,1,0:T(8,128)S(1)}) fusion(f32[64,24,64]{2,1,0:T(8,128)S(1)} %get-tuple-element.24, f32[64,24]{1,0:T(8,128)S(1)} %copy.106, s32[64,24]{1,0:T(8,128)S(1)} %broadcast_minimum_fusion, s32[64,64]{1,0:T(8,128)S(1)} %add_select_fusion, bf16[64,64,256]{2,1,0:T(8,128)(2,1)} %param.16, ...), kind=kOutput, calls=%fused_computation.34 | convolution fusion | flops 25850880 | bytes 2728960 | tf_op jit(solution)/shard_map/slot_attention/nrd,ncd->nrc/dot_general | solution.py:95
  40.0 0.8 fusion.17
  40.9 1.9 %convolution_convert_fusion.2 = bf16[64,24,128]{2,1,0:T(8,128)(2,1)S(1)} fusion(bf16[64,64,256]{2,1,0:T(8,128)(2,1)} %param.17, f32[64,24,64]{2,1,0:T(8,128)S(1)} %get-tuple-element.25, f32[64,24]{1,0:T(8,128)S(1)} %copy.109, s32[64,24]{1,0:T(8,128)S(1)} %broadcast_minimum_fusion, s32[64,64]{1,0:T(8,128)S(1)} %add_select_fusion), kind=kOutput, calls=%fused_computation.17 | convolution fusion | flops 25755648 | bytes 1863680 | tf_op jit(solution)/shard_map/slot_attention/nrc,ncd->nrd/dot_general | solution.py:105
  42.7 0.9 convolution_convert_fusion.3
  44.2 1.2 pad_maximum_fusion
  45.4 4.8 %all-to-all-start.1 = ((bf16[64,64,128]{2,1,0:T(8,128)(2,1)}), bf16[64,64,128]{2,1,0:T(8,128)(2,1)S(1)}, u32[]{:S(2)}, u32[]{:S(2)}) async-start(bf16[64,64,128]{2,1,0:T(8,128)(2,1)} %pad_maximum_fusion), calls=%async_computation.1 | async-start | bytes 2097152 | tf_op jit(solution)/shard_map/partial_exchange/all_to_all | solution.py:126
  51.1 15.7 %all-to-all-done.1 = bf16[64,64,128]{2,1,0:T(8,128)(2,1)S(1)} async-done(((bf16[64,64,128]{2,1,0:T(8,128)(2,1)}), bf16[64,64,128]{2,1,0:T(8,128)(2,1)S(1)}, u32[]{:S(2)}, u32[]{:S(2)}) %all-to-all-start.1) | async-done | bytes 1048608 | tf_op jit(solution)/shard_map/partial_exchange/all_to_all | solution.py:126
  68.1 3.2 %multiply_reduce_fusion.1 = (f32[4]{0:T(128)S(1)}, f32[4,1536]{1,0:T(4,128)S(1)}) fusion(bf16[4,1536]{1,0:T(4,128)(2,1)S(1)} %convert_element_type.260, bf16[1536,1536]{1,0:T(8,128)(2,1)} %param.21, bf16[4,1,1536]{2,0,1:T(4,128)(2,1)S(1)} %copy-done.5), kind=kOutput, calls=%fused_computation.81 | convolution fusion | flops 18911228 | bytes 4767760 | tf_op jit(solution)/shard_map/attention_output/dot_general | solution.py:168
  72.5 22.3 %all_to_all.20 = bf16[128,2,1536]{2,1,0:T(2,128)(2,1)S(1)} all-to-all(bf16[128,2,1536]{2,1,0:T(2,128)(2,1)S(1)} %bitcast.75), channel_id=1, replica_groups=mesh['req'=2,'seq'=64] {'req','seq'}, dimensions={0} | all-to-all | bytes 1572864 | tf_op jit(solution)/shard_map/token_dispatch/all_to_all | solution.py:194
  95.5 1.1 convolution_convert_fusion
  96.7 1.2 reshape.406
  97.9 4.5 %all-to-all-start.3 = ((bf16[128,2,1536]{2,1,0:T(2,128)(2,1)}), bf16[128,2,1536]{2,1,0:T(2,128)(2,1)S(1)}, u32[]{:S(2)}, u32[]{:S(2)}) async-start(bf16[128,2,1536]{2,1,0:T(2,128)(2,1)} %reshape.406), calls=%async_computation.3 | async-start | bytes 1572864 | tf_op jit(solution)/shard_map/expert_return/all_to_all | solution.py:209
  103.3 15.1 %all-to-all-done.3 = bf16[128,2,1536]{2,1,0:T(2,128)(2,1)S(1)} async-done(((bf16[128,2,1536]{2,1,0:T(2,128)(2,1)}), bf16[128,2,1536]{2,1,0:T(2,128)(2,1)S(1)}, u32[]{:S(2)}, u32[]{:S(2)}) %all-to-all-start.3) | async-done | bytes 786464 | tf_op jit(solution)/shard_map/expert_return/all_to_all | solution.py:209
  118.5 0.7 convert_reduce_fusion
  119.2 1.0 fusion.4
  (101 shorter events, 6.3 us)
Async XLA Ops:
  0.0 95.5 %copy-start = (bf16[192,1536]{1,0:T(8,128)(2,1)S(1)}, bf16[192,1536]{1,0:T(8,128)(2,1)}, u32[]{:S(2)}) copy-start(bf16[192,1536]{1,0:T(8,128)(2,1)} %param.26) | copy-start | bytes 1769476
  7.3 13.4 %copy-start.10 = (s32[64]{0:T(128)S(1)}, s32[64]{0:T(128)}, u32[]{:S(2)}) copy-start(s32[64]{0:T(128)} %param.15) | copy-start | bytes 772
  8.7 26.9 %all-to-all-start = ((bf16[64,48,128]{2,1,0:T(8,128)(2,1)}), bf16[64,48,128]{2,1,0:T(8,128)(2,1)S(1)}, u32[]{:S(2)}, u32[]{:S(2)}) async-start(bf16[64,48,128]{2,1,0:T(8,128)(2,1)} %broadcast_in_dim.55), calls=%async_computation | async-start | bytes 1572864 | tf_op jit(solution)/shard_map/query_exchange/all_to_all | solution.py:81
  40.0 2.7 %copy-start.13 = (bf16[64,64,256]{2,1,0:T(8,128)(2,1)S(1)}, bf16[64,64,256]{2,1,0:T(8,128)(2,1)}, u32[]{:S(2)}) copy-start(bf16[64,64,256]{2,1,0:T(8,128)(2,1)} %param.17) | copy-start | bytes 6291460
  44.1 6.0 %copy-start.15 = (f32[12]{0:T(128)S(1)}, f32[12]{0:T(128)}, u32[]{:S(2)}) copy-start(f32[12]{0:T(128)} %param.20) | copy-start | bytes 148
  44.2 6.6 %copy-start.9 = (bf16[1536]{0:T(1024)(128)(2,1)S(1)}, bf16[1536]{0:T(1024)(128)(2,1)}, u32[]{:S(2)}) copy-start(bf16[1536]{0:T(1024)(128)(2,1)} %param.22) | copy-start | bytes 9220
  44.2 6.6 %copy-start.8 = (s32[128,4,4]{0,2,1:T(4,128)S(1)}, s32[128,4,4]{0,2,1:T(4,128)}, u32[]{:S(2)}) copy-start(s32[128,4,4]{0,2,1:T(4,128)} %param.27) | copy-start | bytes 24580
  45.4 22.7 %copy-start.5 = (bf16[4,1,1536]{2,0,1:T(4,128)(2,1)S(1)}, bf16[4,1,1536]{2,0,1:T(4,128)(2,1)}, u32[]{:S(2)}) copy-start(bf16[4,1,1536]{2,0,1:T(4,128)(2,1)} %param.14) | copy-start | bytes 36868
  45.4 21.4 %all-to-all-start.1 = ((bf16[64,64,128]{2,1,0:T(8,128)(2,1)}), bf16[64,64,128]{2,1,0:T(8,128)(2,1)S(1)}, u32[]{:S(2)}, u32[]{:S(2)}) async-start(bf16[64,64,128]{2,1,0:T(8,128)(2,1)} %pad_maximum_fusion), calls=%async_computation.1 | async-start | bytes 2097152 | tf_op jit(solution)/shard_map/partial_exchange/all_to_all | solution.py:126
  51.0 20.2 %copy-start.6 = (pred[4,32]{1,0:T(4,128)(4,1)}, pred[4,32]{1,0:T(4,128)(4,1)S(1)}, u32[]{:S(2)}) copy-start(pred[4,32]{1,0:T(4,128)(4,1)S(1)} %fusion.59) | copy-start | bytes 388
  71.2 0.6 copy-start.3
  71.3 23.5 %copy-start.11 = (f32[4]{0:T(128)}, f32[4]{0:T(128)S(1)}, u32[]{:S(2)}) copy-start(f32[4]{0:T(128)S(1)} %add_rsqrt_fusion) | copy-start | bytes 52
  72.1 23.0 %copy-start.1 = (bf16[1536,192]{0,1:T(8,128)(2,1)S(1)}, bf16[1536,192]{0,1:T(8,128)(2,1)}, u32[]{:S(2)}) copy-start(bf16[1536,192]{0,1:T(8,128)(2,1)} %param.24) | copy-start | bytes 1769476
  72.5 23.0 %copy-start.2 = (bf16[1536,192]{0,1:T(8,128)(2,1)S(1)}, bf16[1536,192]{0,1:T(8,128)(2,1)}, u32[]{:S(2)}) copy-start(bf16[1536,192]{0,1:T(8,128)(2,1)} %param.25) | copy-start | bytes 1769476
  96.7 5.8 %copy-start.4 = (f32[4,1536]{1,0:T(4,128)S(1)}, f32[4,1536]{1,0:T(4,128)}, u32[]{:S(2)}) copy-start(f32[4,1536]{1,0:T(4,128)} %copy-done.3) | copy-start | bytes 73732
  96.7 5.8 %copy-start.12 = (f32[4]{0:T(128)S(1)}, f32[4]{0:T(128)}, u32[]{:S(2)}) copy-start(f32[4]{0:T(128)} %copy-done.11) | copy-start | bytes 52
  96.7 5.8 %copy-start.14 = (bf16[1536,32]{0,1:T(8,128)(2,1)S(1)}, bf16[1536,32]{0,1:T(8,128)(2,1)}, u32[]{:S(2)}) copy-start(bf16[1536,32]{0,1:T(8,128)(2,1)} %param.23) | copy-start | bytes 294916
  96.7 22.5 %copy-start.7 = (pred[4,32]{1,0:T(4,128)(4,1)S(1)}, pred[4,32]{1,0:T(4,128)(4,1)}, u32[]{:S(2)}) copy-start(pred[4,32]{1,0:T(4,128)(4,1)} %copy-done.6) | copy-start | bytes 388
  97.9 20.6 %all-to-all-start.3 = ((bf16[128,2,1536]{2,1,0:T(2,128)(2,1)}), bf16[128,2,1536]{2,1,0:T(2,128)(2,1)S(1)}, u32[]{:S(2)}, u32[]{:S(2)}) async-start(bf16[128,2,1536]{2,1,0:T(2,128)(2,1)} %reshape.406), calls=%async_computation.3 | async-start | bytes 1572864 | tf_op jit(solution)/shard_map/expert_return/all_to_all | solution.py:209

commit v3 on v2

--- a/solution.py
+++ b/solution.py
@@ -68,6 +68,7 @@
         proj = jnp.dot(a, w_qkv, preferred_element_type=jnp.float32)
         place = own_len + step_ids
         query = rotate(proj[:, : QH * HD].reshape(STEPS, QH, HD), place).astype(jnp.bfloat16)
+    with jax.named_scope("fresh_key_value"):
         fresh_key = rotate(
             proj[:, QH * HD : (QH + KVH) * HD].reshape(STEPS, KVH, HD), place
         ).astype(jnp.bfloat16)
@@ -119,7 +120,7 @@
             ],
             axis=1,
         )
-        stats = jnp.pad(stats, ((0, 0), (0, 16 - 3), (0, HD - rows_q)))
+        stats = jnp.pad(stats, ((0, 0), (0, 8 - 3), (0, HD - rows_q)))
         packed = jnp.concatenate(mixed_heads + [stats], axis=1).astype(jnp.bfloat16)
 
     with jax.named_scope("partial_exchange"):
@@ -194,16 +195,13 @@
         arrived = lax.all_to_all(sent_u, ("req", "seq"), 0, 0, tiled=True)
 
     with jax.named_scope("expert_quarter"):
-        rows_in = arrived.reshape(devices * MOST, D)
         hidden = (
-            jax.nn.relu(jnp.dot(rows_in, w_gate, preferred_element_type=jnp.float32))
-            * jnp.dot(rows_in, w_up, preferred_element_type=jnp.float32)
-        ).astype(jnp.bfloat16)
-        produced = (
-            jnp.dot(hidden, w_down, preferred_element_type=jnp.float32)
-            .astype(jnp.bfloat16)
-            .reshape(devices, MOST, D)
-        )
+            jax.nn.relu(jnp.einsum("sjm,mf->sjf", arrived, w_gate, preferred_element_type=jnp.float32))
+            * jnp.einsum("sjm,mf->sjf", arrived, w_up, preferred_element_type=jnp.float32)
+        ).astype(jnp.bfloat16)
+        produced = jnp.einsum(
+            "sjf,fm->sjm", hidden, w_down, preferred_element_type=jnp.float32
+        ).astype(jnp.bfloat16)
 
     with jax.named_scope("expert_return"):
         returned = lax.all_to_all(produced, ("req", "seq"), 0, 0, tiled=True)

time: 121 us -> 119 us (0.983)
  waiting for transfers between devices: 45.5 us -> 44.1 us
    convert_element_type x0 -> x1, local copies, waits for them, and re-layouts: none -> 1.69 us  [on_device(): produced = jnp.einsum('sjf,fm->sjm', hidden, w_down, preferred_element_ty...]
    reshape x2 -> x0, local copies, waits for them, and re-layouts: 1.47 us -> none  [the longest x1 1.17 us: on_device(): produced = jnp.dot(hidden, w_down, preferred_element_type=jnp.float32).as...]
    all_to_all x1, waiting for transfers between devices: 15.7 us -> 14.2 us  [on_device(): parts = lax.all_to_all(packed, 'seq', 0, 0, tiled=True)]
where the time goes in v3:
time: 119 us; the launch traced here: 118 us
  waiting for transfers between devices  44.1 us (37%)
  blocking collectives  22.4 us (19%)
  starting transfers between devices  21.3 us (18%)
  matrix products  17.2 us (14%)
  other arithmetic  8.71 us (7%)
  local copies, waits for them, and re-layouts  4.38 us (4%)
    all_to_all x1, blocking collectives, on_device(): arrived = lax.all_to_all(sent_u, ('req', 'seq'), 0, 0, tiled=True)  22.4 us
    all_to_all x1, waiting for transfers between devices, on_device(): returned = lax.all_to_all(produced, ('req', 'seq'), 0, 0, tiled=True)  15.1 us
    all_to_all x1, waiting for transfers between devices, on_device(): every_query = lax.all_to_all(sent_q, 'seq', 0, 0, tiled=True)  14.7 us
    all_to_all x1, waiting for transfers between devices, on_device(): parts = lax.all_to_all(packed, 'seq', 0, 0, tiled=True)  14.2 us
    all_to_all x1, starting transfers between devices, on_device(): every_query = lax.all_to_all(sent_q, 'seq', 0, 0, tiled=True)  12 us
    all_to_all x1, starting transfers between devices, on_device(): parts = lax.all_to_all(packed, 'seq', 0, 0, tiled=True)  4.78 us
    all_to_all x1, starting transfers between devices, on_device(): returned = lax.all_to_all(produced, ('req', 'seq'), 0, 0, tiled=True)  4.54 us
    dot_general x2, matrix products, on_device(): jnp.einsum('nrd,ncd->nrc', q_k, keys_k, preferred_element_type=jnp.float32)  4.09 us
  transfers between devices with their start and end apart: 3, of which 3 were waited for; matrix products, arithmetic and copies ran while one was open for 2% of the time, Pallas kernels for 0%

profile of v3, /device:TPU:1, one launch (start us, length us, event | category | flops | bytes accessed | tf_op | source)
XLA Modules:
  0.0 118.5 jit_solution(18228386354327729035)
XLA Ops:
  0.0 1.4 %broadcast_add_fusion.1 = (s32[64]{0:T(128)S(1)}, s32[]{:T(128)}) fusion(s32[64]{0:T(128)} %param.15, s32[]{:T(128)S(6)} %axis_index.22), kind=kLoop, calls=%fused_computation.160 | loop fusion | flops 255 | bytes 520 | tf_op jit(solution)/shard_map/slot_attention/sub | solution.py:86
  1.4 0.6 add_convert_fusion.2
  2.0 0.7 convert_element_type.240
  2.7 0.8 fusion.52
  3.6 3.8 %fusion.57 = f32[4,2048]{1,0:T(4,128)S(1)} fusion(bf16[1536,2048]{1,0:T(8,128)(2,1)} %param.19, bf16[4,1,1536]{2,0,1:T(4,128)(2,1)} %param.14, f32[1536]{0:T(1024)S(1)} %convert_element_type.240, f32[4]{0:T(128)S(1)} %add_rsqrt_fusion.1), kind=kOutput, calls=%fused_computation.98 | convolution fusion | flops 25190400 | bytes 6342672 | tf_op jit(solution)/shard_map/qkv_projection/dot_general | solution.py:68
  7.7 1.0 broadcast_in_dim.55
  8.7 12.0 %all-to-all-start = ((bf16[64,48,128]{2,1,0:T(8,128)(2,1)}), bf16[64,48,128]{2,1,0:T(8,128)(2,1)S(1)}, u32[]{:S(2)}, u32[]{:S(2)}) async-start(bf16[64,48,128]{2,1,0:T(8,128)(2,1)} %broadcast_in_dim.55), calls=%async_computation | async-start | bytes 1572864 | tf_op jit(solution)/shard_map/query_exchange/all_to_all | solution.py:82
  20.9 14.7 %all-to-all-done = bf16[64,48,128]{2,1,0:T(8,128)(2,1)S(1)} async-done(((bf16[64,48,128]{2,1,0:T(8,128)(2,1)}), bf16[64,48,128]{2,1,0:T(8,128)(2,1)S(1)}, u32[]{:S(2)}, u32[]{:S(2)}) %all-to-all-start) | async-done | bytes 786464 | tf_op jit(solution)/shard_map/query_exchange/all_to_all | solution.py:82
  35.6 2.0 %fusion.13 = (f32[64,24]{1,0:T(8,128)S(1)}, f32[64,24,64]{2,1,0:T(8,128)S(1)}) fusion(s32[64,24]{1,0:T(8,128)S(1)} %broadcast_minimum_fusion, s32[64,64]{1,0:T(8,128)S(1)} %add_select_fusion, bf16[64,64,256]{2,1,0:T(8,128)(2,1)} %param.16, bf16[64,48,128]{2,1,0:T(8,128)(2,1)S(1)} %all-to-all-done), kind=kOutput, calls=%fused_computation.32 | convolution fusion | flops 25557504 | bytes 1906688 | tf_op jit(solution)/shard_map/slot_attention/nrd,ncd->nrc/dot_general | solution.py:96
  37.7 2.1 %fusion.18 = (bf16[64,24]{1,0:T(8,128)(2,1)S(1)}, f32[64,24]{1,0:T(8,128)S(1)}, f32[64,24,64]{2,1,0:T(8,128)S(1)}) fusion(f32[64,24,64]{2,1,0:T(8,128)S(1)} %get-tuple-element.24, f32[64,24]{1,0:T(8,128)S(1)} %copy.130, s32[64,24]{1,0:T(8,128)S(1)} %broadcast_minimum_fusion, s32[64,64]{1,0:T(8,128)S(1)} %add_select_fusion, bf16[64,64,256]{2,1,0:T(8,128)(2,1)} %param.16, ...), kind=kOutput, calls=%fused_computation.36 | convolution fusion | flops 25850880 | bytes 2728960 | tf_op jit(solution)/shard_map/slot_attention/nrd,ncd->nrc/dot_general | solution.py:96
  40.0 0.8 fusion.20
  40.8 1.9 %convolution_convert_fusion.2 = bf16[64,24,128]{2,1,0:T(8,128)(2,1)S(1)} fusion(bf16[64,64,256]{2,1,0:T(8,128)(2,1)} %param.17, f32[64,24,64]{2,1,0:T(8,128)S(1)} %get-tuple-element.25, f32[64,24]{1,0:T(8,128)S(1)} %copy.133, s32[64,24]{1,0:T(8,128)S(1)} %broadcast_minimum_fusion, s32[64,64]{1,0:T(8,128)S(1)} %add_select_fusion), kind=kOutput, calls=%fused_computation.17 | convolution fusion | flops 25755648 | bytes 1863680 | tf_op jit(solution)/shard_map/slot_attention/nrc,ncd->nrd/dot_general | solution.py:106
  42.7 0.9 convolution_convert_fusion.3
  44.1 1.0 pad_maximum_fusion
  45.2 4.8 %all-to-all-start.1 = ((bf16[64,56,128]{2,1,0:T(8,128)(2,1)}), bf16[64,56,128]{2,1,0:T(8,128)(2,1)S(1)}, u32[]{:S(2)}, u32[]{:S(2)}) async-start(bf16[64,56,128]{2,1,0:T(8,128)(2,1)} %pad_maximum_fusion), calls=%async_computation.1 | async-start | bytes 1835008 | tf_op jit(solution)/shard_map/partial_exchange/all_to_all | solution.py:127
  50.9 14.2 %all-to-all-done.1 = bf16[64,56,128]{2,1,0:T(8,128)(2,1)S(1)} async-done(((bf16[64,56,128]{2,1,0:T(8,128)(2,1)}), bf16[64,56,128]{2,1,0:T(8,128)(2,1)S(1)}, u32[]{:S(2)}, u32[]{:S(2)}) %all-to-all-start.1) | async-done | bytes 917536 | tf_op jit(solution)/shard_map/partial_exchange/all_to_all | solution.py:127
  66.4 3.2 %multiply_reduce_fusion.1 = (f32[4]{0:T(128)S(1)}, f32[4,1536]{1,0:T(4,128)S(1)}) fusion(bf16[4,1536]{1,0:T(4,128)(2,1)S(1)} %convert_element_type.260, bf16[1536,1536]{1,0:T(8,128)(2,1)} %param.21, bf16[4,1,1536]{2,0,1:T(4,128)(2,1)S(1)} %copy-done.2), kind=kOutput, calls=%fused_computation.86 | convolution fusion | flops 18911228 | bytes 4767760 | tf_op jit(solution)/shard_map/attention_output/dot_general | solution.py:169
  70.5 22.4 %all_to_all.20 = bf16[128,2,1536]{2,1,0:T(2,128)(2,1)S(1)} all-to-all(bf16[128,2,1536]{2,1,0:T(2,128)(2,1)S(1)} %bitcast.80), channel_id=1, replica_groups=mesh['req'=2,'seq'=64] {'req','seq'}, dimensions={0} | all-to-all | bytes 1572864 | tf_op jit(solution)/shard_map/token_dispatch/all_to_all | solution.py:195
  93.4 1.2 convolution_convert_fusion
  94.5 1.7 %copy.145 = bf16[128,2,1536]{2,1,0:T(2,128)(2,1)} copy(bf16[128,2,1536]{2,0,1:T(8,128)(2,1)S(1)} %convolution_convert_fusion) | data formatting | bytes 1572864 | tf_op jit(solution)/shard_map/expert_quarter/convert_element_type | solution.py:204
  96.2 4.5 %all-to-all-start.3 = ((bf16[128,2,1536]{2,1,0:T(2,128)(2,1)}), bf16[128,2,1536]{2,1,0:T(2,128)(2,1)S(1)}, u32[]{:S(2)}, u32[]{:S(2)}) async-start(bf16[128,2,1536]{2,1,0:T(2,128)(2,1)} %copy.145), calls=%async_computation.3 | async-start | bytes 1572864 | tf_op jit(solution)/shard_map/expert_return/all_to_all | solution.py:207
  101.6 15.1 %all-to-all-done.3 = bf16[128,2,1536]{2,1,0:T(2,128)(2,1)S(1)} async-done(((bf16[128,2,1536]{2,1,0:T(2,128)(2,1)}), bf16[128,2,1536]{2,1,0:T(2,128)(2,1)S(1)}, u32[]{:S(2)}, u32[]{:S(2)}) %all-to-all-start.3) | async-done | bytes 786464 | tf_op jit(solution)/shard_map/expert_return/all_to_all | solution.py:207
  116.8 0.7 convert_reduce_fusion
  117.5 1.0 fusion.4
  (88 shorter events, 5.7 us)
Async XLA Ops:
  0.0 93.3 %copy-start = (bf16[192,1536]{1,0:T(8,128)(2,1)S(1)}, bf16[192,1536]{1,0:T(8,128)(2,1)}, u32[]{:S(2)}) copy-start(bf16[192,1536]{1,0:T(8,128)(2,1)} %param.26) | copy-start | bytes 1769476
  7.3 13.4 %copy-start.5 = (s32[64]{0:T(128)S(1)}, s32[64]{0:T(128)}, u32[]{:S(2)}) copy-start(s32[64]{0:T(128)} %param.15) | copy-start | bytes 772
  8.7 26.9 %all-to-all-start = ((bf16[64,48,128]{2,1,0:T(8,128)(2,1)}), bf16[64,48,128]{2,1,0:T(8,128)(2,1)S(1)}, u32[]{:S(2)}, u32[]{:S(2)}) async-start(bf16[64,48,128]{2,1,0:T(8,128)(2,1)} %broadcast_in_dim.55), calls=%async_computation | async-start | bytes 1572864 | tf_op jit(solution)/shard_map/query_exchange/all_to_all | solution.py:82
  40.0 2.7 %copy-start.6 = (bf16[64,64,256]{2,1,0:T(8,128)(2,1)S(1)}, bf16[64,64,256]{2,1,0:T(8,128)(2,1)}, u32[]{:S(2)}) copy-start(bf16[64,64,256]{2,1,0:T(8,128)(2,1)} %param.17) | copy-start | bytes 6291460
  43.6 6.5 %copy-start.9 = (f32[12]{0:T(128)S(1)}, f32[12]{0:T(128)}, u32[]{:S(2)}) copy-start(f32[12]{0:T(128)} %param.20) | copy-start | bytes 148
  43.7 6.9 %copy-start.4 = (bf16[1536]{0:T(1024)(128)(2,1)S(1)}, bf16[1536]{0:T(1024)(128)(2,1)}, u32[]{:S(2)}) copy-start(bf16[1536]{0:T(1024)(128)(2,1)} %param.22) | copy-start | bytes 9220
  43.7 6.9 %copy-start.3 = (s32[128,4,4]{0,2,1:T(4,128)S(1)}, s32[128,4,4]{0,2,1:T(4,128)}, u32[]{:S(2)}) copy-start(s32[128,4,4]{0,2,1:T(4,128)} %param.27) | copy-start | bytes 24580
  45.2 21.2 %copy-start.2 = (bf16[4,1,1536]{2,0,1:T(4,128)(2,1)S(1)}, bf16[4,1,1536]{2,0,1:T(4,128)(2,1)}, u32[]{:S(2)}) copy-start(bf16[4,1,1536]{2,0,1:T(4,128)(2,1)} %param.14) | copy-start | bytes 36868
  45.2 19.9 %all-to-all-start.1 = ((bf16[64,56,128]{2,1,0:T(8,128)(2,1)}), bf16[64,56,128]{2,1,0:T(8,128)(2,1)S(1)}, u32[]{:S(2)}, u32[]{:S(2)}) async-start(bf16[64,56,128]{2,1,0:T(8,128)(2,1)} %pad_maximum_fusion), calls=%async_computation.1 | async-start | bytes 1835008 | tf_op jit(solution)/shard_map/partial_exchange/all_to_all | solution.py:127
  69.6 23.3 %copy-start.7 = (bf16[1536,192]{0,1:T(8,128)(2,1)S(1)}, bf16[1536,192]{0,1:T(8,128)(2,1)}, u32[]{:S(2)}) copy-start(bf16[1536,192]{0,1:T(8,128)(2,1)} %param.24) | copy-start | bytes 1769476
  70.1 23.3 %copy-start.1 = (bf16[1536,192]{0,1:T(8,128)(2,1)S(1)}, bf16[1536,192]{0,1:T(8,128)(2,1)}, u32[]{:S(2)}) copy-start(bf16[1536,192]{0,1:T(8,128)(2,1)} %param.25) | copy-start | bytes 1769476
  94.5 6.2 %copy-start.8 = (bf16[1536,32]{0,1:T(8,128)(2,1)S(1)}, bf16[1536,32]{0,1:T(8,128)(2,1)}, u32[]{:S(2)}) copy-start(bf16[1536,32]{0,1:T(8,128)(2,1)} %param.23) | copy-start | bytes 294916
  96.2 20.6 %all-to-all-start.3 = ((bf16[128,2,1536]{2,1,0:T(2,128)(2,1)}), bf16[128,2,1536]{2,1,0:T(2,128)(2,1)S(1)}, u32[]{:S(2)}, u32[]{:S(2)}) async-start(bf16[128,2,1536]{2,1,0:T(2,128)(2,1)} %copy.145), calls=%async_computation.3 | async-start | bytes 1572864 | tf_op jit(solution)/shard_map/expert_return/all_to_all | solution.py:207

commit v4 on v2

--- a/solution.py
+++ b/solution.py
@@ -1,6 +1,8 @@
 import jax
 import jax.numpy as jnp
 from jax import lax
+from jax.experimental import pallas as pl
+from jax.experimental.pallas import tpu as pltpu
 from jax.sharding import PartitionSpec as P
 
 D = 1536
@@ -32,6 +34,49 @@
     return jnp.concatenate(
         [first * cosine - second * sine, second * cosine + first * sine], axis=-1
     )
+
+
+def qkv_kernel(x_ref, gain_ref, w_ref, proj_ref):
+    xf = x_ref[...].astype(jnp.float32)
+    inv = lax.rsqrt(jnp.mean(xf * xf, axis=-1, keepdims=True) + 1e-05)
+    a = (xf * inv * gain_ref[...].astype(jnp.float32)).astype(jnp.bfloat16)
+    proj_ref[...] = jnp.dot(a, w_ref[...], preferred_element_type=jnp.float32)
+
+
+def qkv_projection(x, gain, w_qkv):
+    rows, width = x.shape
+    columns = w_qkv.shape[1]
+    return pl.pallas_call(
+        qkv_kernel,
+        out_shape=jax.ShapeDtypeStruct((rows, columns), jnp.float32),
+        in_specs=[pl.BlockSpec(memory_space=pltpu.VMEM)] * 3,
+        out_specs=pl.BlockSpec(memory_space=pltpu.VMEM),
+        cost_estimate=pl.CostEstimate(
+            flops=2 * rows * width * columns,
+            transcendentals=rows,
+            bytes_accessed=w_qkv.size * 2 + rows * (width * 2 + columns * 4),
+        ),
+    )(x, gain.reshape(1, width), w_qkv)
+
+
+def output_projection_kernel(attn_ref, w_ref, x_ref, h_ref):
+    product = jnp.dot(attn_ref[...], w_ref[...], preferred_element_type=jnp.float32)
+    h_ref[...] = (x_ref[...].astype(jnp.float32) + product).astype(h_ref.dtype)
+
+
+def output_projection(attn, w_out, x):
+    rows, width = x.shape
+    return pl.pallas_call(
+        output_projection_kernel,
+        out_shape=jax.ShapeDtypeStruct((rows, width), jnp.bfloat16),
+        in_specs=[pl.BlockSpec(memory_space=pltpu.VMEM)] * 3,
+        out_specs=pl.BlockSpec(memory_space=pltpu.VMEM),
+        cost_estimate=pl.CostEstimate(
+            flops=2 * rows * attn.shape[1] * width,
+            transcendentals=0,
+            bytes_accessed=w_out.size * 2 + 3 * rows * width * 2,
+        ),
+    )(attn, w_out, x)
 
 
 def on_device(
@@ -64,10 +109,10 @@
     x = tokens[:, 0, :]
     own_len = jnp.sum(jnp.where(jnp.arange(group_rows) == seq_place, lengths, 0))
     with jax.named_scope("qkv_projection"):
-        a = normalize(x, attn_gain)
-        proj = jnp.dot(a, w_qkv, preferred_element_type=jnp.float32)
+        proj = qkv_projection(x, attn_gain, w_qkv)
         place = own_len + step_ids
         query = rotate(proj[:, : QH * HD].reshape(STEPS, QH, HD), place).astype(jnp.bfloat16)
+    with jax.named_scope("fresh_key_value"):
         fresh_key = rotate(
             proj[:, QH * HD : (QH + KVH) * HD].reshape(STEPS, KVH, HD), place
         ).astype(jnp.bfloat16)
@@ -119,7 +164,7 @@
             ],
             axis=1,
         )
-        stats = jnp.pad(stats, ((0, 0), (0, 16 - 3), (0, HD - rows_q)))
+        stats = jnp.pad(stats, ((0, 0), (0, 8 - 3), (0, HD - rows_q)))
         packed = jnp.concatenate(mixed_heads + [stats], axis=1).astype(jnp.bfloat16)
 
     with jax.named_scope("partial_exchange"):
@@ -164,9 +209,7 @@
         )
 
     with jax.named_scope("attention_output"):
-        h = (
-            x.astype(jnp.float32) + jnp.dot(attn, w_out, preferred_element_type=jnp.float32)
-        ).astype(jnp.bfloat16)
+        h = output_projection(attn, w_out, x)
         u = normalize(h, moe_gain)
 
     with jax.named_scope("route"):

time: 121 us -> 124 us (1.025)
  Pallas kernels: 0 us -> 8.08 us
  matrix products: 17.2 us -> 11.7 us
  local copies, waits for them, and re-layouts: 4.49 us -> 7.99 us
  waiting for transfers between devices: 45.5 us -> 43.4 us
    pallas_call x0 -> x2, Pallas kernels: none -> 8.08 us  [the longest x1 4.42 us: qkv_projection(): pl.pallas_call(qkv_kernel, out_shape=jax.ShapeDtypeStruct((rows, columns)...]
    dot_general x2 -> x0, matrix products: 6.93 us -> none  [the longest x1 3.76 us: on_device(): proj = jnp.dot(a, w_qkv, preferred_element_type=jnp.float32)]
    all_to_all x1, waiting for transfers between devices: 15.7 us -> 14.2 us  [on_device(): parts = lax.all_to_all(packed, 'seq', 0, 0, tiled=True)]
    reshape x0 -> x1, local copies, waits for them, and re-layouts: none -> 1.29 us  [qkv_projection(): gain.reshape(1, width)]
where the time goes in v4:
time: 124 us; the launch traced here: 123 us
  waiting for transfers between devices  43.4 us (35%)
  blocking collectives  22.4 us (18%)
  starting transfers between devices  21.2 us (17%)
  matrix products  11.7 us (9%)
  Pallas kernels  8.08 us (7%)
  other arithmetic  8 us (6%)
  local copies, waits for them, and re-layouts  7.99 us (6%)
    all_to_all x1, blocking collectives, on_device(): arrived = lax.all_to_all(sent_u, ('req', 'seq'), 0, 0, tiled=True)  22.4 us
    all_to_all x1, waiting for transfers between devices, on_device(): returned = lax.all_to_all(produced, ('req', 'seq'), 0, 0, tiled=True)  15.1 us
    all_to_all x1, waiting for transfers between devices, on_device(): parts = lax.all_to_all(packed, 'seq', 0, 0, tiled=True)  14.2 us
    all_to_all x1, waiting for transfers between devices, on_device(): every_query = lax.all_to_all(sent_q, 'seq', 0, 0, tiled=True)  14.1 us
    all_to_all x1, starting transfers between devices, on_device(): every_query = lax.all_to_all(sent_q, 'seq', 0, 0, tiled=True)  12 us
    all_to_all x1, starting transfers between devices, on_device(): parts = lax.all_to_all(packed, 'seq', 0, 0, tiled=True)  4.65 us
    all_to_all x1, starting transfers between devices, on_device(): returned = lax.all_to_all(produced, ('req', 'seq'), 0, 0, tiled=True)  4.55 us
    pallas_call x1, Pallas kernels, qkv_projection(): pl.pallas_call(qkv_kernel, out_shape=jax.ShapeDtypeStruct((rows, columns)...  4.42 us
  transfers between devices with their start and end apart: 3, of which 3 were waited for; matrix products, arithmetic and copies ran while one was open for 2% of the time, Pallas kernels for 0%

profile of v4, /device:TPU:1, one launch (start us, length us, event | category | flops | bytes accessed | tf_op | source)
XLA Modules:
  0.0 123.2 jit_solution(13616940562139389661)
XLA Ops:
  0.0 1.4 %broadcast_add_fusion.1 = (s32[64]{0:T(128)S(1)}, s32[]{:T(128)}) fusion(s32[64]{0:T(128)} %param.15, s32[]{:T(128)S(6)} %axis_index.22), kind=kLoop, calls=%fused_computation.145 | loop fusion | flops 255 | bytes 520 | tf_op jit(solution)/shard_map/slot_attention/sub | solution.py:130
  2.0 1.3 %reshape.394.gain_ref = bf16[1,1536]{1,0:T(2,128)(2,1)} reshape(bf16[1536]{0:T(1024)(128)(2,1)} %param.18) | data formatting | bytes 6144 | tf_op jit(solution)/shard_map/qkv_projection/reshape | solution.py:59
  3.3 4.4 %qkv_projection.1 = f32[4,2048]{1,0:T(4,128)} custom-call(bf16[4,1536]{1,0:T(4,128)(2,1)} %bitcast.69, bf16[1,1536]{1,0:T(2,128)(2,1)} %reshape.394.gain_ref, bf16[1536,2048]{1,0:T(8,128)(2,1)} %w_ref.2), custom_call_target="tpu_custom_call" | custom-call | flops 25165824 | bytes 6336512 | tf_op jit(solution)/shard_map/qkv_projection/pallas_call | solution.py:49
  8.9 1.0 broadcast_in_dim.55
  9.8 12.0 %all-to-all-start = ((bf16[64,48,128]{2,1,0:T(8,128)(2,1)}), bf16[64,48,128]{2,1,0:T(8,128)(2,1)S(1)}, u32[]{:S(2)}, u32[]{:S(2)}) async-start(bf16[64,48,128]{2,1,0:T(8,128)(2,1)} %broadcast_in_dim.55), calls=%async_computation | async-start | bytes 1572864 | tf_op jit(solution)/shard_map/query_exchange/all_to_all | solution.py:126
  22.7 14.1 %all-to-all-done = bf16[64,48,128]{2,1,0:T(8,128)(2,1)S(1)} async-done(((bf16[64,48,128]{2,1,0:T(8,128)(2,1)}), bf16[64,48,128]{2,1,0:T(8,128)(2,1)S(1)}, u32[]{:S(2)}, u32[]{:S(2)}) %all-to-all-start) | async-done | bytes 786464 | tf_op jit(solution)/shard_map/query_exchange/all_to_all | solution.py:126
  36.7 2.0 %fusion.11 = (f32[64,24]{1,0:T(8,128)S(1)}, f32[64,24,64]{2,1,0:T(8,128)S(1)}) fusion(s32[64,24]{1,0:T(8,128)S(1)} %broadcast_minimum_fusion, s32[64,64]{1,0:T(8,128)S(1)} %add_select_fusion, bf16[64,64,256]{2,1,0:T(8,128)(2,1)} %param.16, bf16[64,48,128]{2,1,0:T(8,128)(2,1)S(1)} %all-to-all-done), kind=kOutput, calls=%fused_computation.29 | convolution fusion | flops 25557504 | bytes 1906688 | tf_op jit(solution)/shard_map/slot_attention/nrd,ncd->nrc/dot_general | solution.py:140
  38.9 2.1 %fusion.13 = (bf16[64,24]{1,0:T(8,128)(2,1)S(1)}, f32[64,24]{1,0:T(8,128)S(1)}, f32[64,24,64]{2,1,0:T(8,128)S(1)}) fusion(f32[64,24,64]{2,1,0:T(8,128)S(1)} %get-tuple-element.24, f32[64,24]{1,0:T(8,128)S(1)} %copy.107, s32[64,24]{1,0:T(8,128)S(1)} %broadcast_minimum_fusion, s32[64,64]{1,0:T(8,128)S(1)} %add_select_fusion, bf16[64,64,256]{2,1,0:T(8,128)(2,1)} %param.16, ...), kind=kOutput, calls=%fused_computation.31 | convolution fusion | flops 25850880 | bytes 2728960 | tf_op jit(solution)/shard_map/slot_attention/nrd,ncd->nrc/dot_general | solution.py:140
  41.2 0.8 fusion.15
  42.0 1.9 %convolution_convert_fusion.2 = bf16[64,24,128]{2,1,0:T(8,128)(2,1)S(1)} fusion(bf16[64,64,256]{2,1,0:T(8,128)(2,1)} %param.17, f32[64,24,64]{2,1,0:T(8,128)S(1)} %get-tuple-element.25, f32[64,24]{1,0:T(8,128)S(1)} %copy.110, s32[64,24]{1,0:T(8,128)S(1)} %broadcast_minimum_fusion, s32[64,64]{1,0:T(8,128)S(1)} %add_select_fusion), kind=kOutput, calls=%fused_computation.14 | convolution fusion | flops 25755648 | bytes 1863680 | tf_op jit(solution)/shard_map/slot_attention/nrc,ncd->nrd/dot_general | solution.py:150
  43.9 0.9 convolution_convert_fusion.3
  45.3 1.0 pad_maximum_fusion
  46.4 4.6 %all-to-all-start.1 = ((bf16[64,56,128]{2,1,0:T(8,128)(2,1)}), bf16[64,56,128]{2,1,0:T(8,128)(2,1)S(1)}, u32[]{:S(2)}, u32[]{:S(2)}) async-start(bf16[64,56,128]{2,1,0:T(8,128)(2,1)} %pad_maximum_fusion), calls=%async_computation.1 | async-start | bytes 1835008 | tf_op jit(solution)/shard_map/partial_exchange/all_to_all | solution.py:171
  52.0 14.2 %all-to-all-done.1 = bf16[64,56,128]{2,1,0:T(8,128)(2,1)S(1)} async-done(((bf16[64,56,128]{2,1,0:T(8,128)(2,1)}), bf16[64,56,128]{2,1,0:T(8,128)(2,1)S(1)}, u32[]{:S(2)}, u32[]{:S(2)}) %all-to-all-start.1) | async-done | bytes 917536 | tf_op jit(solution)/shard_map/partial_exchange/all_to_all | solution.py:171
  67.2 0.9 fusion.6
  68.7 3.7 %attention_output.1 = bf16[4,1536]{1,0:T(4,128)(2,1)} custom-call(bf16[4,1536]{1,0:T(4,128)(2,1)} %convert_element_type.239.attn_ref, bf16[1536,1536]{1,0:T(8,128)(2,1)} %w_ref.3, bf16[4,1536]{1,0:T(4,128)(2,1)} %bitcast.70), custom_call_target="tpu_custom_call" | custom-call | flops 18874368 | bytes 4755456 | tf_op jit(solution)/shard_map/attention_output/pallas_call | solution.py:69
  72.4 0.8 fusion.43
  73.8 1.0 convolution_convert_fusion.1
  75.4 22.4 %all_to_all.20 = bf16[128,2,1536]{2,1,0:T(2,128)(2,1)S(1)} all-to-all(bf16[128,2,1536]{2,1,0:T(2,128)(2,1)S(1)} %bitcast.65), channel_id=1, replica_groups=mesh['req'=2,'seq'=64] {'req','seq'}, dimensions={0} | all-to-all | bytes 1572864 | tf_op jit(solution)/shard_map/token_dispatch/all_to_all | solution.py:237
  98.6 1.1 convolution_convert_fusion
  99.8 1.2 reshape.399
  100.9 4.5 %all-to-all-start.3 = ((bf16[128,2,1536]{2,1,0:T(2,128)(2,1)}), bf16[128,2,1536]{2,1,0:T(2,128)(2,1)S(1)}, u32[]{:S(2)}, u32[]{:S(2)}) async-start(bf16[128,2,1536]{2,1,0:T(2,128)(2,1)} %reshape.399), calls=%async_computation.3 | async-start | bytes 1572864 | tf_op jit(solution)/shard_map/expert_return/all_to_all | solution.py:252
  106.4 15.1 %all-to-all-done.3 = bf16[128,2,1536]{2,1,0:T(2,128)(2,1)S(1)} async-done(((bf16[128,2,1536]{2,1,0:T(2,128)(2,1)}), bf16[128,2,1536]{2,1,0:T(2,128)(2,1)S(1)}, u32[]{:S(2)}, u32[]{:S(2)}) %all-to-all-start.3) | async-done | bytes 786464 | tf_op jit(solution)/shard_map/expert_return/all_to_all | solution.py:252
  122.2 1.0 fusion.2
  (96 shorter events, 9.4 us)
Async XLA Ops:
  0.0 98.5 %copy-start = (bf16[192,1536]{1,0:T(8,128)(2,1)S(1)}, bf16[192,1536]{1,0:T(8,128)(2,1)}, u32[]{:S(2)}) copy-start(bf16[192,1536]{1,0:T(8,128)(2,1)} %param.26) | copy-start | bytes 1769476
  7.7 14.8 %copy-start.8 = (s32[64]{0:T(128)S(1)}, s32[64]{0:T(128)}, u32[]{:S(2)}) copy-start(s32[64]{0:T(128)} %param.15) | copy-start | bytes 772
  9.8 26.9 %all-to-all-start = ((bf16[64,48,128]{2,1,0:T(8,128)(2,1)}), bf16[64,48,128]{2,1,0:T(8,128)(2,1)S(1)}, u32[]{:S(2)}, u32[]{:S(2)}) async-start(bf16[64,48,128]{2,1,0:T(8,128)(2,1)} %broadcast_in_dim.55), calls=%async_computation | async-start | bytes 1572864 | tf_op jit(solution)/shard_map/query_exchange/all_to_all | solution.py:126
  41.2 2.7 %copy-start.11 = (bf16[64,64,256]{2,1,0:T(8,128)(2,1)S(1)}, bf16[64,64,256]{2,1,0:T(8,128)(2,1)}, u32[]{:S(2)}) copy-start(bf16[64,64,256]{2,1,0:T(8,128)(2,1)} %param.17) | copy-start | bytes 6291460
  44.8 6.3 %copy-start.13 = (f32[12]{0:T(128)S(1)}, f32[12]{0:T(128)}, u32[]{:S(2)}) copy-start(f32[12]{0:T(128)} %param.20) | copy-start | bytes 148
  44.9 6.7 %copy-start.7 = (bf16[1536]{0:T(1024)(128)(2,1)S(1)}, bf16[1536]{0:T(1024)(128)(2,1)}, u32[]{:S(2)}) copy-start(bf16[1536]{0:T(1024)(128)(2,1)} %param.22) | copy-start | bytes 9220
  44.9 6.7 %copy-start.6 = (s32[128,4,4]{0,2,1:T(4,128)S(1)}, s32[128,4,4]{0,2,1:T(4,128)}, u32[]{:S(2)}) copy-start(s32[128,4,4]{0,2,1:T(4,128)} %param.27) | copy-start | bytes 24580
  46.4 19.8 %all-to-all-start.1 = ((bf16[64,56,128]{2,1,0:T(8,128)(2,1)}), bf16[64,56,128]{2,1,0:T(8,128)(2,1)S(1)}, u32[]{:S(2)}, u32[]{:S(2)}) async-start(bf16[64,56,128]{2,1,0:T(8,128)(2,1)} %pad_maximum_fusion), calls=%async_computation.1 | async-start | bytes 1835008 | tf_op jit(solution)/shard_map/partial_exchange/all_to_all | solution.py:171
  51.9 21.4 %copy-start.4 = (pred[4,32]{1,0:T(4,128)(4,1)}, pred[4,32]{1,0:T(4,128)(4,1)S(1)}, u32[]{:S(2)}) copy-start(pred[4,32]{1,0:T(4,128)(4,1)S(1)} %fusion.52) | copy-start | bytes 388
  73.3 0.5 copy-start.9
  75.0 23.2 %copy-start.1 = (bf16[1536,192]{0,1:T(8,128)(2,1)S(1)}, bf16[1536,192]{0,1:T(8,128)(2,1)}, u32[]{:S(2)}) copy-start(bf16[1536,192]{0,1:T(8,128)(2,1)} %param.24) | copy-start | bytes 1769476
  75.4 23.2 %copy-start.2 = (bf16[1536,192]{0,1:T(8,128)(2,1)S(1)}, bf16[1536,192]{0,1:T(8,128)(2,1)}, u32[]{:S(2)}) copy-start(bf16[1536,192]{0,1:T(8,128)(2,1)} %param.25) | copy-start | bytes 1769476
  99.7 5.8 %copy-start.3 = (bf16[4,1536]{1,0:T(4,128)(2,1)S(1)}, bf16[4,1536]{1,0:T(4,128)(2,1)}, u32[]{:S(2)}) copy-start(bf16[4,1536]{1,0:T(4,128)(2,1)} %attention_output.1) | copy-start | bytes 36868
  99.7 5.8 %copy-start.10 = (f32[4]{0:T(128)S(1)}, f32[4]{0:T(128)}, u32[]{:S(2)}) copy-start(f32[4]{0:T(128)} %copy-done.9) | copy-start | bytes 52
  99.7 5.8 %copy-start.12 = (bf16[1536,32]{0,1:T(8,128)(2,1)S(1)}, bf16[1536,32]{0,1:T(8,128)(2,1)}, u32[]{:S(2)}) copy-start(bf16[1536,32]{0,1:T(8,128)(2,1)} %param.23) | copy-start | bytes 294916
  99.7 22.5 %copy-start.5 = (pred[4,32]{1,0:T(4,128)(4,1)S(1)}, pred[4,32]{1,0:T(4,128)(4,1)}, u32[]{:S(2)}) copy-start(pred[4,32]{1,0:T(4,128)(4,1)} %copy-done.4) | copy-start | bytes 388
  100.9 20.6 %all-to-all-start.3 = ((bf16[128,2,1536]{2,1,0:T(2,128)(2,1)}), bf16[128,2,1536]{2,1,0:T(2,128)(2,1)S(1)}, u32[]{:S(2)}, u32[]{:S(2)}) async-start(bf16[128,2,1536]{2,1,0:T(2,128)(2,1)} %reshape.399), calls=%async_computation.3 | async-start | bytes 1572864 | tf_op jit(solution)/shard_map/expert_return/all_to_all | solution.py:252

commit v5 on v2

--- a/solution.py
+++ b/solution.py
@@ -68,6 +68,7 @@
         proj = jnp.dot(a, w_qkv, preferred_element_type=jnp.float32)
         place = own_len + step_ids
         query = rotate(proj[:, : QH * HD].reshape(STEPS, QH, HD), place).astype(jnp.bfloat16)
+    with jax.named_scope("fresh_key_value"):
         fresh_key = rotate(
             proj[:, QH * HD : (QH + KVH) * HD].reshape(STEPS, KVH, HD), place
         ).astype(jnp.bfloat16)
@@ -119,7 +120,7 @@
             ],
             axis=1,
         )
-        stats = jnp.pad(stats, ((0, 0), (0, 16 - 3), (0, HD - rows_q)))
+        stats = jnp.pad(stats, ((0, 0), (0, 8 - 3), (0, HD - rows_q)))
         packed = jnp.concatenate(mixed_heads + [stats], axis=1).astype(jnp.bfloat16)
 
     with jax.named_scope("partial_exchange"):
@@ -209,11 +210,12 @@
         returned = lax.all_to_all(produced, ("req", "seq"), 0, 0, tiled=True)
 
     with jax.named_scope("expert_sum"):
-        by_expert = jnp.sum(returned.astype(jnp.float32).reshape(E, per_device, MOST, D), axis=1)
-        mix = (weight_te[:, :, None] * select).reshape(STEPS, E * MOST)
+        mix = jnp.broadcast_to(
+            (weight_te[:, :, None] * select)[:, :, None, :], (STEPS, E, per_device, MOST)
+        ).reshape(STEPS, devices * MOST)
         moe = jnp.dot(
-            mix, by_expert.reshape(E * MOST, D), precision=lax.Precision.HIGHEST,
-            preferred_element_type=jnp.float32,
+            mix, returned.reshape(devices * MOST, D).astype(jnp.float32),
+            precision=lax.Precision.HIGHEST, preferred_element_type=jnp.float32,
         )
         out = (h.astype(jnp.float32) + moe).astype(jnp.bfloat16)
     return out[:, None, :]

time: 121 us -> 120 us (level)
  blocking collectives: 22.3 us -> 0 us
  waiting for transfers between devices: 45.5 us -> 60.1 us
  starting transfers between devices: 21.3 us -> 28.2 us
    all_to_all x1 -> x0, blocking collectives: 22.3 us -> none  [on_device(): arrived = lax.all_to_all(sent_u, ('req', 'seq'), 0, 0, tiled=True)]
    all_to_all x0 -> x1, waiting for transfers between devices: none -> 15.9 us  [on_device(): arrived = lax.all_to_all(sent_u, ('req', 'seq'), 0, 0, tiled=True)]
    all_to_all x0 -> x1, starting transfers between devices: none -> 6.88 us  [on_device(): arrived = lax.all_to_all(sent_u, ('req', 'seq'), 0, 0, tiled=True)]
    all_to_all x1, waiting for transfers between devices: 15.7 us -> 14.2 us  [on_device(): parts = lax.all_to_all(packed, 'seq', 0, 0, tiled=True)]
  transfers between devices with their start and end apart: 3 -> 4, of which waited for: 3 -> 4; matrix products, arithmetic and copies ran while one was open for 2% -> 2% of each run, Pallas kernels for 0% -> 0%
where the time goes in v5:
time: 120 us
  waiting for transfers between devices  60.1 us (50%)
  starting transfers between devices  28.2 us (24%)
  matrix products  17.3 us (14%)
  other arithmetic  7.96 us (7%)
  local copies, waits for them, and re-layouts  5.48 us (5%)
    all_to_all x1, waiting for transfers between devices, on_device(): arrived = lax.all_to_all(sent_u, ('req', 'seq'), 0, 0, tiled=True)  15.9 us
    all_to_all x1, waiting for transfers between devices, on_device(): returned = lax.all_to_all(produced, ('req', 'seq'), 0, 0, tiled=True)  15.2 us
    all_to_all x1, waiting for transfers between devices, on_device(): every_query = lax.all_to_all(sent_q, 'seq', 0, 0, tiled=True)  14.7 us
    all_to_all x1, waiting for transfers between devices, on_device(): parts = lax.all_to_all(packed, 'seq', 0, 0, tiled=True)  14.2 us
    all_to_all x1, starting transfers between devices, on_device(): every_query = lax.all_to_all(sent_q, 'seq', 0, 0, tiled=True)  12 us
    all_to_all x1, starting transfers between devices, on_device(): arrived = lax.all_to_all(sent_u, ('req', 'seq'), 0, 0, tiled=True)  6.88 us
    all_to_all x1, starting transfers between devices, on_device(): parts = lax.all_to_all(packed, 'seq', 0, 0, tiled=True)  4.78 us
    all_to_all x1, starting transfers between devices, on_device(): returned = lax.all_to_all(produced, ('req', 'seq'), 0, 0, tiled=True)  4.54 us
  transfers between devices with their start and end apart: 4, of which 4 were waited for; matrix products, arithmetic and copies ran while one was open for 2% of the time, Pallas kernels for 0%

profile of v5, /device:TPU:1, one launch (start us, length us, event | category | flops | bytes accessed | tf_op | source)
XLA Modules:
  0.0 119.5 jit_solution(17733208680232799717)
XLA Ops:
  0.0 1.4 %broadcast_add_fusion.1 = (s32[64]{0:T(128)S(1)}, s32[]{:T(128)}) fusion(s32[64]{0:T(128)} %param.15, s32[]{:T(128)S(6)} %axis_index.22), kind=kLoop, calls=%fused_computation.148 | loop fusion | flops 255 | bytes 520 | tf_op jit(solution)/shard_map/slot_attention/sub | solution.py:86
  2.0 0.7 convert_element_type.240
  2.7 0.8 fusion.43
  3.6 3.8 %fusion.48 = f32[4,2048]{1,0:T(4,128)S(1)} fusion(bf16[1536,2048]{1,0:T(8,128)(2,1)} %param.19, bf16[4,1,1536]{2,0,1:T(4,128)(2,1)} %param.14, f32[1536]{0:T(1024)S(1)} %convert_element_type.240, f32[4]{0:T(128)S(1)} %add_rsqrt_fusion.1), kind=kOutput, calls=%fused_computation.90 | convolution fusion | flops 25190400 | bytes 6342672 | tf_op jit(solution)/shard_map/qkv_projection/dot_general | solution.py:68
  7.7 1.0 broadcast_in_dim.57
  8.7 12.0 %all-to-all-start = ((bf16[64,48,128]{2,1,0:T(8,128)(2,1)}), bf16[64,48,128]{2,1,0:T(8,128)(2,1)S(1)}, u32[]{:S(2)}, u32[]{:S(2)}) async-start(bf16[64,48,128]{2,1,0:T(8,128)(2,1)} %broadcast_in_dim.57), calls=%async_computation | async-start | bytes 1572864 | tf_op jit(solution)/shard_map/query_exchange/all_to_all | solution.py:82
  20.9 14.7 %all-to-all-done = bf16[64,48,128]{2,1,0:T(8,128)(2,1)S(1)} async-done(((bf16[64,48,128]{2,1,0:T(8,128)(2,1)}), bf16[64,48,128]{2,1,0:T(8,128)(2,1)S(1)}, u32[]{:S(2)}, u32[]{:S(2)}) %all-to-all-start) | async-done | bytes 786464 | tf_op jit(solution)/shard_map/query_exchange/all_to_all | solution.py:82
  35.6 2.0 %fusion.12 = (f32[64,24]{1,0:T(8,128)S(1)}, f32[64,24,64]{2,1,0:T(8,128)S(1)}) fusion(s32[64,24]{1,0:T(8,128)S(1)} %broadcast_minimum_fusion, s32[64,64]{1,0:T(8,128)S(1)} %add_select_fusion, bf16[64,64,256]{2,1,0:T(8,128)(2,1)} %param.16, bf16[64,48,128]{2,1,0:T(8,128)(2,1)S(1)} %all-to-all-done), kind=kOutput, calls=%fused_computation.30 | convolution fusion | flops 25557504 | bytes 1906688 | tf_op jit(solution)/shard_map/slot_attention/nrd,ncd->nrc/dot_general | solution.py:96
  37.7 2.1 %fusion.14 = (bf16[64,24]{1,0:T(8,128)(2,1)S(1)}, f32[64,24]{1,0:T(8,128)S(1)}, f32[64,24,64]{2,1,0:T(8,128)S(1)}) fusion(f32[64,24,64]{2,1,0:T(8,128)S(1)} %get-tuple-element.24, f32[64,24]{1,0:T(8,128)S(1)} %copy.110, s32[64,24]{1,0:T(8,128)S(1)} %broadcast_minimum_fusion, s32[64,64]{1,0:T(8,128)S(1)} %add_select_fusion, bf16[64,64,256]{2,1,0:T(8,128)(2,1)} %param.16, ...), kind=kOutput, calls=%fused_computation.32 | convolution fusion | flops 25850880 | bytes 2728960 | tf_op jit(solution)/shard_map/slot_attention/nrd,ncd->nrc/dot_general | solution.py:96
  40.0 0.8 fusion.16
  40.9 1.9 %convolution_convert_fusion.2 = bf16[64,24,128]{2,1,0:T(8,128)(2,1)S(1)} fusion(bf16[64,64,256]{2,1,0:T(8,128)(2,1)} %param.17, f32[64,24,64]{2,1,0:T(8,128)S(1)} %get-tuple-element.25, f32[64,24]{1,0:T(8,128)S(1)} %copy.113, s32[64,24]{1,0:T(8,128)S(1)} %broadcast_minimum_fusion, s32[64,64]{1,0:T(8,128)S(1)} %add_select_fusion), kind=kOutput, calls=%fused_computation.15 | convolution fusion | flops 25755648 | bytes 1863680 | tf_op jit(solution)/shard_map/slot_attention/nrc,ncd->nrd/dot_general | solution.py:106
  42.7 0.9 convolution_convert_fusion.3
  44.2 1.0 pad_maximum_fusion
  45.2 4.8 %all-to-all-start.1 = ((bf16[64,56,128]{2,1,0:T(8,128)(2,1)}), bf16[64,56,128]{2,1,0:T(8,128)(2,1)S(1)}, u32[]{:S(2)}, u32[]{:S(2)}) async-start(bf16[64,56,128]{2,1,0:T(8,128)(2,1)} %pad_maximum_fusion), calls=%async_computation.1 | async-start | bytes 1835008 | tf_op jit(solution)/shard_map/partial_exchange/all_to_all | solution.py:127
  50.9 14.2 %all-to-all-done.1 = bf16[64,56,128]{2,1,0:T(8,128)(2,1)S(1)} async-done(((bf16[64,56,128]{2,1,0:T(8,128)(2,1)}), bf16[64,56,128]{2,1,0:T(8,128)(2,1)S(1)}, u32[]{:S(2)}, u32[]{:S(2)}) %all-to-all-start.1) | async-done | bytes 917536 | tf_op jit(solution)/shard_map/partial_exchange/all_to_all | solution.py:127
  66.4 3.2 %multiply_reduce_fusion.1 = (f32[4]{0:T(128)S(1)}, f32[4,1536]{1,0:T(4,128)S(1)}) fusion(bf16[4,1536]{1,0:T(4,128)(2,1)S(1)} %convert_element_type.260, bf16[1536,1536]{1,0:T(8,128)(2,1)} %param.21, bf16[4,1,1536]{2,0,1:T(4,128)(2,1)S(1)} %copy-done.5), kind=kOutput, calls=%fused_computation.78 | convolution fusion | flops 18911228 | bytes 4767760 | tf_op jit(solution)/shard_map/attention_output/dot_general | solution.py:169
  70.1 1.3 %broadcast_in_dim.66 = bf16[32,4,2,1536]{3,2,1,0:T(2,128)(2,1)} broadcast(bf16[32,2,1536]{2,1,0:T(2,128)(2,1)S(1)} %copy.123), dimensions={0,2,3} | broadcast | bytes 983040 | tf_op jit(solution)/shard_map/route/broadcast_in_dim | solution.py:190
  71.4 6.9 %all-to-all-start.2 = ((bf16[128,2,1536]{2,1,0:T(2,128)(2,1)}), bf16[128,2,1536]{2,1,0:T(2,128)(2,1)S(1)}, u32[]{:S(2)}, u32[]{:S(2)}) async-start(bf16[128,2,1536]{2,1,0:T(2,128)(2,1)} %bitcast.22), calls=%async_computation.2 | async-start | bytes 1572864 | tf_op jit(solution)/shard_map/token_dispatch/all_to_all | solution.py:195
  78.5 15.9 %all-to-all-done.2 = bf16[128,2,1536]{2,1,0:T(2,128)(2,1)S(1)} async-done(((bf16[128,2,1536]{2,1,0:T(2,128)(2,1)}), bf16[128,2,1536]{2,1,0:T(2,128)(2,1)S(1)}, u32[]{:S(2)}, u32[]{:S(2)}) %all-to-all-start.2) | async-done | bytes 786464 | tf_op jit(solution)/shard_map/token_dispatch/all_to_all | solution.py:195
  95.2 1.1 convolution_convert_fusion
  96.3 1.2 reshape.410
  97.5 4.5 %all-to-all-start.3 = ((bf16[128,2,1536]{2,1,0:T(2,128)(2,1)}), bf16[128,2,1536]{2,1,0:T(2,128)(2,1)S(1)}, u32[]{:S(2)}, u32[]{:S(2)}) async-start(bf16[128,2,1536]{2,1,0:T(2,128)(2,1)} %reshape.410), calls=%async_computation.3 | async-start | bytes 1572864 | tf_op jit(solution)/shard_map/expert_return/all_to_all | solution.py:210
  102.8 15.2 %all-to-all-done.3 = bf16[128,2,1536]{2,1,0:T(2,128)(2,1)S(1)} async-done(((bf16[128,2,1536]{2,1,0:T(2,128)(2,1)}), bf16[128,2,1536]{2,1,0:T(2,128)(2,1)S(1)}, u32[]{:S(2)}, u32[]{:S(2)}) %all-to-all-start.3) | async-done | bytes 786464 | tf_op jit(solution)/shard_map/expert_return/all_to_all | solution.py:210
  118.4 1.1 fusion.3
  (97 shorter events, 6.6 us)
Async XLA Ops:
  0.0 95.2 %copy-start = (bf16[192,1536]{1,0:T(8,128)(2,1)S(1)}, bf16[192,1536]{1,0:T(8,128)(2,1)}, u32[]{:S(2)}) copy-start(bf16[192,1536]{1,0:T(8,128)(2,1)} %param.26) | copy-start | bytes 1769476
  7.3 13.4 %copy-start.8 = (s32[64]{0:T(128)S(1)}, s32[64]{0:T(128)}, u32[]{:S(2)}) copy-start(s32[64]{0:T(128)} %param.15) | copy-start | bytes 772
  8.7 26.9 %all-to-all-start = ((bf16[64,48,128]{2,1,0:T(8,128)(2,1)}), bf16[64,48,128]{2,1,0:T(8,128)(2,1)S(1)}, u32[]{:S(2)}, u32[]{:S(2)}) async-start(bf16[64,48,128]{2,1,0:T(8,128)(2,1)} %broadcast_in_dim.57), calls=%async_computation | async-start | bytes 1572864 | tf_op jit(solution)/shard_map/query_exchange/all_to_all | solution.py:82
  40.0 2.7 %copy-start.9 = (bf16[64,64,256]{2,1,0:T(8,128)(2,1)S(1)}, bf16[64,64,256]{2,1,0:T(8,128)(2,1)}, u32[]{:S(2)}) copy-start(bf16[64,64,256]{2,1,0:T(8,128)(2,1)} %param.17) | copy-start | bytes 6291460
  43.6 6.5 %copy-start.11 = (f32[12]{0:T(128)S(1)}, f32[12]{0:T(128)}, u32[]{:S(2)}) copy-start(f32[12]{0:T(128)} %param.20) | copy-start | bytes 148
  43.7 6.9 %copy-start.6 = (s32[128,4,4]{0,2,1:T(4,128)S(1)}, s32[128,4,4]{0,2,1:T(4,128)}, u32[]{:S(2)}) copy-start(s32[128,4,4]{0,2,1:T(4,128)} %param.27) | copy-start | bytes 24580
  43.7 7.1 %copy-start.7 = (bf16[1536]{0:T(1024)(128)(2,1)S(1)}, bf16[1536]{0:T(1024)(128)(2,1)}, u32[]{:S(2)}) copy-start(bf16[1536]{0:T(1024)(128)(2,1)} %param.22) | copy-start | bytes 9220
  45.2 21.2 %copy-start.5 = (bf16[4,1,1536]{2,0,1:T(4,128)(2,1)S(1)}, bf16[4,1,1536]{2,0,1:T(4,128)(2,1)}, u32[]{:S(2)}) copy-start(bf16[4,1,1536]{2,0,1:T(4,128)(2,1)} %param.14) | copy-start | bytes 36868
  45.2 19.9 %all-to-all-start.1 = ((bf16[64,56,128]{2,1,0:T(8,128)(2,1)}), bf16[64,56,128]{2,1,0:T(8,128)(2,1)S(1)}, u32[]{:S(2)}, u32[]{:S(2)}) async-start(bf16[64,56,128]{2,1,0:T(8,128)(2,1)} %pad_maximum_fusion), calls=%async_computation.1 | async-start | bytes 1835008 | tf_op jit(solution)/shard_map/partial_exchange/all_to_all | solution.py:127
  69.6 24.9 %copy-start.3 = (f32[4,1536]{1,0:T(4,128)}, f32[4,1536]{1,0:T(4,128)S(1)}, u32[]{:S(2)}) copy-start(f32[4,1536]{1,0:T(4,128)S(1)} %get-tuple-element.29) | copy-start | bytes 73732
  69.6 8.7 %copy-start.10 = (bf16[1536,32]{0,1:T(8,128)(2,1)S(1)}, bf16[1536,32]{0,1:T(8,128)(2,1)}, u32[]{:S(2)}) copy-start(bf16[1536,32]{0,1:T(8,128)(2,1)} %param.23) | copy-start | bytes 294916
  70.1 24.6 %copy-start.1 = (bf16[1536,192]{0,1:T(8,128)(2,1)S(1)}, bf16[1536,192]{0,1:T(8,128)(2,1)}, u32[]{:S(2)}) copy-start(bf16[1536,192]{0,1:T(8,128)(2,1)} %param.24) | copy-start | bytes 1769476
  71.4 23.8 %copy-start.2 = (bf16[1536,192]{0,1:T(8,128)(2,1)S(1)}, bf16[1536,192]{0,1:T(8,128)(2,1)}, u32[]{:S(2)}) copy-start(bf16[1536,192]{0,1:T(8,128)(2,1)} %param.25) | copy-start | bytes 1769476
  71.4 23.0 %all-to-all-start.2 = ((bf16[128,2,1536]{2,1,0:T(2,128)(2,1)}), bf16[128,2,1536]{2,1,0:T(2,128)(2,1)S(1)}, u32[]{:S(2)}, u32[]{:S(2)}) async-start(bf16[128,2,1536]{2,1,0:T(2,128)(2,1)} %bitcast.22), calls=%async_computation.2 | async-start | bytes 1572864 | tf_op jit(solution)/shard_map/token_dispatch/all_to_all | solution.py:195
  96.3 22.1 %copy-start.4 = (f32[4,1536]{1,0:T(4,128)S(1)}, f32[4,1536]{1,0:T(4,128)}, u32[]{:S(2)}) copy-start(f32[4,1536]{1,0:T(4,128)} %copy-done.3) | copy-start | bytes 73732
  97.5 20.6 %all-to-all-start.3 = ((bf16[128,2,1536]{2,1,0:T(2,128)(2,1)}), bf16[128,2,1536]{2,1,0:T(2,128)(2,1)S(1)}, u32[]{:S(2)}, u32[]{:S(2)}) async-start(bf16[128,2,1536]{2,1,0:T(2,128)(2,1)} %reshape.410), calls=%async_computation.3 | async-start | bytes 1572864 | tf_op jit(solution)/shard_map/expert_return/all_to_all | solution.py:210

commit v6 on v3

--- a/solution.py
+++ b/solution.py
@@ -84,44 +84,35 @@
     with jax.named_scope("slot_attention"):
         key_slot = seq_place * local_pos + jnp.arange(local_pos, dtype=jnp.int32)
         back = jnp.mod(lengths[:, None] - 1 - key_slot[None, :], window)
-        row_step = jnp.arange(per_head, dtype=jnp.int32) // heads_per
+        row_ids = jnp.arange(rows_q, dtype=jnp.int32)
+        row_head = row_ids // per_head
+        row_step = (row_ids % per_head) // heads_per
         reach = jnp.minimum(lengths[:, None], window - 1 - row_step[None, :])
         valid = back[:, None, :] < reach[:, :, None]
-        mixed_heads, total_heads, hi_heads, mid_heads = [], [], [], []
-        for k in range(KVH):
-            q_k = every_query[:, k * per_head : (k + 1) * per_head, :]
-            keys_k = k_cache[:, :, k * HD : (k + 1) * HD]
-            vals_k = v_cache[:, :, k * HD : (k + 1) * HD]
-            scores = (
-                jnp.einsum("nrd,ncd->nrc", q_k, keys_k, preferred_element_type=jnp.float32)
-                * scale
-            )
-            peak = jnp.max(jnp.where(valid, scores, -1e30), axis=-1)
-            hi = peak.astype(jnp.bfloat16)
-            mid = (peak - hi.astype(jnp.float32)).astype(jnp.bfloat16)
-            shard_peak = hi.astype(jnp.float32) + mid.astype(jnp.float32)
-            weights = jnp.where(valid, jnp.exp(scores - shard_peak[..., None]), 0.0)
-            total_heads.append(jnp.sum(weights, axis=-1))
-            mixed_heads.append(
-                jnp.einsum(
-                    "nrc,ncd->nrd",
-                    weights.astype(jnp.bfloat16),
-                    vals_k,
-                    preferred_element_type=jnp.float32,
-                )
-            )
-            hi_heads.append(hi)
-            mid_heads.append(mid)
+        lane_head = jnp.arange(KVH * HD, dtype=jnp.int32) // HD
+        own_half = row_head[None, :, None] == lane_head[None, None, :]
+        q_spread = jnp.where(
+            own_half, jnp.concatenate([every_query] * KVH, axis=-1), jnp.zeros((), jnp.bfloat16)
+        )
+        scores = (
+            jnp.einsum("nre,nce->nrc", q_spread, k_cache, preferred_element_type=jnp.float32)
+            * scale
+        )
+        peak = jnp.max(jnp.where(valid, scores, -1e30), axis=-1)
+        hi = peak.astype(jnp.bfloat16)
+        mid = (peak - hi.astype(jnp.float32)).astype(jnp.bfloat16)
+        shard_peak = hi.astype(jnp.float32) + mid.astype(jnp.float32)
+        weights = jnp.where(valid, jnp.exp(scores - shard_peak[..., None]), 0.0)
+        total = jnp.sum(weights, axis=-1)
+        spread = jnp.einsum(
+            "nrc,nce->nre", weights.astype(jnp.bfloat16), v_cache, preferred_element_type=jnp.float32
+        )
+        mixed_local = jnp.where(row_head[None, :, None] == 0, spread[..., :HD], spread[..., HD:])
         stats = jnp.stack(
-            [
-                jnp.concatenate(total_heads, axis=1),
-                jnp.concatenate(hi_heads, axis=1).astype(jnp.float32),
-                jnp.concatenate(mid_heads, axis=1).astype(jnp.float32),
-            ],
-            axis=1,
+            [total, hi.astype(jnp.float32), mid.astype(jnp.float32)], axis=1
         )
         stats = jnp.pad(stats, ((0, 0), (0, 8 - 3), (0, HD - rows_q)))
-        packed = jnp.concatenate(mixed_heads + [stats], axis=1).astype(jnp.bfloat16)
+        packed = jnp.concatenate([mixed_local, stats], axis=1).astype(jnp.bfloat16)
 
     with jax.named_scope("partial_exchange"):
         parts = lax.all_to_all(packed, "seq", 0, 0, tiled=True)

time: 119 us -> 123 us (1.034)
  other arithmetic: 8.71 us -> 11.2 us
    dot_general x1, matrix products: 1.15 us -> 3.14 us  [on_device(): jnp.einsum('sjf,fm->sjm', hidden, w_down, preferred_element_type=jnp.floa...]
    dot_general x4 -> x2, matrix products: 6.8 us -> 4.98 us  [the longest x1 2.68 us: on_device(): jnp.einsum('nrc,nce->nre', weights.astype(jnp.bfloat16), v_cache, preferr...]
    another operation x4, other arithmetic: 0.44 us -> 1.87 us  [the longest x2 0.28 us: on_device(): jnp.stack([jnp.concatenate(total_heads, axis=1), jnp.concatenate(hi_heads...]
where the time goes in v6:
time: 123 us
  waiting for transfers between devices  43.9 us (36%)
  blocking collectives  22.4 us (18%)
  starting transfers between devices  21.3 us (17%)
  matrix products  18 us (15%)
  other arithmetic  11.2 us (9%)
  local copies, waits for them, and re-layouts  5.24 us (4%)
    all_to_all x1, blocking collectives, on_device(): arrived = lax.all_to_all(sent_u, ('req', 'seq'), 0, 0, tiled=True)  22.4 us
    all_to_all x1, waiting for transfers between devices, on_device(): returned = lax.all_to_all(produced, ('req', 'seq'), 0, 0, tiled=True)  15.1 us
    all_to_all x1, waiting for transfers between devices, on_device(): parts = lax.all_to_all(packed, 'seq', 0, 0, tiled=True)  14.5 us
    all_to_all x1, waiting for transfers between devices, on_device(): every_query = lax.all_to_all(sent_q, 'seq', 0, 0, tiled=True)  14.3 us
    all_to_all x1, starting transfers between devices, on_device(): every_query = lax.all_to_all(sent_q, 'seq', 0, 0, tiled=True)  12 us
    all_to_all x1, starting transfers between devices, on_device(): parts = lax.all_to_all(packed, 'seq', 0, 0, tiled=True)  4.78 us
    all_to_all x1, starting transfers between devices, on_device(): returned = lax.all_to_all(produced, ('req', 'seq'), 0, 0, tiled=True)  4.54 us
    dot_general x1, matrix products, on_device(): proj = jnp.dot(a, w_qkv, preferred_element_type=jnp.float32)  3.76 us
  transfers between devices with their start and end apart: 3, of which 3 were waited for; matrix products, arithmetic and copies ran while one was open for 2% of the time, Pallas kernels for 0%

profile of v6, /device:TPU:1, one launch (start us, length us, event | category | flops | bytes accessed | tf_op | source)
XLA Modules:
  0.0 122.5 jit_solution(13137235917124336248)
XLA Ops:
  0.0 1.0 fusion.47
  1.0 1.3 %broadcast_add_fusion.1 = (s32[64]{0:T(128)S(1)}, s32[]{:T(128)}) fusion(s32[64]{0:T(128)} %param.15, s32[]{:T(128)S(6)} %axis_index.22), kind=kLoop, calls=%fused_computation.150 | loop fusion | flops 255 | bytes 520 | tf_op jit(solution)/shard_map/slot_attention/sub | solution.py:86
  2.3 0.6 add_convert_fusion.2
  3.0 0.7 convert_element_type.188
  3.7 3.8 %fusion.50 = f32[4,2048]{1,0:T(4,128)S(1)} fusion(bf16[1536,2048]{1,0:T(8,128)(2,1)} %param.19, bf16[4,1,1536]{2,0,1:T(4,128)(2,1)} %param.14, f32[1536]{0:T(1024)S(1)} %convert_element_type.188, f32[4]{0:T(128)S(1)} %add_rsqrt_fusion.1), kind=kOutput, calls=%fused_computation.87 | convolution fusion | flops 25190400 | bytes 6342672 | tf_op jit(solution)/shard_map/qkv_projection/dot_general | solution.py:68
  7.8 1.0 broadcast_in_dim.75
  8.8 12.0 %all-to-all-start = ((bf16[64,48,128]{2,1,0:T(8,128)(2,1)}), bf16[64,48,128]{2,1,0:T(8,128)(2,1)S(1)}, u32[]{:S(2)}, u32[]{:S(2)}) async-start(bf16[64,48,128]{2,1,0:T(8,128)(2,1)} %broadcast_in_dim.75), calls=%async_computation | async-start | bytes 1572864 | tf_op jit(solution)/shard_map/query_exchange/all_to_all | solution.py:82
  21.4 14.3 %all-to-all-done = bf16[64,48,128]{2,1,0:T(8,128)(2,1)S(1)} async-done(((bf16[64,48,128]{2,1,0:T(8,128)(2,1)}), bf16[64,48,128]{2,1,0:T(8,128)(2,1)S(1)}, u32[]{:S(2)}, u32[]{:S(2)}) %all-to-all-start) | async-done | bytes 786464 | tf_op jit(solution)/shard_map/query_exchange/all_to_all | solution.py:82
  35.7 2.3 %fusion.5 = (f32[64,48]{1,0:T(8,128)S(1)}, f32[64,48,64]{2,1,0:T(8,128)S(1)}) fusion(s32[64,48]{1,0:T(8,128)S(1)} %broadcast_minimum_fusion, s32[64,64]{1,0:T(8,128)S(1)} %add_select_fusion, bf16[64,64,256]{2,1,0:T(8,128)(2,1)} %param.16, bf16[64,48,128]{2,1,0:T(8,128)(2,1)S(1)} %all-to-all-done, pred[48,256]{1,0:T(8,128)(4,1)S(1)} %broadcast_compare_fusion), kind=kOutput, calls=%fused_computation.11 | convolution fusion | flops 105378816 | bytes 3723264 | tf_op jit(solution)/shard_map/slot_attention/nre,nce->nrc/dot_general | solution.py:98
  38.1 1.7 %fusion.12 = bf16[64,48]{1,0:T(8,128)(2,1)S(1)} fusion(f32[64,48,64]{2,1,0:T(8,128)S(1)} %get-tuple-element.16, f32[64,48]{1,0:T(8,128)S(1)} %convert_add_fusion, s32[64,48]{1,0:T(8,128)S(1)} %broadcast_minimum_fusion, s32[64,64]{1,0:T(8,128)S(1)} %add_select_fusion), kind=kLoop, calls=%fused_computation.22 | loop fusion | flops 783360 | bytes 833536 | tf_op jit(solution)/shard_map/slot_attention/reduce_sum | solution.py:106
  39.8 2.7 %fusion.18 = bf16[64,48,256]{2,1,0:T(8,128)(2,1)} fusion(bf16[64,64,256]{2,1,0:T(8,128)(2,1)S(1)} %copy-done, f32[64,48,64]{2,1,0:T(8,128)S(1)} %get-tuple-element.16, f32[64,48]{1,0:T(8,128)S(1)} %convert_add_fusion, s32[64,48]{1,0:T(8,128)S(1)} %broadcast_minimum_fusion, s32[64,64]{1,0:T(8,128)S(1)} %add_select_fusion), kind=kOutput, calls=%fused_computation.33 | convolution fusion | flops 101449728 | bytes 4497408 | tf_op jit(solution)/shard_map/slot_attention/nrc,nce->nre/dot_general | solution.py:107
  42.7 1.5 %fusion.6 = bf16[64,48,128]{2,1,0:T(8,128)(2,1)S(1)} fusion(bf16[64,48,256]{2,1,0:T(8,128)(2,1)} %fusion.18, pred[48]{0:T(512)(128)(4,1)S(1)} %broadcast_compare_fusion.1), kind=kLoop, calls=%fused_computation.13 | loop fusion | flops 393216 | bytes 2359344 | tf_op jit(solution)/shard_map/convert.5
  44.4 1.0 pad_maximum_fusion
  45.4 4.8 %all-to-all-start.1 = ((bf16[64,56,128]{2,1,0:T(8,128)(2,1)}), bf16[64,56,128]{2,1,0:T(8,128)(2,1)S(1)}, u32[]{:S(2)}, u32[]{:S(2)}) async-start(bf16[64,56,128]{2,1,0:T(8,128)(2,1)} %pad_maximum_fusion), calls=%async_computation.1 | async-start | bytes 1835008 | tf_op jit(solution)/shard_map/partial_exchange/all_to_all | solution.py:118
  50.9 14.5 %all-to-all-done.1 = bf16[64,56,128]{2,1,0:T(8,128)(2,1)S(1)} async-done(((bf16[64,56,128]{2,1,0:T(8,128)(2,1)}), bf16[64,56,128]{2,1,0:T(8,128)(2,1)S(1)}, u32[]{:S(2)}, u32[]{:S(2)}) %all-to-all-start.1) | async-done | bytes 917536 | tf_op jit(solution)/shard_map/partial_exchange/all_to_all | solution.py:118
  66.6 3.2 %multiply_reduce_fusion.1 = (f32[4]{0:T(128)S(1)}, f32[4,1536]{1,0:T(4,128)S(1)}) fusion(bf16[4,1536]{1,0:T(4,128)(2,1)S(1)} %convert_element_type.206, bf16[1536,1536]{1,0:T(8,128)(2,1)} %param.21, bf16[4,1,1536]{2,0,1:T(4,128)(2,1)S(1)} %copy-done.2), kind=kOutput, calls=%fused_computation.81 | convolution fusion | flops 18911228 | bytes 4767760 | tf_op jit(solution)/shard_map/attention_output/dot_general | solution.py:160
  70.7 22.4 %all_to_all.20 = bf16[128,2,1536]{2,1,0:T(2,128)(2,1)S(1)} all-to-all(bf16[128,2,1536]{2,1,0:T(2,128)(2,1)S(1)} %bitcast.76), channel_id=1, replica_groups=mesh['req'=2,'seq'=64] {'req','seq'}, dimensions={0} | all-to-all | bytes 1572864 | tf_op jit(solution)/shard_map/token_dispatch/all_to_all | solution.py:186
  93.2 1.1 convolution_maximum_fusion
  94.3 3.1 %convolution_convert_fusion = bf16[128,2,1536]{2,0,1:T(8,128)(2,1)} fusion(f32[128,2,192]{0,2,1:T(8,128)} %convolution_maximum_fusion, bf16[128,2,1536]{2,1,0:T(2,128)(2,1)S(1)} %all_to_all.20, bf16[192,1536]{1,0:T(8,128)(2,1)S(1)} %copy-done.1, bf16[1536,192]{0,1:T(8,128)(2,1)} %param.25), kind=kOutput, calls=%fused_computation | convolution fusion | flops 302481408 | bytes 2949120 | tf_op jit(solution)/shard_map/expert_quarter/sjf,fm->sjm/dot_general | solution.py:193
  97.4 2.9 %copy.83 = bf16[128,2,1536]{2,1,0:T(2,128)(2,1)} copy(bf16[128,2,1536]{2,0,1:T(8,128)(2,1)} %convolution_convert_fusion) | data formatting | bytes 1572864 | tf_op jit(solution)/shard_map/expert_quarter/convert_element_type | solution.py:195
  100.3 4.5 %all-to-all-start.3 = ((bf16[128,2,1536]{2,1,0:T(2,128)(2,1)}), bf16[128,2,1536]{2,1,0:T(2,128)(2,1)S(1)}, u32[]{:S(2)}, u32[]{:S(2)}) async-start(bf16[128,2,1536]{2,1,0:T(2,128)(2,1)} %copy.83), calls=%async_computation.3 | async-start | bytes 1572864 | tf_op jit(solution)/shard_map/expert_return/all_to_all | solution.py:198
  105.7 15.1 %all-to-all-done.3 = bf16[128,2,1536]{2,1,0:T(2,128)(2,1)S(1)} async-done(((bf16[128,2,1536]{2,1,0:T(2,128)(2,1)}), bf16[128,2,1536]{2,1,0:T(2,128)(2,1)S(1)}, u32[]{:S(2)}, u32[]{:S(2)}) %all-to-all-start.3) | async-done | bytes 786464 | tf_op jit(solution)/shard_map/expert_return/all_to_all | solution.py:198
  120.8 0.7 convert_reduce_fusion
  121.6 1.0 fusion.4
  (83 shorter events, 5.0 us)
Async XLA Ops:
  0.0 39.8 %copy-start = (bf16[64,64,256]{2,1,0:T(8,128)(2,1)S(1)}, bf16[64,64,256]{2,1,0:T(8,128)(2,1)}, u32[]{:S(2)}) copy-start(bf16[64,64,256]{2,1,0:T(8,128)(2,1)} %param.17) | copy-start | bytes 6291460
  7.4 13.4 %copy-start.3 = (s32[128,4,4]{0,2,1:T(4,128)S(1)}, s32[128,4,4]{0,2,1:T(4,128)}, u32[]{:S(2)}) copy-start(s32[128,4,4]{0,2,1:T(4,128)} %param.27) | copy-start | bytes 24580
  7.4 13.8 %copy-start.5 = (s32[64]{0:T(128)S(1)}, s32[64]{0:T(128)}, u32[]{:S(2)}) copy-start(s32[64]{0:T(128)} %param.15) | copy-start | bytes 772
  8.8 26.9 %all-to-all-start = ((bf16[64,48,128]{2,1,0:T(8,128)(2,1)}), bf16[64,48,128]{2,1,0:T(8,128)(2,1)S(1)}, u32[]{:S(2)}, u32[]{:S(2)}) async-start(bf16[64,48,128]{2,1,0:T(8,128)(2,1)} %broadcast_in_dim.75), calls=%async_computation | async-start | bytes 1572864 | tf_op jit(solution)/shard_map/query_exchange/all_to_all | solution.py:82
  44.4 5.8 %copy-start.8 = (f32[12]{0:T(128)S(1)}, f32[12]{0:T(128)}, u32[]{:S(2)}) copy-start(f32[12]{0:T(128)} %param.20) | copy-start | bytes 148
  44.4 6.0 %copy-start.4 = (bf16[1536]{0:T(1024)(128)(2,1)S(1)}, bf16[1536]{0:T(1024)(128)(2,1)}, u32[]{:S(2)}) copy-start(bf16[1536]{0:T(1024)(128)(2,1)} %param.22) | copy-start | bytes 9220
  45.4 21.2 %copy-start.2 = (bf16[4,1,1536]{2,0,1:T(4,128)(2,1)S(1)}, bf16[4,1,1536]{2,0,1:T(4,128)(2,1)}, u32[]{:S(2)}) copy-start(bf16[4,1,1536]{2,0,1:T(4,128)(2,1)} %param.14) | copy-start | bytes 36868
  45.4 19.9 %all-to-all-start.1 = ((bf16[64,56,128]{2,1,0:T(8,128)(2,1)}), bf16[64,56,128]{2,1,0:T(8,128)(2,1)S(1)}, u32[]{:S(2)}, u32[]{:S(2)}) async-start(bf16[64,56,128]{2,1,0:T(8,128)(2,1)} %pad_maximum_fusion), calls=%async_computation.1 | async-start | bytes 1835008 | tf_op jit(solution)/shard_map/partial_exchange/all_to_all | solution.py:118
  69.8 23.3 %copy-start.6 = (bf16[1536,192]{0,1:T(8,128)(2,1)S(1)}, bf16[1536,192]{0,1:T(8,128)(2,1)}, u32[]{:S(2)}) copy-start(bf16[1536,192]{0,1:T(8,128)(2,1)} %param.24) | copy-start | bytes 1769476
  70.7 23.5 %copy-start.1 = (bf16[192,1536]{1,0:T(8,128)(2,1)S(1)}, bf16[192,1536]{1,0:T(8,128)(2,1)}, u32[]{:S(2)}) copy-start(bf16[192,1536]{1,0:T(8,128)(2,1)} %param.26) | copy-start | bytes 1769476
  97.4 7.4 %copy-start.7 = (bf16[1536,32]{0,1:T(8,128)(2,1)S(1)}, bf16[1536,32]{0,1:T(8,128)(2,1)}, u32[]{:S(2)}) copy-start(bf16[1536,32]{0,1:T(8,128)(2,1)} %param.23) | copy-start | bytes 294916
  100.3 20.6 %all-to-all-start.3 = ((bf16[128,2,1536]{2,1,0:T(2,128)(2,1)}), bf16[128,2,1536]{2,1,0:T(2,128)(2,1)S(1)}, u32[]{:S(2)}, u32[]{:S(2)}) async-start(bf16[128,2,1536]{2,1,0:T(2,128)(2,1)} %copy.83), calls=%async_computation.3 | async-start | bytes 1572864 | tf_op jit(solution)/shard_map/expert_return/all_to_all | solution.py:198

commit v7 on v2

--- a/solution.py
+++ b/solution.py
@@ -62,23 +62,37 @@
     step_ids = jnp.arange(STEPS, dtype=jnp.int32)
 
     x = tokens[:, 0, :]
-    own_len = jnp.sum(jnp.where(jnp.arange(group_rows) == seq_place, lengths, 0))
-    with jax.named_scope("qkv_projection"):
-        a = normalize(x, attn_gain)
-        proj = jnp.dot(a, w_qkv, preferred_element_type=jnp.float32)
-        place = own_len + step_ids
-        query = rotate(proj[:, : QH * HD].reshape(STEPS, QH, HD), place).astype(jnp.bfloat16)
-        fresh_key = rotate(
-            proj[:, QH * HD : (QH + KVH) * HD].reshape(STEPS, KVH, HD), place
-        ).astype(jnp.bfloat16)
-        fresh_val = proj[:, (QH + KVH) * HD :].reshape(STEPS, KVH, HD).astype(jnp.bfloat16)
-
     per_head = STEPS * heads_per
     rows_q = KVH * per_head
-    q_heads = query.reshape(STEPS, KVH, heads_per, HD).transpose(1, 0, 2, 3)
-    with jax.named_scope("query_exchange"):
-        sent_q = jnp.broadcast_to(q_heads.reshape(1, rows_q, HD), (seq_count, rows_q, HD))
-        every_query = lax.all_to_all(sent_q, "seq", 0, 0, tiled=True)
+    with jax.named_scope("token_exchange"):
+        sent_x = jnp.broadcast_to(x[None], (seq_count, STEPS, D))
+        every_x = lax.all_to_all(sent_x, "seq", 0, 0, tiled=True)
+
+    with jax.named_scope("qkv_projection"):
+        a_all = normalize(every_x.reshape(group_rows * STEPS, D), attn_gain)
+        proj_all = jnp.dot(a_all, w_qkv, preferred_element_type=jnp.float32).reshape(
+            group_rows, STEPS, (QH + 2 * KVH) * HD
+        )
+        place_all = lengths[:, None] + step_ids[None, :]
+        query_all = rotate(proj_all[..., : QH * HD].reshape(group_rows, STEPS, QH, HD), place_all).astype(
+            jnp.bfloat16
+        )
+        every_query = (
+            query_all.reshape(group_rows, STEPS, KVH, heads_per, HD)
+            .transpose(0, 2, 1, 3, 4)
+            .reshape(group_rows, rows_q, HD)
+        )
+
+    with jax.named_scope("fresh_key_value"):
+        mine = (jnp.arange(group_rows) == seq_place)[:, None, None]
+        own_proj = jnp.sum(jnp.where(mine, proj_all[..., QH * HD :], 0.0), axis=0)
+        own_len = jnp.sum(jnp.where(jnp.arange(group_rows) == seq_place, lengths, 0))
+        place = own_len + step_ids
+        fresh_key = rotate(own_proj[:, : KVH * HD].reshape(STEPS, KVH, HD), place).astype(jnp.bfloat16)
+        fresh_val = own_proj[:, KVH * HD :].reshape(STEPS, KVH, HD).astype(jnp.bfloat16)
+        q_heads = jnp.sum(
+            jnp.where(mine, every_query.astype(jnp.float32), 0.0), axis=0
+        ).astype(jnp.bfloat16).reshape(KVH, STEPS, heads_per, HD)
 
     with jax.named_scope("slot_attention"):
         key_slot = seq_place * local_pos + jnp.arange(local_pos, dtype=jnp.int32)
@@ -119,7 +133,7 @@
             ],
             axis=1,
         )
-        stats = jnp.pad(stats, ((0, 0), (0, 16 - 3), (0, HD - rows_q)))
+        stats = jnp.pad(stats, ((0, 0), (0, 8 - 3), (0, HD - rows_q)))
         packed = jnp.concatenate(mixed_heads + [stats], axis=1).astype(jnp.bfloat16)
 
     with jax.named_scope("partial_exchange"):

time: 121 us -> 127 us (1.050)
  local copies, waits for them, and re-layouts: 4.49 us -> 11.4 us
  waiting for transfers between devices: 45.5 us -> 40.7 us
  matrix products: 17.2 us -> 18.9 us
  other arithmetic: 8.85 us -> 10.4 us
    unnamed x32 -> x39, local copies, waits for them, and re-layouts: 0.38 us -> 3.19 us
    all_to_all x1, waiting for transfers between devices: 14.7 us -> 12.2 us  [on_device(): every_x = lax.all_to_all(sent_x, 'seq', 0, 0, tiled=True)]
    reduce_sum x0 -> x3, other arithmetic: none -> 2.43 us  [the longest x1 1.17 us: on_device(): own_proj = jnp.sum(jnp.where(mine, proj_all[..., QH * HD:], 0.0), axis=0)]
    all_to_all x1, waiting for transfers between devices: 15.7 us -> 13.3 us  [on_device(): parts = lax.all_to_all(packed, 'seq', 0, 0, tiled=True)]
    reshape x2, local copies, waits for them, and re-layouts: 0.02 us -> 1.52 us  [the longest x1 1.52 us: on_device(): proj_all[..., :QH * HD].reshape(group_rows, STEPS, QH, HD)]
    sub x1 -> x0, other arithmetic: 1.35 us -> none  [on_device(): back = jnp.mod(lengths[:, None] - 1 - key_slot[None, :], window)]
    slice x1 -> x2, local copies, waits for them, and re-layouts: 0.01 us -> 1.31 us  [the longest x1 1.26 us: on_device(): proj_all[..., :QH * HD].reshape(group_rows, STEPS, QH, HD)]
  transfers between devices with their start and end apart: 3 -> 3, of which waited for: 3 -> 3; matrix products, arithmetic and copies ran while one was open for 2% -> 4% of each run, Pallas kernels for 0% -> 0%
where the time goes in v7:
time: 127 us; the launch traced here: 126 us
  waiting for transfers between devices  40.7 us (32%)
  blocking collectives  22.4 us (18%)
  starting transfers between devices  21.5 us (17%)
  matrix products  18.9 us (15%)
  local copies, waits for them, and re-layouts  11.4 us (9%)
  other arithmetic  10.4 us (8%)
    all_to_all x1, blocking collectives, on_device(): arrived = lax.all_to_all(sent_u, ('req', 'seq'), 0, 0, tiled=True)  22.4 us
    all_to_all x1, waiting for transfers between devices, on_device(): returned = lax.all_to_all(produced, ('req', 'seq'), 0, 0, tiled=True)  15.1 us
    all_to_all x1, waiting for transfers between devices, on_device(): parts = lax.all_to_all(packed, 'seq', 0, 0, tiled=True)  13.3 us
    all_to_all x1, waiting for transfers between devices, on_device(): every_x = lax.all_to_all(sent_x, 'seq', 0, 0, tiled=True)  12.2 us
    all_to_all x1, starting transfers between devices, on_device(): every_x = lax.all_to_all(sent_x, 'seq', 0, 0, tiled=True)  12 us
    all_to_all x1, starting transfers between devices, on_device(): parts = lax.all_to_all(packed, 'seq', 0, 0, tiled=True)  4.96 us
    dot_general x1, matrix products, on_device(): jnp.dot(a_all, w_qkv, preferred_element_type=jnp.float32)  4.57 us
    all_to_all x1, starting transfers between devices, on_device(): returned = lax.all_to_all(produced, ('req', 'seq'), 0, 0, tiled=True)  4.54 us
  transfers between devices with their start and end apart: 3, of which 3 were waited for; matrix products, arithmetic and copies ran while one was open for 4% of the time, Pallas kernels for 0%

profile of v7, /device:TPU:1, one launch (start us, length us, event | category | flops | bytes accessed | tf_op | source)
XLA Modules:
  0.0 125.8 jit_solution(326563904948053817)
XLA Ops:
  0.0 1.8 %broadcast_in_dim.75 = bf16[64,4,1536]{2,1,0:T(4,128)(2,1)} broadcast(bf16[4,1536]{1,0:T(4,128)(2,1)} %bitcast.78), dimensions={1,2} | broadcast | bytes 798720 | tf_op jit(solution)/shard_map/token_exchange/broadcast_in_dim | solution.py:68
  1.9 12.0 %all-to-all-start = ((bf16[64,4,1536]{2,1,0:T(4,128)(2,1)}), bf16[64,4,1536]{2,1,0:T(4,128)(2,1)S(1)}, u32[]{:S(2)}, u32[]{:S(2)}) async-start(bf16[64,4,1536]{2,1,0:T(4,128)(2,1)} %broadcast_in_dim.75), calls=%async_computation | async-start | bytes 1572864 | tf_op jit(solution)/shard_map/token_exchange/all_to_all | solution.py:69
  16.6 12.2 %all-to-all-done = bf16[64,4,1536]{2,1,0:T(4,128)(2,1)S(1)} async-done(((bf16[64,4,1536]{2,1,0:T(4,128)(2,1)}), bf16[64,4,1536]{2,1,0:T(4,128)(2,1)S(1)}, u32[]{:S(2)}, u32[]{:S(2)}) %all-to-all-start) | async-done | bytes 786464 | tf_op jit(solution)/shard_map/token_exchange/all_to_all | solution.py:69
  29.8 4.6 %fusion = f32[64,4,2048]{2,0,1:T(8,128)S(1)} fusion(bf16[1536,2048]{1,0:T(8,128)(2,1)} %param.19, bf16[64,4,1536]{2,1,0:T(4,128)(2,1)S(1)} %fusion.9), kind=kOutput, calls=%fused_computation | convolution fusion | flops 1610612736 | bytes 9175040 | tf_op jit(solution)/shard_map/qkv_projection/dot_general | solution.py:73
  34.4 1.3 %copy-done.1 = f32[64,4,2048]{2,0,1:T(8,128)} copy-done((f32[64,4,2048]{2,0,1:T(8,128)}, f32[64,4,2048]{2,0,1:T(8,128)S(1)}, u32[]{:S(2)}) %copy-start.1) | copy-done | bytes 2097176
  35.7 1.3 slice.73
  37.0 1.5 %reshape.461 = f32[64,4,12,128]{3,2,0,1:T(8,128)S(1)} reshape(f32[64,4,1536]{2,0,1:T(8,128)} %slice.73) | data formatting | bytes 3145728 | tf_op jit(solution)/shard_map/qkv_projection/reshape | solution.py:77
  40.5 1.5 %copy-done.15 = bf16[64,64,256]{2,1,0:T(8,128)(2,1)S(1)} copy-done((bf16[64,64,256]{2,1,0:T(8,128)(2,1)S(1)}, bf16[64,64,256]{2,1,0:T(8,128)(2,1)}, u32[]{:S(2)}) %copy-start.15) | copy-done | bytes 2097176
  41.9 1.4 %fusion.18 = (f32[64,24]{1,0:T(8,128)S(1)}, f32[64,24,64]{2,1,0:T(8,128)S(1)}) fusion(s32[64,24]{1,0:T(8,128)S(1)} %broadcast_minimum_fusion, s32[64,64]{1,0:T(8,128)S(1)} %add_select_fusion, bf16[64,64,256]{2,1,0:T(8,128)(2,1)S(1)} %copy-done.15, bf16[64,24,128]{2,0,1:T(8,128)(2,1)S(1)} %get-tuple-element.14), kind=kOutput, calls=%fused_computation.42 | convolution fusion | flops 25557504 | bytes 1906688 | tf_op jit(solution)/shard_map/slot_attention/nrd,ncd->nrc/dot_general | solution.py:109
  43.5 2.0 %convolution_convert_fusion.3 = bf16[64,24,128]{2,1,0:T(8,128)(2,1)S(1)} fusion(bf16[64,64,256]{2,1,0:T(8,128)(2,1)} %param.17, f32[64,24,64]{2,1,0:T(8,128)S(1)} %get-tuple-element.30, f32[64,24]{1,0:T(8,128)S(1)} %copy.124, s32[64,24]{1,0:T(8,128)S(1)} %broadcast_minimum_fusion, s32[64,64]{1,0:T(8,128)S(1)} %add_select_fusion), kind=kOutput, calls=%fused_computation.28 | convolution fusion | flops 25755648 | bytes 1863680 | tf_op jit(solution)/shard_map/slot_attention/nrc,ncd->nrd/dot_general | solution.py:119
  45.5 2.4 %fusion.21 = (bf16[64,24]{1,0:T(8,128)(2,1)S(1)}, f32[64,24]{1,0:T(8,128)S(1)}, f32[64,24,64]{2,1,0:T(8,128)S(1)}) fusion(f32[64,24,64]{2,1,0:T(8,128)} %copy-done.18, f32[64,24]{1,0:T(8,128)S(1)} %copy.124, s32[64,24]{1,0:T(8,128)S(1)} %broadcast_minimum_fusion, s32[64,64]{1,0:T(8,128)S(1)} %add_select_fusion, bf16[64,64,256]{2,1,0:T(8,128)(2,1)} %param.16, ...), kind=kOutput, calls=%fused_computation.46 | convolution fusion | flops 25850880 | bytes 2659328 | tf_op jit(solution)/shard_map/slot_attention/nrd,ncd->nrc/dot_general | solution.py:109
  48.1 0.8 fusion.23
  48.9 1.9 %convolution_convert_fusion.2 = bf16[64,24,128]{2,1,0:T(8,128)(2,1)S(1)} fusion(bf16[64,64,256]{2,1,0:T(8,128)(2,1)} %param.17, f32[64,24,64]{2,1,0:T(8,128)S(1)} %get-tuple-element.31, f32[64,24]{1,0:T(8,128)S(1)} %copy.128, s32[64,24]{1,0:T(8,128)S(1)} %broadcast_minimum_fusion, s32[64,64]{1,0:T(8,128)S(1)} %add_select_fusion), kind=kOutput, calls=%fused_computation.27 | convolution fusion | flops 25755648 | bytes 1863680 | tf_op jit(solution)/shard_map/slot_attention/nrc,ncd->nrd/dot_general | solution.py:119
  51.3 1.0 pad_maximum_fusion
  52.4 5.0 %all-to-all-start.1 = ((bf16[64,56,128]{2,1,0:T(8,128)(2,1)}), bf16[64,56,128]{2,1,0:T(8,128)(2,1)S(1)}, u32[]{:S(2)}, u32[]{:S(2)}) async-start(bf16[64,56,128]{2,1,0:T(8,128)(2,1)} %pad_maximum_fusion), calls=%async_computation.1 | async-start | bytes 1835008 | tf_op jit(solution)/shard_map/partial_exchange/all_to_all | solution.py:140
  57.4 1.2 fusion.25
  58.9 13.3 %all-to-all-done.1 = bf16[64,56,128]{2,1,0:T(8,128)(2,1)S(1)} async-done(((bf16[64,56,128]{2,1,0:T(8,128)(2,1)}), bf16[64,56,128]{2,1,0:T(8,128)(2,1)S(1)}, u32[]{:S(2)}, u32[]{:S(2)}) %all-to-all-start.1) | async-done | bytes 917536 | tf_op jit(solution)/shard_map/partial_exchange/all_to_all | solution.py:140
  73.6 3.2 %multiply_reduce_fusion.1 = (f32[4]{0:T(128)S(1)}, f32[4,1536]{1,0:T(4,128)S(1)}) fusion(bf16[4,1536]{1,0:T(4,128)(2,1)S(1)} %convert_element_type.279, bf16[1536,1536]{1,0:T(8,128)(2,1)} %param.21, bf16[4,1,1536]{2,0,1:T(4,128)(2,1)S(1)} %copy-done.6), kind=kOutput, calls=%fused_computation.91 | convolution fusion | flops 18911228 | bytes 4767760 | tf_op jit(solution)/shard_map/attention_output/dot_general | solution.py:182
  78.0 22.4 %all_to_all.20 = bf16[128,2,1536]{2,1,0:T(2,128)(2,1)S(1)} all-to-all(bf16[128,2,1536]{2,1,0:T(2,128)(2,1)S(1)} %bitcast.76), channel_id=1, replica_groups=mesh['req'=2,'seq'=64] {'req','seq'}, dimensions={0} | all-to-all | bytes 1572864 | tf_op jit(solution)/shard_map/token_dispatch/all_to_all | solution.py:208
  101.2 1.1 convolution_convert_fusion
  102.4 1.2 reshape.466
  103.5 4.5 %all-to-all-start.3 = ((bf16[128,2,1536]{2,1,0:T(2,128)(2,1)}), bf16[128,2,1536]{2,1,0:T(2,128)(2,1)S(1)}, u32[]{:S(2)}, u32[]{:S(2)}) async-start(bf16[128,2,1536]{2,1,0:T(2,128)(2,1)} %reshape.466), calls=%async_computation.3 | async-start | bytes 1572864 | tf_op jit(solution)/shard_map/expert_return/all_to_all | solution.py:223
  109.0 15.1 %all-to-all-done.3 = bf16[128,2,1536]{2,1,0:T(2,128)(2,1)S(1)} async-done(((bf16[128,2,1536]{2,1,0:T(2,128)(2,1)}), bf16[128,2,1536]{2,1,0:T(2,128)(2,1)S(1)}, u32[]{:S(2)}, u32[]{:S(2)}) %all-to-all-start.3) | async-done | bytes 786464 | tf_op jit(solution)/shard_map/expert_return/all_to_all | solution.py:223
  124.9 1.0 fusion.6
  (112 shorter events, 11.5 us)
Async XLA Ops:
  0.0 101.2 %copy-start = (bf16[192,1536]{1,0:T(8,128)(2,1)S(1)}, bf16[192,1536]{1,0:T(8,128)(2,1)}, u32[]{:S(2)}) copy-start(bf16[192,1536]{1,0:T(8,128)(2,1)} %param.26) | copy-start | bytes 1769476
  0.0 13.9 %copy-start.10 = (s32[64]{0:T(128)S(1)}, s32[64]{0:T(128)}, u32[]{:S(2)}) copy-start(s32[64]{0:T(128)} %param.15) | copy-start | bytes 772
  0.0 15.2 %copy-start.17 = (f32[12]{0:T(128)S(1)}, f32[12]{0:T(128)}, u32[]{:S(2)}) copy-start(f32[12]{0:T(128)} %param.20) | copy-start | bytes 148
  0.0 15.3 %copy-start.9 = (s32[128,4,4]{0,2,1:T(4,128)S(1)}, s32[128,4,4]{0,2,1:T(4,128)}, u32[]{:S(2)}) copy-start(s32[128,4,4]{0,2,1:T(4,128)} %param.27) | copy-start | bytes 24580
  0.0 15.7 %copy-start.11 = (bf16[1536]{0:T(1024)(128)(2,1)S(1)}, bf16[1536]{0:T(1024)(128)(2,1)}, u32[]{:S(2)}) copy-start(bf16[1536]{0:T(1024)(128)(2,1)} %param.22) | copy-start | bytes 9220
  0.0 15.7 %copy-start.12 = (bf16[1536]{0:T(1024)(128)(2,1)S(1)}, bf16[1536]{0:T(1024)(128)(2,1)}, u32[]{:S(2)}) copy-start(bf16[1536]{0:T(1024)(128)(2,1)} %param.18) | copy-start | bytes 9220
  1.9 26.9 %all-to-all-start = ((bf16[64,4,1536]{2,1,0:T(4,128)(2,1)}), bf16[64,4,1536]{2,1,0:T(4,128)(2,1)S(1)}, u32[]{:S(2)}, u32[]{:S(2)}) async-start(bf16[64,4,1536]{2,1,0:T(4,128)(2,1)} %broadcast_in_dim.75), calls=%async_computation | async-start | bytes 1572864 | tf_op jit(solution)/shard_map/token_exchange/all_to_all | solution.py:69
  15.6 61.2 %copy-start.7 = (pred[4,32]{1,0:T(4,128)(4,1)}, pred[4,32]{1,0:T(4,128)(4,1)S(1)}, u32[]{:S(2)}) copy-start(pred[4,32]{1,0:T(4,128)(4,1)S(1)} %fusion.59) | copy-start | bytes 388
  34.3 1.4 %copy-start.1 = (f32[64,4,2048]{2,0,1:T(8,128)}, f32[64,4,2048]{2,0,1:T(8,128)S(1)}, u32[]{:S(2)}) copy-start(f32[64,4,2048]{2,0,1:T(8,128)S(1)} %fusion) | copy-start | bytes 6291460
  40.3 1.6 %copy-start.15 = (bf16[64,64,256]{2,1,0:T(8,128)(2,1)S(1)}, bf16[64,64,256]{2,1,0:T(8,128)(2,1)}, u32[]{:S(2)}) copy-start(bf16[64,64,256]{2,1,0:T(8,128)(2,1)} %param.16) | copy-start | bytes 6291460
  43.3 2.2 %copy-start.18 = (f32[64,24,64]{2,1,0:T(8,128)}, f32[64,24,64]{2,1,0:T(8,128)S(1)}, u32[]{:S(2)}) copy-start(f32[64,24,64]{2,1,0:T(8,128)S(1)} %get-tuple-element.30) | copy-start | bytes 1179652
  52.4 21.2 %copy-start.6 = (bf16[4,1,1536]{2,0,1:T(4,128)(2,1)S(1)}, bf16[4,1,1536]{2,0,1:T(4,128)(2,1)}, u32[]{:S(2)}) copy-start(bf16[4,1,1536]{2,0,1:T(4,128)(2,1)} %param.14) | copy-start | bytes 36868
  52.4 19.9 %all-to-all-start.1 = ((bf16[64,56,128]{2,1,0:T(8,128)(2,1)}), bf16[64,56,128]{2,1,0:T(8,128)(2,1)S(1)}, u32[]{:S(2)}, u32[]{:S(2)}) async-start(bf16[64,56,128]{2,1,0:T(8,128)(2,1)} %pad_maximum_fusion), calls=%async_computation.1 | async-start | bytes 1835008 | tf_op jit(solution)/shard_map/partial_exchange/all_to_all | solution.py:140
  76.8 0.6 copy-start.4
  76.8 1.2 copy-start.13
  77.6 23.2 %copy-start.2 = (bf16[1536,192]{0,1:T(8,128)(2,1)S(1)}, bf16[1536,192]{0,1:T(8,128)(2,1)}, u32[]{:S(2)}) copy-start(bf16[1536,192]{0,1:T(8,128)(2,1)} %param.24) | copy-start | bytes 1769476
  78.0 23.2 %copy-start.3 = (bf16[1536,192]{0,1:T(8,128)(2,1)S(1)}, bf16[1536,192]{0,1:T(8,128)(2,1)}, u32[]{:S(2)}) copy-start(bf16[1536,192]{0,1:T(8,128)(2,1)} %param.25) | copy-start | bytes 1769476
  102.3 5.8 %copy-start.5 = (f32[4,1536]{1,0:T(4,128)S(1)}, f32[4,1536]{1,0:T(4,128)}, u32[]{:S(2)}) copy-start(f32[4,1536]{1,0:T(4,128)} %copy-done.4) | copy-start | bytes 73732
  102.3 5.8 %copy-start.14 = (f32[4]{0:T(128)S(1)}, f32[4]{0:T(128)}, u32[]{:S(2)}) copy-start(f32[4]{0:T(128)} %copy-done.13) | copy-start | bytes 52
  102.4 5.8 %copy-start.16 = (bf16[1536,32]{0,1:T(8,128)(2,1)S(1)}, bf16[1536,32]{0,1:T(8,128)(2,1)}, u32[]{:S(2)}) copy-start(bf16[1536,32]{0,1:T(8,128)(2,1)} %param.23) | copy-start | bytes 294916
  102.4 22.5 %copy-start.8 = (pred[4,32]{1,0:T(4,128)(4,1)S(1)}, pred[4,32]{1,0:T(4,128)(4,1)}, u32[]{:S(2)}) copy-start(pred[4,32]{1,0:T(4,128)(4,1)} %copy-done.7) | copy-start | bytes 388
  103.5 20.6 %all-to-all-start.3 = ((bf16[128,2,1536]{2,1,0:T(2,128)(2,1)}), bf16[128,2,1536]{2,1,0:T(2,128)(2,1)S(1)}, u32[]{:S(2)}, u32[]{:S(2)}) async-start(bf16[128,2,1536]{2,1,0:T(2,128)(2,1)} %reshape.466), calls=%async_computation.3 | async-start | bytes 1572864 | tf_op jit(solution)/shard_map/expert_return/all_to_all | solution.py:223

commit v8 on v2

--- a/solution.py
+++ b/solution.py
@@ -68,6 +68,7 @@
         proj = jnp.dot(a, w_qkv, preferred_element_type=jnp.float32)
         place = own_len + step_ids
         query = rotate(proj[:, : QH * HD].reshape(STEPS, QH, HD), place).astype(jnp.bfloat16)
+    with jax.named_scope("fresh_key_value"):
         fresh_key = rotate(
             proj[:, QH * HD : (QH + KVH) * HD].reshape(STEPS, KVH, HD), place
         ).astype(jnp.bfloat16)
@@ -119,7 +120,7 @@
             ],
             axis=1,
         )
-        stats = jnp.pad(stats, ((0, 0), (0, 16 - 3), (0, HD - rows_q)))
+        stats = jnp.pad(stats, ((0, 0), (0, 8 - 3), (0, HD - rows_q)))
         packed = jnp.concatenate(mixed_heads + [stats], axis=1).astype(jnp.bfloat16)
 
     with jax.named_scope("partial_exchange"):

time: 121 us -> 119 us (0.983)
  waiting for transfers between devices: 45.5 us -> 44 us
    all_to_all x1, waiting for transfers between devices: 15.7 us -> 14.2 us  [on_device(): parts = lax.all_to_all(packed, 'seq', 0, 0, tiled=True)]
where the time goes in v8:
time: 119 us
  waiting for transfers between devices  44 us (37%)
  blocking collectives  22.4 us (19%)
  starting transfers between devices  21.3 us (18%)
  matrix products  17.2 us (14%)
  other arithmetic  8.69 us (7%)
  local copies, waits for them, and re-layouts  4.68 us (4%)
    all_to_all x1, blocking collectives, on_device(): arrived = lax.all_to_all(sent_u, ('req', 'seq'), 0, 0, tiled=True)  22.4 us
    all_to_all x1, waiting for transfers between devices, on_device(): returned = lax.all_to_all(produced, ('req', 'seq'), 0, 0, tiled=True)  15.1 us
    all_to_all x1, waiting for transfers between devices, on_device(): every_query = lax.all_to_all(sent_q, 'seq', 0, 0, tiled=True)  14.7 us
    all_to_all x1, waiting for transfers between devices, on_device(): parts = lax.all_to_all(packed, 'seq', 0, 0, tiled=True)  14.2 us
    all_to_all x1, starting transfers between devices, on_device(): every_query = lax.all_to_all(sent_q, 'seq', 0, 0, tiled=True)  12 us
    all_to_all x1, starting transfers between devices, on_device(): parts = lax.all_to_all(packed, 'seq', 0, 0, tiled=True)  4.78 us
    all_to_all x1, starting transfers between devices, on_device(): returned = lax.all_to_all(produced, ('req', 'seq'), 0, 0, tiled=True)  4.54 us
    dot_general x2, matrix products, on_device(): jnp.einsum('nrd,ncd->nrc', q_k, keys_k, preferred_element_type=jnp.float32)  4.1 us
  transfers between devices with their start and end apart: 3, of which 3 were waited for; matrix products, arithmetic and copies ran while one was open for 2% of the time, Pallas kernels for 0%

profile of v8, /device:TPU:1, one launch (start us, length us, event | category | flops | bytes accessed | tf_op | source)
XLA Modules:
  0.0 118.8 jit_solution(12296993356331657264)
XLA Ops:
  0.0 1.4 %broadcast_add_fusion.1 = (s32[64]{0:T(128)S(1)}, s32[]{:T(128)}) fusion(s32[64]{0:T(128)} %param.15, s32[]{:T(128)S(6)} %axis_index.22), kind=kLoop, calls=%fused_computation.155 | loop fusion | flops 255 | bytes 520 | tf_op jit(solution)/shard_map/slot_attention/sub | solution.py:86
  1.4 0.6 add_convert_fusion.2
  2.0 0.7 convert_element_type.240
  2.7 0.8 fusion.45
  3.6 3.8 %fusion.50 = f32[4,2048]{1,0:T(4,128)S(1)} fusion(bf16[1536,2048]{1,0:T(8,128)(2,1)} %param.19, bf16[4,1,1536]{2,0,1:T(4,128)(2,1)} %param.14, f32[1536]{0:T(1024)S(1)} %convert_element_type.240, f32[4]{0:T(128)S(1)} %add_rsqrt_fusion.1), kind=kOutput, calls=%fused_computation.93 | convolution fusion | flops 25190400 | bytes 6342672 | tf_op jit(solution)/shard_map/qkv_projection/dot_general | solution.py:68
  7.7 1.0 broadcast_in_dim.55
  8.7 12.0 %all-to-all-start = ((bf16[64,48,128]{2,1,0:T(8,128)(2,1)}), bf16[64,48,128]{2,1,0:T(8,128)(2,1)S(1)}, u32[]{:S(2)}, u32[]{:S(2)}) async-start(bf16[64,48,128]{2,1,0:T(8,128)(2,1)} %broadcast_in_dim.55), calls=%async_computation | async-start | bytes 1572864 | tf_op jit(solution)/shard_map/query_exchange/all_to_all | solution.py:82
  20.9 14.7 %all-to-all-done = bf16[64,48,128]{2,1,0:T(8,128)(2,1)S(1)} async-done(((bf16[64,48,128]{2,1,0:T(8,128)(2,1)}), bf16[64,48,128]{2,1,0:T(8,128)(2,1)S(1)}, u32[]{:S(2)}, u32[]{:S(2)}) %all-to-all-start) | async-done | bytes 786464 | tf_op jit(solution)/shard_map/query_exchange/all_to_all | solution.py:82
  35.6 2.0 %fusion.13 = (f32[64,24]{1,0:T(8,128)S(1)}, f32[64,24,64]{2,1,0:T(8,128)S(1)}) fusion(s32[64,24]{1,0:T(8,128)S(1)} %broadcast_minimum_fusion, s32[64,64]{1,0:T(8,128)S(1)} %add_select_fusion, bf16[64,64,256]{2,1,0:T(8,128)(2,1)} %param.16, bf16[64,48,128]{2,1,0:T(8,128)(2,1)S(1)} %all-to-all-done), kind=kOutput, calls=%fused_computation.32 | convolution fusion | flops 25557504 | bytes 1906688 | tf_op jit(solution)/shard_map/slot_attention/nrd,ncd->nrc/dot_general | solution.py:96
  37.7 2.1 %fusion.15 = (bf16[64,24]{1,0:T(8,128)(2,1)S(1)}, f32[64,24]{1,0:T(8,128)S(1)}, f32[64,24,64]{2,1,0:T(8,128)S(1)}) fusion(f32[64,24,64]{2,1,0:T(8,128)S(1)} %get-tuple-element.24, f32[64,24]{1,0:T(8,128)S(1)} %copy.106, s32[64,24]{1,0:T(8,128)S(1)} %broadcast_minimum_fusion, s32[64,64]{1,0:T(8,128)S(1)} %add_select_fusion, bf16[64,64,256]{2,1,0:T(8,128)(2,1)} %param.16, ...), kind=kOutput, calls=%fused_computation.34 | convolution fusion | flops 25850880 | bytes 2728960 | tf_op jit(solution)/shard_map/slot_attention/nrd,ncd->nrc/dot_general | solution.py:96
  40.0 0.8 fusion.17
  40.9 1.9 %convolution_convert_fusion.2 = bf16[64,24,128]{2,1,0:T(8,128)(2,1)S(1)} fusion(bf16[64,64,256]{2,1,0:T(8,128)(2,1)} %param.17, f32[64,24,64]{2,1,0:T(8,128)S(1)} %get-tuple-element.25, f32[64,24]{1,0:T(8,128)S(1)} %copy.109, s32[64,24]{1,0:T(8,128)S(1)} %broadcast_minimum_fusion, s32[64,64]{1,0:T(8,128)S(1)} %add_select_fusion), kind=kOutput, calls=%fused_computation.17 | convolution fusion | flops 25755648 | bytes 1863680 | tf_op jit(solution)/shard_map/slot_attention/nrc,ncd->nrd/dot_general | solution.py:106
  42.7 0.9 convolution_convert_fusion.3
  44.2 1.0 pad_maximum_fusion
  45.2 4.8 %all-to-all-start.1 = ((bf16[64,56,128]{2,1,0:T(8,128)(2,1)}), bf16[64,56,128]{2,1,0:T(8,128)(2,1)S(1)}, u32[]{:S(2)}, u32[]{:S(2)}) async-start(bf16[64,56,128]{2,1,0:T(8,128)(2,1)} %pad_maximum_fusion), calls=%async_computation.1 | async-start | bytes 1835008 | tf_op jit(solution)/shard_map/partial_exchange/all_to_all | solution.py:127
  50.9 14.2 %all-to-all-done.1 = bf16[64,56,128]{2,1,0:T(8,128)(2,1)S(1)} async-done(((bf16[64,56,128]{2,1,0:T(8,128)(2,1)}), bf16[64,56,128]{2,1,0:T(8,128)(2,1)S(1)}, u32[]{:S(2)}, u32[]{:S(2)}) %all-to-all-start.1) | async-done | bytes 917536 | tf_op jit(solution)/shard_map/partial_exchange/all_to_all | solution.py:127
  66.4 3.2 %multiply_reduce_fusion.1 = (f32[4]{0:T(128)S(1)}, f32[4,1536]{1,0:T(4,128)S(1)}) fusion(bf16[4,1536]{1,0:T(4,128)(2,1)S(1)} %convert_element_type.260, bf16[1536,1536]{1,0:T(8,128)(2,1)} %param.21, bf16[4,1,1536]{2,0,1:T(4,128)(2,1)S(1)} %copy-done.5), kind=kOutput, calls=%fused_computation.81 | convolution fusion | flops 18911228 | bytes 4767760 | tf_op jit(solution)/shard_map/attention_output/dot_general | solution.py:169
  71.0 22.4 %all_to_all.20 = bf16[128,2,1536]{2,1,0:T(2,128)(2,1)S(1)} all-to-all(bf16[128,2,1536]{2,1,0:T(2,128)(2,1)S(1)} %bitcast.75), channel_id=1, replica_groups=mesh['req'=2,'seq'=64] {'req','seq'}, dimensions={0} | all-to-all | bytes 1572864 | tf_op jit(solution)/shard_map/token_dispatch/all_to_all | solution.py:195
  94.2 1.1 convolution_convert_fusion
  95.4 1.2 reshape.406
  96.6 4.5 %all-to-all-start.3 = ((bf16[128,2,1536]{2,1,0:T(2,128)(2,1)}), bf16[128,2,1536]{2,1,0:T(2,128)(2,1)S(1)}, u32[]{:S(2)}, u32[]{:S(2)}) async-start(bf16[128,2,1536]{2,1,0:T(2,128)(2,1)} %reshape.406), calls=%async_computation.3 | async-start | bytes 1572864 | tf_op jit(solution)/shard_map/expert_return/all_to_all | solution.py:210
  102.0 15.1 %all-to-all-done.3 = bf16[128,2,1536]{2,1,0:T(2,128)(2,1)S(1)} async-done(((bf16[128,2,1536]{2,1,0:T(2,128)(2,1)}), bf16[128,2,1536]{2,1,0:T(2,128)(2,1)S(1)}, u32[]{:S(2)}, u32[]{:S(2)}) %all-to-all-start.3) | async-done | bytes 786464 | tf_op jit(solution)/shard_map/expert_return/all_to_all | solution.py:210
  117.1 0.7 convert_reduce_fusion
  117.9 1.0 fusion.4
  (101 shorter events, 6.5 us)
Async XLA Ops:
  0.0 94.2 %copy-start = (bf16[192,1536]{1,0:T(8,128)(2,1)S(1)}, bf16[192,1536]{1,0:T(8,128)(2,1)}, u32[]{:S(2)}) copy-start(bf16[192,1536]{1,0:T(8,128)(2,1)} %param.26) | copy-start | bytes 1769476
  7.3 13.4 %copy-start.10 = (s32[64]{0:T(128)S(1)}, s32[64]{0:T(128)}, u32[]{:S(2)}) copy-start(s32[64]{0:T(128)} %param.15) | copy-start | bytes 772
  8.7 26.9 %all-to-all-start = ((bf16[64,48,128]{2,1,0:T(8,128)(2,1)}), bf16[64,48,128]{2,1,0:T(8,128)(2,1)S(1)}, u32[]{:S(2)}, u32[]{:S(2)}) async-start(bf16[64,48,128]{2,1,0:T(8,128)(2,1)} %broadcast_in_dim.55), calls=%async_computation | async-start | bytes 1572864 | tf_op jit(solution)/shard_map/query_exchange/all_to_all | solution.py:82
  40.0 2.7 %copy-start.13 = (bf16[64,64,256]{2,1,0:T(8,128)(2,1)S(1)}, bf16[64,64,256]{2,1,0:T(8,128)(2,1)}, u32[]{:S(2)}) copy-start(bf16[64,64,256]{2,1,0:T(8,128)(2,1)} %param.17) | copy-start | bytes 6291460
  43.6 6.5 %copy-start.15 = (f32[12]{0:T(128)S(1)}, f32[12]{0:T(128)}, u32[]{:S(2)}) copy-start(f32[12]{0:T(128)} %param.20) | copy-start | bytes 148
  43.7 6.9 %copy-start.9 = (bf16[1536]{0:T(1024)(128)(2,1)S(1)}, bf16[1536]{0:T(1024)(128)(2,1)}, u32[]{:S(2)}) copy-start(bf16[1536]{0:T(1024)(128)(2,1)} %param.22) | copy-start | bytes 9220
  43.7 6.9 %copy-start.8 = (s32[128,4,4]{0,2,1:T(4,128)S(1)}, s32[128,4,4]{0,2,1:T(4,128)}, u32[]{:S(2)}) copy-start(s32[128,4,4]{0,2,1:T(4,128)} %param.27) | copy-start | bytes 24580
  45.2 21.2 %copy-start.5 = (bf16[4,1,1536]{2,0,1:T(4,128)(2,1)S(1)}, bf16[4,1,1536]{2,0,1:T(4,128)(2,1)}, u32[]{:S(2)}) copy-start(bf16[4,1,1536]{2,0,1:T(4,128)(2,1)} %param.14) | copy-start | bytes 36868
  45.2 19.9 %all-to-all-start.1 = ((bf16[64,56,128]{2,1,0:T(8,128)(2,1)}), bf16[64,56,128]{2,1,0:T(8,128)(2,1)S(1)}, u32[]{:S(2)}, u32[]{:S(2)}) async-start(bf16[64,56,128]{2,1,0:T(8,128)(2,1)} %pad_maximum_fusion), calls=%async_computation.1 | async-start | bytes 1835008 | tf_op jit(solution)/shard_map/partial_exchange/all_to_all | solution.py:127
  50.8 18.8 %copy-start.6 = (pred[4,32]{1,0:T(4,128)(4,1)}, pred[4,32]{1,0:T(4,128)(4,1)S(1)}, u32[]{:S(2)}) copy-start(pred[4,32]{1,0:T(4,128)(4,1)S(1)} %fusion.59) | copy-start | bytes 388
  69.6 0.8 copy-start.3
  69.6 0.5 copy-start.11
  70.6 23.2 %copy-start.1 = (bf16[1536,192]{0,1:T(8,128)(2,1)S(1)}, bf16[1536,192]{0,1:T(8,128)(2,1)}, u32[]{:S(2)}) copy-start(bf16[1536,192]{0,1:T(8,128)(2,1)} %param.24) | copy-start | bytes 1769476
  71.0 23.2 %copy-start.2 = (bf16[1536,192]{0,1:T(8,128)(2,1)S(1)}, bf16[1536,192]{0,1:T(8,128)(2,1)}, u32[]{:S(2)}) copy-start(bf16[1536,192]{0,1:T(8,128)(2,1)} %param.25) | copy-start | bytes 1769476
  95.4 5.8 %copy-start.4 = (f32[4,1536]{1,0:T(4,128)S(1)}, f32[4,1536]{1,0:T(4,128)}, u32[]{:S(2)}) copy-start(f32[4,1536]{1,0:T(4,128)} %copy-done.3) | copy-start | bytes 73732
  95.4 5.8 %copy-start.12 = (f32[4]{0:T(128)S(1)}, f32[4]{0:T(128)}, u32[]{:S(2)}) copy-start(f32[4]{0:T(128)} %copy-done.11) | copy-start | bytes 52
  95.4 5.8 %copy-start.14 = (bf16[1536,32]{0,1:T(8,128)(2,1)S(1)}, bf16[1536,32]{0,1:T(8,128)(2,1)}, u32[]{:S(2)}) copy-start(bf16[1536,32]{0,1:T(8,128)(2,1)} %param.23) | copy-start | bytes 294916
  95.4 22.5 %copy-start.7 = (pred[4,32]{1,0:T(4,128)(4,1)S(1)}, pred[4,32]{1,0:T(4,128)(4,1)}, u32[]{:S(2)}) copy-start(pred[4,32]{1,0:T(4,128)(4,1)} %copy-done.6) | copy-start | bytes 388
  96.6 20.6 %all-to-all-start.3 = ((bf16[128,2,1536]{2,1,0:T(2,128)(2,1)}), bf16[128,2,1536]{2,1,0:T(2,128)(2,1)S(1)}, u32[]{:S(2)}, u32[]{:S(2)}) async-start(bf16[128,2,1536]{2,1,0:T(2,128)(2,1)} %reshape.406), calls=%async_computation.3 | async-start | bytes 1572864 | tf_op jit(solution)/shard_map/expert_return/all_to_all | solution.py:210

commit v9 on v3

--- a/solution.py
+++ b/solution.py
@@ -88,10 +88,13 @@
         reach = jnp.minimum(lengths[:, None], window - 1 - row_step[None, :])
         valid = back[:, None, :] < reach[:, :, None]
         mixed_heads, total_heads, hi_heads, mid_heads = [], [], [], []
+        halves = lax.optimization_barrier(
+            tuple(c[:, :, k * HD : (k + 1) * HD] for c in (k_cache, v_cache) for k in range(KVH))
+        )
         for k in range(KVH):
             q_k = every_query[:, k * per_head : (k + 1) * per_head, :]
-            keys_k = k_cache[:, :, k * HD : (k + 1) * HD]
-            vals_k = v_cache[:, :, k * HD : (k + 1) * HD]
+            keys_k = halves[k]
+            vals_k = halves[KVH + k]
             scores = (
                 jnp.einsum("nrd,ncd->nrc", q_k, keys_k, preferred_element_type=jnp.float32)
                 * scale

time: 119 us -> 135 us (1.13)
  local copies, waits for them, and re-layouts: 4.38 us -> 15.4 us
  waiting for transfers between devices: 44.1 us -> 38.3 us
  other arithmetic: 8.71 us -> 14.2 us
  matrix products: 17.2 us -> 21.9 us
    all_to_all x1, waiting for transfers between devices: 14.7 us -> 8.97 us  [on_device(): every_query = lax.all_to_all(sent_q, 'seq', 0, 0, tiled=True)]
    slice x0 -> x1, local copies, waits for them, and re-layouts: none -> 4.51 us  [on_device(): c[:, :, k * HD:(k + 1) * HD]]
    reduce_max x2, local copies, waits for them, and re-layouts: 0.13 us -> 2.86 us  [on_device(): peak = jnp.max(jnp.where(valid, scores, -1e+30), axis=-1)]
    dot_general x2, matrix products: 4.09 us -> 6.81 us  [on_device(): jnp.einsum('nrd,ncd->nrc', q_k, keys_k, preferred_element_type=jnp.float32)]
    add x2, local copies, waits for them, and re-layouts: 0.17 us -> 2.78 us  [on_device(): shard_peak = hi.astype(jnp.float32) + mid.astype(jnp.float32)]
    add x1, other arithmetic: 0.01 us -> 1.39 us  [on_device(): shard_peak = hi.astype(jnp.float32) + mid.astype(jnp.float32)]
    concatenate x2, other arithmetic: 0.02 us -> 1.4 us  [on_device(): jnp.concatenate(hi_heads, axis=1).astype(jnp.float32)]
  transfers between devices with their start and end apart: 3 -> 3, of which waited for: 3 -> 3; matrix products, arithmetic and copies ran while one was open for 2% -> 6% of each run, Pallas kernels for 0% -> 0%
where the time goes in v9:
time: 135 us; the launch traced here: 134 us
  waiting for transfers between devices  38.3 us (28%)
  blocking collectives  22.4 us (17%)
  matrix products  21.9 us (16%)
  starting transfers between devices  21.3 us (16%)
  local copies, waits for them, and re-layouts  15.4 us (11%)
  other arithmetic  14.2 us (11%)
    all_to_all x1, blocking collectives, on_device(): arrived = lax.all_to_all(sent_u, ('req', 'seq'), 0, 0, tiled=True)  22.4 us
    all_to_all x1, waiting for transfers between devices, on_device(): returned = lax.all_to_all(produced, ('req', 'seq'), 0, 0, tiled=True)  15.1 us
    all_to_all x1, waiting for transfers between devices, on_device(): parts = lax.all_to_all(packed, 'seq', 0, 0, tiled=True)  14.2 us
    all_to_all x1, starting transfers between devices, on_device(): every_query = lax.all_to_all(sent_q, 'seq', 0, 0, tiled=True)  12 us
    all_to_all x1, waiting for transfers between devices, on_device(): every_query = lax.all_to_all(sent_q, 'seq', 0, 0, tiled=True)  8.97 us
    dot_general x2, matrix products, on_device(): jnp.einsum('nrd,ncd->nrc', q_k, keys_k, preferred_element_type=jnp.float32)  6.81 us
    all_to_all x1, starting transfers between devices, on_device(): parts = lax.all_to_all(packed, 'seq', 0, 0, tiled=True)  4.78 us
    all_to_all x1, starting transfers between devices, on_device(): returned = lax.all_to_all(produced, ('req', 'seq'), 0, 0, tiled=True)  4.54 us
  transfers between devices with their start and end apart: 3, of which 3 were waited for; matrix products, arithmetic and copies ran while one was open for 6% of the time, Pallas kernels for 0%

profile of v9, /device:TPU:1, one launch (start us, length us, event | category | flops | bytes accessed | tf_op | source)
XLA Modules:
  0.0 133.9 jit_solution(426053137232045045)
XLA Ops:
  0.0 1.9 %broadcast_add_fusion.1 = (s32[64]{0:T(128)}, s32[]{:T(128)}) fusion(s32[64]{0:T(128)} %param.15, s32[]{:T(128)S(6)} %axis_index.22), kind=kLoop, calls=%fused_computation.156 | loop fusion | flops 255 | bytes 520 | tf_op jit(solution)/shard_map/slot_attention/sub | solution.py:86
  4.2 3.8 %fusion.53 = f32[4,2048]{1,0:T(4,128)S(1)} fusion(bf16[1536,2048]{1,0:T(8,128)(2,1)} %param.19, bf16[4,1,1536]{2,0,1:T(4,128)(2,1)} %param.14, f32[1536]{0:T(1024)S(1)} %convert_element_type.240, f32[4]{0:T(128)S(1)} %add_rsqrt_fusion.1), kind=kOutput, calls=%fused_computation.94 | convolution fusion | flops 25190400 | bytes 6342672 | tf_op jit(solution)/shard_map/qkv_projection/dot_general | solution.py:68
  9.8 12.0 %all-to-all-start = ((bf16[64,48,128]{2,1,0:T(8,128)(2,1)}), bf16[64,48,128]{2,1,0:T(8,128)(2,1)S(1)}, u32[]{:S(2)}, u32[]{:S(2)}) async-start(bf16[64,48,128]{2,1,0:T(8,128)(2,1)} %broadcast_in_dim.55), calls=%async_computation | async-start | bytes 1572864 | tf_op jit(solution)/shard_map/query_exchange/all_to_all | solution.py:82
  21.8 4.5 %fusion.93 = (bf16[64,64,128]{2,1,0:T(8,128)(2,1)S(1)}, bf16[64,64,128]{2,1,0:T(8,128)(2,1)S(1)}, bf16[64,64,128]{2,1,0:T(8,128)(2,1)}, bf16[64,64,128]{2,1,0:T(8,128)(2,1)}) fusion(bf16[64,64,256]{2,1,0:T(8,128)(2,1)} %param.17, bf16[64,64,256]{2,1,0:T(8,128)(2,1)} %param.16), kind=kLoop, calls=%fused_computation.164 | loop fusion | bytes 8388608 | tf_op jit(solution)/shard_map/slot_attention/slice | solution.py:92
  27.8 9.0 %all-to-all-done = bf16[64,48,128]{2,1,0:T(8,128)(2,1)S(1)} async-done(((bf16[64,48,128]{2,1,0:T(8,128)(2,1)}), bf16[64,48,128]{2,1,0:T(8,128)(2,1)S(1)}, u32[]{:S(2)}, u32[]{:S(2)}) %all-to-all-start) | async-done | bytes 786464 | tf_op jit(solution)/shard_map/query_exchange/all_to_all | solution.py:82
  36.7 3.7 %fusion.9 = (f32[64,24]{1,0:T(8,128)}, f32[64,24,64]{2,1,0:T(8,128)}) fusion(s32[64,24]{1,0:T(8,128)S(1)} %broadcast_minimum_fusion, s32[64,64]{1,0:T(8,128)S(1)} %add_select_fusion, bf16[64,64,128]{2,1,0:T(8,128)(2,1)} %get-tuple-element.9, bf16[64,48,128]{2,1,0:T(8,128)(2,1)S(1)} %all-to-all-done), kind=kOutput, calls=%fused_computation.28 | convolution fusion | flops 25557504 | bytes 1906688 | tf_op jit(solution)/shard_map/slot_attention/nrd,ncd->nrc/dot_general | solution.py:99
  40.4 1.4 %copy.128 = f32[64,24]{0,1:T(8,128)} copy(f32[64,24]{1,0:T(8,128)} %get-tuple-element.35) | data formatting | bytes 12288 | tf_op jit(solution)/shard_map/slot_attention/reduce_max | solution.py:102
  41.9 1.4 %convert_bitcast_fusion.1 = (bf16[64,1,24]{0,2,1:T(8,128)(2,1)}, f32[64,24]{0,1:T(8,128)}, bf16[64,1,24]{0,2,1:T(8,128)(2,1)}) fusion(f32[64,24]{0,1:T(8,128)} %copy.128), kind=kLoop, calls=%fused_computation.113 | loop fusion | flops 9216 | bytes 18432 | tf_op jit(solution)/shard_map/slot_attention/concatenate | solution.py:121
  43.3 1.4 %copy.130 = f32[64,24]{1,0:T(8,128)} copy(f32[64,24]{0,1:T(8,128)} %get-tuple-element.27) | data formatting | bytes 12288 | tf_op jit(solution)/shard_map/slot_attention/add | solution.py:105
  44.7 3.1 %fusion.14 = (bf16[64,24]{1,0:T(8,128)(2,1)}, f32[64,24]{1,0:T(8,128)}, f32[64,24,64]{2,1,0:T(8,128)S(1)}) fusion(f32[64,24,64]{2,1,0:T(8,128)} %get-tuple-element.36, f32[64,24]{1,0:T(8,128)} %copy.130, s32[64,24]{1,0:T(8,128)S(1)} %broadcast_minimum_fusion, s32[64,64]{1,0:T(8,128)S(1)} %add_select_fusion, bf16[64,64,128]{2,1,0:T(8,128)(2,1)} %get-tuple-element.11, ...), kind=kOutput, calls=%fused_computation.32 | convolution fusion | flops 25850880 | bytes 2685952 | tf_op jit(solution)/shard_map/slot_attention/nrd,ncd->nrc/dot_general | solution.py:99
  47.8 1.4 %copy.131 = f32[64,24]{0,1:T(8,128)} copy(f32[64,24]{1,0:T(8,128)} %get-tuple-element.14) | data formatting | bytes 12288 | tf_op jit(solution)/shard_map/slot_attention/reduce_max | solution.py:102
  49.2 1.4 %convert_add_fusion = (f32[64,24]{0,1:T(8,128)}, bf16[64,1,24]{0,2,1:T(8,128)(2,1)}, bf16[64,1,24]{0,2,1:T(8,128)(2,1)}) fusion(f32[64,24]{0,1:T(8,128)} %copy.131), kind=kLoop, calls=%fused_computation.88 | loop fusion | flops 9216 | bytes 18432 | tf_op jit(solution)/shard_map/slot_attention/add | solution.py:105
  50.6 1.4 %copy.133 = f32[64,24]{1,0:T(8,128)} copy(f32[64,24]{0,1:T(8,128)} %get-tuple-element.23) | data formatting | bytes 12288 | tf_op jit(solution)/shard_map/slot_attention/add | solution.py:105
  52.0 1.6 %fusion.16 = bf16[64,24]{1,0:T(8,128)(2,1)S(1)} fusion(f32[64,24,64]{2,1,0:T(8,128)S(1)} %get-tuple-element.37, f32[64,24]{1,0:T(8,128)} %copy.133, s32[64,24]{1,0:T(8,128)S(1)} %broadcast_minimum_fusion, s32[64,64]{1,0:T(8,128)S(1)} %add_select_fusion), kind=kLoop, calls=%fused_computation.34 | loop fusion | flops 391680 | bytes 424960 | tf_op jit(solution)/shard_map/slot_attention/reduce_sum | solution.py:107
  53.6 2.2 %convolution_convert_fusion.2 = bf16[64,24,128]{2,1,0:T(8,128)(2,1)} fusion(bf16[64,64,128]{2,1,0:T(8,128)(2,1)S(1)} %get-tuple-element.12, f32[64,24,64]{2,1,0:T(8,128)S(1)} %get-tuple-element.37, f32[64,24]{1,0:T(8,128)} %copy.133, s32[64,24]{1,0:T(8,128)S(1)} %broadcast_minimum_fusion, s32[64,64]{1,0:T(8,128)S(1)} %add_select_fusion), kind=kOutput, calls=%fused_computation.17 | convolution fusion | flops 25755648 | bytes 1863680 | tf_op jit(solution)/shard_map/slot_attention/nrc,ncd->nrd/dot_general | solution.py:109
  56.9 1.8 %convolution_convert_fusion.3 = bf16[64,24,128]{2,1,0:T(8,128)(2,1)S(1)} fusion(bf16[64,64,128]{2,1,0:T(8,128)(2,1)S(1)} %get-tuple-element.10, f32[64,24,64]{2,1,0:T(8,128)} %get-tuple-element.36, f32[64,24]{1,0:T(8,128)} %copy.130, s32[64,24]{1,0:T(8,128)S(1)} %broadcast_minimum_fusion, s32[64,64]{1,0:T(8,128)S(1)} %add_select_fusion), kind=kOutput, calls=%fused_computation.18 | convolution fusion | flops 25755648 | bytes 1863680 | tf_op jit(solution)/shard_map/slot_attention/nrc,ncd->nrd/dot_general | solution.py:109
  60.0 4.8 %all-to-all-start.1 = ((bf16[64,56,128]{2,1,0:T(8,128)(2,1)}), bf16[64,56,128]{2,1,0:T(8,128)(2,1)S(1)}, u32[]{:S(2)}, u32[]{:S(2)}) async-start(bf16[64,56,128]{2,1,0:T(8,128)(2,1)} %pad_maximum_fusion), calls=%async_computation.1 | async-start | bytes 1835008 | tf_op jit(solution)/shard_map/partial_exchange/all_to_all | solution.py:130
  65.7 14.2 %all-to-all-done.1 = bf16[64,56,128]{2,1,0:T(8,128)(2,1)S(1)} async-done(((bf16[64,56,128]{2,1,0:T(8,128)(2,1)}), bf16[64,56,128]{2,1,0:T(8,128)(2,1)S(1)}, u32[]{:S(2)}, u32[]{:S(2)}) %all-to-all-start.1) | async-done | bytes 917536 | tf_op jit(solution)/shard_map/partial_exchange/all_to_all | solution.py:130
  81.9 3.2 %multiply_reduce_fusion.1 = (f32[4]{0:T(128)S(1)}, f32[4,1536]{1,0:T(4,128)S(1)}) fusion(bf16[4,1536]{1,0:T(4,128)(2,1)S(1)} %convert_element_type.260, bf16[1536,1536]{1,0:T(8,128)(2,1)} %param.21, bf16[4,1,1536]{2,0,1:T(4,128)(2,1)S(1)} %copy-done.5), kind=kOutput, calls=%fused_computation.82 | convolution fusion | flops 18911228 | bytes 4767760 | tf_op jit(solution)/shard_map/attention_output/dot_general | solution.py:172
  86.0 22.4 %all_to_all.20 = bf16[128,2,1536]{2,1,0:T(2,128)(2,1)S(1)} all-to-all(bf16[128,2,1536]{2,1,0:T(2,128)(2,1)S(1)} %bitcast.84), channel_id=1, replica_groups=mesh['req'=2,'seq'=64] {'req','seq'}, dimensions={0} | all-to-all | bytes 1572864 | tf_op jit(solution)/shard_map/token_dispatch/all_to_all | solution.py:198
  108.8 1.2 convolution_convert_fusion
  110.0 1.7 %copy.145 = bf16[128,2,1536]{2,1,0:T(2,128)(2,1)} copy(bf16[128,2,1536]{2,0,1:T(8,128)(2,1)S(1)} %convolution_convert_fusion) | data formatting | bytes 1572864 | tf_op jit(solution)/shard_map/expert_quarter/convert_element_type | solution.py:207
  111.7 4.5 %all-to-all-start.3 = ((bf16[128,2,1536]{2,1,0:T(2,128)(2,1)}), bf16[128,2,1536]{2,1,0:T(2,128)(2,1)S(1)}, u32[]{:S(2)}, u32[]{:S(2)}) async-start(bf16[128,2,1536]{2,1,0:T(2,128)(2,1)} %copy.145), calls=%async_computation.3 | async-start | bytes 1572864 | tf_op jit(solution)/shard_map/expert_return/all_to_all | solution.py:210
  117.1 15.1 %all-to-all-done.3 = bf16[128,2,1536]{2,1,0:T(2,128)(2,1)S(1)} async-done(((bf16[128,2,1536]{2,1,0:T(2,128)(2,1)}), bf16[128,2,1536]{2,1,0:T(2,128)(2,1)S(1)}, u32[]{:S(2)}, u32[]{:S(2)}) %all-to-all-start.3) | async-done | bytes 786464 | tf_op jit(solution)/shard_map/expert_return/all_to_all | solution.py:210
  (110 shorter events, 14.5 us)
Async XLA Ops:
  0.0 108.8 %copy-start = (bf16[192,1536]{1,0:T(8,128)(2,1)S(1)}, bf16[192,1536]{1,0:T(8,128)(2,1)}, u32[]{:S(2)}) copy-start(bf16[192,1536]{1,0:T(8,128)(2,1)} %param.26) | copy-start | bytes 1769476
  7.9 18.4 %copy-start.4 = (f32[4,2048]{1,0:T(4,128)}, f32[4,2048]{1,0:T(4,128)S(1)}, u32[]{:S(2)}) copy-start(f32[4,2048]{1,0:T(4,128)S(1)} %fusion.53) | copy-start | bytes 98308
  8.1 0.6 copy-start.9
  8.1 0.6 copy-start.11
  9.8 26.9 %all-to-all-start = ((bf16[64,48,128]{2,1,0:T(8,128)(2,1)}), bf16[64,48,128]{2,1,0:T(8,128)(2,1)S(1)}, u32[]{:S(2)}, u32[]{:S(2)}) async-start(bf16[64,48,128]{2,1,0:T(8,128)(2,1)} %broadcast_in_dim.55), calls=%async_computation | async-start | bytes 1572864 | tf_op jit(solution)/shard_map/query_exchange/all_to_all | solution.py:82
  21.8 5.1 %copy-start.16 = (s32[64]{0:T(128)S(1)}, s32[64]{0:T(128)}, u32[]{:S(2)}) copy-start(s32[64]{0:T(128)} %param.15) | copy-start | bytes 772
  36.7 7.9 %copy-start.1 = (bf16[64,48,128]{2,1,0:T(8,128)(2,1)}, bf16[64,48,128]{2,1,0:T(8,128)(2,1)S(1)}, u32[]{:S(2)}) copy-start(bf16[64,48,128]{2,1,0:T(8,128)(2,1)S(1)} %all-to-all-done) | copy-start | bytes 2359300
  52.0 3.8 %copy-start.13 = (bf16[64,24]{1,0:T(8,128)(2,1)S(1)}, bf16[64,24]{1,0:T(8,128)(2,1)}, u32[]{:S(2)}) copy-start(bf16[64,24]{1,0:T(8,128)(2,1)} %get-tuple-element.13) | copy-start | bytes 9220
  52.0 3.9 %copy-start.7 = (bf16[64,1,24]{0,2,1:T(8,128)(2,1)S(1)}, bf16[64,1,24]{0,2,1:T(8,128)(2,1)}, u32[]{:S(2)}) copy-start(bf16[64,1,24]{0,2,1:T(8,128)(2,1)} %get-tuple-element.26) | copy-start | bytes 9220
  52.0 3.9 %copy-start.8 = (bf16[64,1,24]{0,2,1:T(8,128)(2,1)S(1)}, bf16[64,1,24]{0,2,1:T(8,128)(2,1)}, u32[]{:S(2)}) copy-start(bf16[64,1,24]{0,2,1:T(8,128)(2,1)} %get-tuple-element.25) | copy-start | bytes 9220
  55.8 3.1 %copy-start.2 = (bf16[64,24,128]{2,1,0:T(8,128)(2,1)S(1)}, bf16[64,24,128]{2,1,0:T(8,128)(2,1)}, u32[]{:S(2)}) copy-start(bf16[64,24,128]{2,1,0:T(8,128)(2,1)} %convolution_convert_fusion.2) | copy-start | bytes 1179652
  58.7 6.1 %copy-start.6 = (f32[4,2,128]{2,0,1:T(4,128)S(1)}, f32[4,2,128]{2,0,1:T(4,128)}, u32[]{:S(2)}) copy-start(f32[4,2,128]{2,0,1:T(4,128)} %slice_bitcast_fusion) | copy-start | bytes 12292
  58.7 6.1 %copy-start.10 = (f32[4,64]{1,0:T(4,128)S(1)}, f32[4,64]{1,0:T(4,128)}, u32[]{:S(2)}) copy-start(f32[4,64]{1,0:T(4,128)} %copy-done.9) | copy-start | bytes 3076
  58.7 6.1 %copy-start.12 = (f32[4,64]{1,0:T(4,128)S(1)}, f32[4,64]{1,0:T(4,128)}, u32[]{:S(2)}) copy-start(f32[4,64]{1,0:T(4,128)} %copy-done.11) | copy-start | bytes 3076
  58.7 6.2 %copy-start.19 = (f32[12]{0:T(128)S(1)}, f32[12]{0:T(128)}, u32[]{:S(2)}) copy-start(f32[12]{0:T(128)} %param.20) | copy-start | bytes 148
  58.7 6.7 %copy-start.15 = (bf16[1536]{0:T(1024)(128)(2,1)S(1)}, bf16[1536]{0:T(1024)(128)(2,1)}, u32[]{:S(2)}) copy-start(bf16[1536]{0:T(1024)(128)(2,1)} %param.22) | copy-start | bytes 9220
  58.7 6.7 %copy-start.14 = (s32[128,4,4]{0,2,1:T(4,128)S(1)}, s32[128,4,4]{0,2,1:T(4,128)}, u32[]{:S(2)}) copy-start(s32[128,4,4]{0,2,1:T(4,128)} %param.27) | copy-start | bytes 24580
  60.0 21.9 %copy-start.5 = (bf16[4,1,1536]{2,0,1:T(4,128)(2,1)S(1)}, bf16[4,1,1536]{2,0,1:T(4,128)(2,1)}, u32[]{:S(2)}) copy-start(bf16[4,1,1536]{2,0,1:T(4,128)(2,1)} %param.14) | copy-start | bytes 36868
  60.0 19.9 %all-to-all-start.1 = ((bf16[64,56,128]{2,1,0:T(8,128)(2,1)}), bf16[64,56,128]{2,1,0:T(8,128)(2,1)S(1)}, u32[]{:S(2)}, u32[]{:S(2)}) async-start(bf16[64,56,128]{2,1,0:T(8,128)(2,1)} %pad_maximum_fusion), calls=%async_computation.1 | async-start | bytes 1835008 | tf_op jit(solution)/shard_map/partial_exchange/all_to_all | solution.py:130
  85.0 23.3 %copy-start.17 = (bf16[1536,192]{0,1:T(8,128)(2,1)S(1)}, bf16[1536,192]{0,1:T(8,128)(2,1)}, u32[]{:S(2)}) copy-start(bf16[1536,192]{0,1:T(8,128)(2,1)} %param.24) | copy-start | bytes 1769476
  85.5 23.3 %copy-start.3 = (bf16[1536,192]{0,1:T(8,128)(2,1)S(1)}, bf16[1536,192]{0,1:T(8,128)(2,1)}, u32[]{:S(2)}) copy-start(bf16[1536,192]{0,1:T(8,128)(2,1)} %param.25) | copy-start | bytes 1769476
  110.0 6.2 %copy-start.18 = (bf16[1536,32]{0,1:T(8,128)(2,1)S(1)}, bf16[1536,32]{0,1:T(8,128)(2,1)}, u32[]{:S(2)}) copy-start(bf16[1536,32]{0,1:T(8,128)(2,1)} %param.23) | copy-start | bytes 294916
  111.7 20.6 %all-to-all-start.3 = ((bf16[128,2,1536]{2,1,0:T(2,128)(2,1)}), bf16[128,2,1536]{2,1,0:T(2,128)(2,1)S(1)}, u32[]{:S(2)}, u32[]{:S(2)}) async-start(bf16[128,2,1536]{2,1,0:T(2,128)(2,1)} %copy.145), calls=%async_computation.3 | async-start | bytes 1572864 | tf_op jit(solution)/shard_map/expert_return/all_to_all | solution.py:210

commit v10 on v8

--- a/solution.py
+++ b/solution.py
@@ -84,34 +84,38 @@
     with jax.named_scope("slot_attention"):
         key_slot = seq_place * local_pos + jnp.arange(local_pos, dtype=jnp.int32)
         back = jnp.mod(lengths[:, None] - 1 - key_slot[None, :], window)
-        row_step = jnp.arange(per_head, dtype=jnp.int32) // heads_per
+        row_ids = jnp.arange(rows_q, dtype=jnp.int32)
+        row_head = row_ids // per_head
+        row_step = (row_ids % per_head) // heads_per
         reach = jnp.minimum(lengths[:, None], window - 1 - row_step[None, :])
         valid = back[:, None, :] < reach[:, :, None]
-        mixed_heads, total_heads, hi_heads, mid_heads = [], [], [], []
+        lane_head = jnp.arange(KVH * HD, dtype=jnp.int32) // HD
+        own_half = row_head[None, :, None] == lane_head[None, None, :]
+        q_spread = jnp.where(
+            own_half, jnp.concatenate([every_query] * KVH, axis=-1), jnp.zeros((), jnp.bfloat16)
+        )
+        scores = (
+            jnp.einsum("nre,nce->nrc", q_spread, k_cache, preferred_element_type=jnp.float32)
+            * scale
+        )
+        peak = jnp.max(jnp.where(valid, scores, -1e30), axis=-1)
+        hi = peak.astype(jnp.bfloat16)
+        mid = (peak - hi.astype(jnp.float32)).astype(jnp.bfloat16)
+        shard_peak = hi.astype(jnp.float32) + mid.astype(jnp.float32)
+        weights = jnp.where(valid, jnp.exp(scores - shard_peak[..., None]), 0.0)
+        total_heads = [jnp.sum(weights, axis=-1)]
+        hi_heads, mid_heads = [hi], [mid]
+        mixed_heads = []
         for k in range(KVH):
-            q_k = every_query[:, k * per_head : (k + 1) * per_head, :]
-            keys_k = k_cache[:, :, k * HD : (k + 1) * HD]
             vals_k = v_cache[:, :, k * HD : (k + 1) * HD]
-            scores = (
-                jnp.einsum("nrd,ncd->nrc", q_k, keys_k, preferred_element_type=jnp.float32)
-                * scale
-            )
-            peak = jnp.max(jnp.where(valid, scores, -1e30), axis=-1)
-            hi = peak.astype(jnp.bfloat16)
-            mid = (peak - hi.astype(jnp.float32)).astype(jnp.bfloat16)
-            shard_peak = hi.astype(jnp.float32) + mid.astype(jnp.float32)
-            weights = jnp.where(valid, jnp.exp(scores - shard_peak[..., None]), 0.0)
-            total_heads.append(jnp.sum(weights, axis=-1))
             mixed_heads.append(
                 jnp.einsum(
                     "nrc,ncd->nrd",
-                    weights.astype(jnp.bfloat16),
+                    weights[:, k * per_head : (k + 1) * per_head].astype(jnp.bfloat16),
                     vals_k,
                     preferred_element_type=jnp.float32,
                 )
             )
-            hi_heads.append(hi)
-            mid_heads.append(mid)
         stats = jnp.stack(
             [
                 jnp.concatenate(total_heads, axis=1),

time: 119 us -> 122 us (1.025)
  local copies, waits for them, and re-layouts: 4.68 us -> 7.52 us
  matrix products: 17.2 us -> 15.3 us
    dot_general x4 -> x3, matrix products: 6.82 us -> 1.75 us  [the longest x1 0.95 us: on_device(): jnp.einsum('nre,nce->nrc', q_spread, k_cache, preferred_element_type=jnp....]
    dot_general x1, matrix products: 1.15 us -> 3.27 us  [on_device(): jnp.dot(hidden, w_down, preferred_element_type=jnp.float32)]
    reshape x1, local copies, waits for them, and re-layouts: 0.3 us -> 2.27 us  [on_device(): rows_in = arrived.reshape(devices * MOST, D)]
    reshape x1, local copies, waits for them, and re-layouts: 1.17 us -> 2.9 us  [on_device(): produced = jnp.dot(hidden, w_down, preferred_element_type=jnp.float32).as...]
    another operation x2 -> x3, other arithmetic: 0.16 us -> 1.88 us
where the time goes in v10:
time: 122 us; the launch traced here: 121 us
  waiting for transfers between devices  44 us (36%)
  blocking collectives  22.9 us (19%)
  starting transfers between devices  21.3 us (17%)
  matrix products  15.3 us (13%)
  other arithmetic  9.72 us (8%)
  local copies, waits for them, and re-layouts  7.52 us (6%)
    all_to_all x1, blocking collectives, on_device(): arrived = lax.all_to_all(sent_u, ('req', 'seq'), 0, 0, tiled=True)  22.9 us
    all_to_all x1, waiting for transfers between devices, on_device(): returned = lax.all_to_all(produced, ('req', 'seq'), 0, 0, tiled=True)  15.1 us
    all_to_all x1, waiting for transfers between devices, on_device(): every_query = lax.all_to_all(sent_q, 'seq', 0, 0, tiled=True)  14.6 us
    all_to_all x1, waiting for transfers between devices, on_device(): parts = lax.all_to_all(packed, 'seq', 0, 0, tiled=True)  14.2 us
    all_to_all x1, starting transfers between devices, on_device(): every_query = lax.all_to_all(sent_q, 'seq', 0, 0, tiled=True)  12 us
    all_to_all x1, starting transfers between devices, on_device(): parts = lax.all_to_all(packed, 'seq', 0, 0, tiled=True)  4.78 us
    all_to_all x1, starting transfers between devices, on_device(): returned = lax.all_to_all(produced, ('req', 'seq'), 0, 0, tiled=True)  4.54 us
    dot_general x1, matrix products, on_device(): proj = jnp.dot(a, w_qkv, preferred_element_type=jnp.float32)  3.76 us
  transfers between devices with their start and end apart: 3, of which 3 were waited for; matrix products, arithmetic and copies ran while one was open for 2% of the time, Pallas kernels for 0%

profile of v10, /device:TPU:1, one launch (start us, length us, event | category | flops | bytes accessed | tf_op | source)
XLA Modules:
  0.0 121.2 jit_solution(14524328630781713611)
XLA Ops:
  0.0 1.4 %broadcast_add_fusion.1 = (s32[64]{0:T(128)S(1)}, s32[]{:T(128)}) fusion(s32[64]{0:T(128)} %param.15, s32[]{:T(128)S(6)} %axis_index.22), kind=kLoop, calls=%fused_computation.144 | loop fusion | flops 255 | bytes 520 | tf_op jit(solution)/shard_map/slot_attention/sub | solution.py:86
  1.5 0.6 add_convert_fusion.2
  2.1 0.7 convert_element_type.187
  2.8 0.8 fusion.37
  3.6 3.8 %fusion.40 = f32[4,2048]{1,0:T(4,128)S(1)} fusion(bf16[1536,2048]{1,0:T(8,128)(2,1)} %param.19, bf16[4,1,1536]{2,0,1:T(4,128)(2,1)} %param.14, f32[1536]{0:T(1024)S(1)} %convert_element_type.187, f32[4]{0:T(128)S(1)} %add_rsqrt_fusion.1), kind=kOutput, calls=%fused_computation.81 | convolution fusion | flops 25190400 | bytes 6342672 | tf_op jit(solution)/shard_map/qkv_projection/dot_general | solution.py:68
  7.8 1.0 broadcast_in_dim.66
  8.8 12.0 %all-to-all-start = ((bf16[64,48,128]{2,1,0:T(8,128)(2,1)}), bf16[64,48,128]{2,1,0:T(8,128)(2,1)S(1)}, u32[]{:S(2)}, u32[]{:S(2)}) async-start(bf16[64,48,128]{2,1,0:T(8,128)(2,1)} %broadcast_in_dim.66), calls=%async_computation | async-start | bytes 1572864 | tf_op jit(solution)/shard_map/query_exchange/all_to_all | solution.py:82
  21.1 14.6 %all-to-all-done = bf16[64,48,128]{2,1,0:T(8,128)(2,1)S(1)} async-done(((bf16[64,48,128]{2,1,0:T(8,128)(2,1)}), bf16[64,48,128]{2,1,0:T(8,128)(2,1)S(1)}, u32[]{:S(2)}, u32[]{:S(2)}) %all-to-all-start) | async-done | bytes 786464 | tf_op jit(solution)/shard_map/query_exchange/all_to_all | solution.py:82
  35.7 1.0 fusion.5
  36.7 1.7 %fusion.12 = (bf16[64,48,64]{2,1,0:T(8,128)(2,1)S(1)}, bf16[64,48]{1,0:T(8,128)(2,1)S(1)}) fusion(f32[64,48,64]{2,1,0:T(8,128)S(1)} %get-tuple-element.18, f32[64,48]{1,0:T(8,128)S(1)} %convert_add_fusion, s32[64,48]{1,0:T(8,128)S(1)} %broadcast_minimum_fusion, s32[64,64]{1,0:T(8,128)S(1)} %add_select_fusion), kind=kLoop, calls=%fused_computation.23 | loop fusion | flops 979968 | bytes 1226752 | tf_op jit(solution)/shard_map/convert.15
  39.7 1.0 pad_maximum_fusion
  40.7 4.8 %all-to-all-start.1 = ((bf16[64,56,128]{2,1,0:T(8,128)(2,1)}), bf16[64,56,128]{2,1,0:T(8,128)(2,1)S(1)}, u32[]{:S(2)}, u32[]{:S(2)}) async-start(bf16[64,56,128]{2,1,0:T(8,128)(2,1)} %pad_maximum_fusion), calls=%async_computation.1 | async-start | bytes 1835008 | tf_op jit(solution)/shard_map/partial_exchange/all_to_all | solution.py:131
  46.5 14.2 %all-to-all-done.1 = bf16[64,56,128]{2,1,0:T(8,128)(2,1)S(1)} async-done(((bf16[64,56,128]{2,1,0:T(8,128)(2,1)}), bf16[64,56,128]{2,1,0:T(8,128)(2,1)S(1)}, u32[]{:S(2)}, u32[]{:S(2)}) %all-to-all-start.1) | async-done | bytes 917536 | tf_op jit(solution)/shard_map/partial_exchange/all_to_all | solution.py:131
  61.1 0.5 multiply_reduce_fusion
  62.0 3.2 %multiply_reduce_fusion.1 = (f32[4]{0:T(128)S(1)}, f32[4,1536]{1,0:T(4,128)S(1)}) fusion(bf16[4,1536]{1,0:T(4,128)(2,1)S(1)} %convert_element_type.204, bf16[1536,1536]{1,0:T(8,128)(2,1)} %param.21, bf16[4,1,1536]{2,0,1:T(4,128)(2,1)S(1)} %copy-done.2), kind=kOutput, calls=%fused_computation.75 | convolution fusion | flops 18911228 | bytes 4767760 | tf_op jit(solution)/shard_map/attention_output/dot_general | solution.py:173
  66.1 22.9 %all_to_all.20 = bf16[128,2,1536]{2,1,0:T(2,128)(2,1)} all-to-all(bf16[128,2,1536]{2,1,0:T(2,128)(2,1)S(1)} %bitcast.70), channel_id=1, replica_groups=mesh['req'=2,'seq'=64] {'req','seq'}, dimensions={0} | all-to-all | bytes 1572864 | tf_op jit(solution)/shard_map/token_dispatch/all_to_all | solution.py:199
  89.0 2.3 %reshape.436 = bf16[256,1536]{1,0:T(8,128)(2,1)S(1)} reshape(bf16[128,2,1536]{2,1,0:T(2,128)(2,1)} %all_to_all.20) | data formatting | bytes 1572864 | tf_op jit(solution)/shard_map/expert_quarter/reshape | solution.py:202
  91.3 1.5 %convolution_maximum_fusion = f32[256,192]{0,1:T(8,128)S(1)} fusion(bf16[256,1536]{1,0:T(8,128)(2,1)S(1)} %reshape.436, bf16[1536,192]{0,1:T(8,128)(2,1)} %param.24), kind=kOutput, calls=%fused_computation.25 | convolution fusion | flops 151044096 | bytes 1572864 | tf_op jit(solution)/shard_map/expert_quarter/dot_general | solution.py:204
  92.8 3.3 %convolution_convert_fusion = bf16[256,1536]{1,0:T(8,128)(2,1)} fusion(bf16[192,1536]{1,0:T(8,128)(2,1)} %param.26, f32[256,192]{0,1:T(8,128)S(1)} %convolution_maximum_fusion, bf16[256,1536]{1,0:T(8,128)(2,1)S(1)} %reshape.436, bf16[1536,192]{0,1:T(8,128)(2,1)} %param.25), kind=kOutput, calls=%fused_computation | convolution fusion | flops 302481408 | bytes 2949120 | tf_op jit(solution)/shard_map/expert_quarter/dot_general | solution.py:208
  96.0 2.9 %reshape.437 = bf16[128,2,1536]{2,1,0:T(2,128)(2,1)} reshape(bf16[256,1536]{1,0:T(8,128)(2,1)} %convolution_convert_fusion) | data formatting | bytes 1572864 | tf_op jit(solution)/shard_map/expert_quarter/reshape | solution.py:210
  98.9 4.5 %all-to-all-start.3 = ((bf16[128,2,1536]{2,1,0:T(2,128)(2,1)}), bf16[128,2,1536]{2,1,0:T(2,128)(2,1)S(1)}, u32[]{:S(2)}, u32[]{:S(2)}) async-start(bf16[128,2,1536]{2,1,0:T(2,128)(2,1)} %reshape.437), calls=%async_computation.3 | async-start | bytes 1572864 | tf_op jit(solution)/shard_map/expert_return/all_to_all | solution.py:214
  104.3 15.1 %all-to-all-done.3 = bf16[128,2,1536]{2,1,0:T(2,128)(2,1)S(1)} async-done(((bf16[128,2,1536]{2,1,0:T(2,128)(2,1)}), bf16[128,2,1536]{2,1,0:T(2,128)(2,1)S(1)}, u32[]{:S(2)}, u32[]{:S(2)}) %all-to-all-start.3) | async-done | bytes 786464 | tf_op jit(solution)/shard_map/expert_return/all_to_all | solution.py:214
  119.5 0.7 convert_reduce_fusion
  120.2 1.0 fusion.4
  (81 shorter events, 5.3 us)
Async XLA Ops:
  0.0 35.7 %copy-start = (bf16[64,64,256]{2,1,0:T(8,128)(2,1)S(1)}, bf16[64,64,256]{2,1,0:T(8,128)(2,1)}, u32[]{:S(2)}) copy-start(bf16[64,64,256]{2,1,0:T(8,128)(2,1)} %param.16) | copy-start | bytes 6291460
  7.4 13.5 %copy-start.5 = (s32[64]{0:T(128)S(1)}, s32[64]{0:T(128)}, u32[]{:S(2)}) copy-start(s32[64]{0:T(128)} %param.15) | copy-start | bytes 772
  8.8 26.9 %all-to-all-start = ((bf16[64,48,128]{2,1,0:T(8,128)(2,1)}), bf16[64,48,128]{2,1,0:T(8,128)(2,1)S(1)}, u32[]{:S(2)}, u32[]{:S(2)}) async-start(bf16[64,48,128]{2,1,0:T(8,128)(2,1)} %broadcast_in_dim.66), calls=%async_computation | async-start | bytes 1572864 | tf_op jit(solution)/shard_map/query_exchange/all_to_all | solution.py:82
  36.6 1.8 %copy-start.1 = (bf16[64,64,256]{2,1,0:T(8,128)(2,1)S(1)}, bf16[64,64,256]{2,1,0:T(8,128)(2,1)}, u32[]{:S(2)}) copy-start(bf16[64,64,256]{2,1,0:T(8,128)(2,1)} %param.17) | copy-start | bytes 6291460
  39.7 5.9 %copy-start.7 = (f32[12]{0:T(128)S(1)}, f32[12]{0:T(128)}, u32[]{:S(2)}) copy-start(f32[12]{0:T(128)} %param.20) | copy-start | bytes 148
  39.7 6.4 %copy-start.4 = (bf16[1536]{0:T(1024)(128)(2,1)S(1)}, bf16[1536]{0:T(1024)(128)(2,1)}, u32[]{:S(2)}) copy-start(bf16[1536]{0:T(1024)(128)(2,1)} %param.22) | copy-start | bytes 9220
  39.7 6.5 %copy-start.3 = (s32[128,4,4]{0,2,1:T(4,128)S(1)}, s32[128,4,4]{0,2,1:T(4,128)}, u32[]{:S(2)}) copy-start(s32[128,4,4]{0,2,1:T(4,128)} %param.27) | copy-start | bytes 24580
  40.7 21.2 %copy-start.2 = (bf16[4,1,1536]{2,0,1:T(4,128)(2,1)S(1)}, bf16[4,1,1536]{2,0,1:T(4,128)(2,1)}, u32[]{:S(2)}) copy-start(bf16[4,1,1536]{2,0,1:T(4,128)(2,1)} %param.14) | copy-start | bytes 36868
  40.7 19.9 %all-to-all-start.1 = ((bf16[64,56,128]{2,1,0:T(8,128)(2,1)}), bf16[64,56,128]{2,1,0:T(8,128)(2,1)S(1)}, u32[]{:S(2)}, u32[]{:S(2)}) async-start(bf16[64,56,128]{2,1,0:T(8,128)(2,1)} %pad_maximum_fusion), calls=%async_computation.1 | async-start | bytes 1835008 | tf_op jit(solution)/shard_map/partial_exchange/all_to_all | solution.py:131
  96.0 7.4 %copy-start.6 = (bf16[1536,32]{0,1:T(8,128)(2,1)S(1)}, bf16[1536,32]{0,1:T(8,128)(2,1)}, u32[]{:S(2)}) copy-start(bf16[1536,32]{0,1:T(8,128)(2,1)} %param.23) | copy-start | bytes 294916
  98.9 20.6 %all-to-all-start.3 = ((bf16[128,2,1536]{2,1,0:T(2,128)(2,1)}), bf16[128,2,1536]{2,1,0:T(2,128)(2,1)S(1)}, u32[]{:S(2)}, u32[]{:S(2)}) async-start(bf16[128,2,1536]{2,1,0:T(2,128)(2,1)} %reshape.437), calls=%async_computation.3 | async-start | bytes 1572864 | tf_op jit(solution)/shard_map/expert_return/all_to_all | solution.py:214

commit v11 on v10

--- a/solution.py
+++ b/solution.py
@@ -1,6 +1,8 @@
 import jax
 import jax.numpy as jnp
 from jax import lax
+from jax.experimental import pallas as pl
+from jax.experimental.pallas import tpu as pltpu
 from jax.sharding import PartitionSpec as P
 
 D = 1536
@@ -32,6 +34,32 @@
     return jnp.concatenate(
         [first * cosine - second * sine, second * cosine + first * sine], axis=-1
     )
+
+
+def expert_kernel(rows_ref, gate_ref, up_ref, down_ref, out_ref):
+    rows = rows_ref[...]
+    gate = jnp.dot(rows, gate_ref[...], preferred_element_type=jnp.float32)
+    up = jnp.dot(rows, up_ref[...], preferred_element_type=jnp.float32)
+    hidden = (jnp.maximum(gate, 0.0) * up).astype(jnp.bfloat16)
+    out_ref[...] = jnp.dot(hidden, down_ref[...], preferred_element_type=jnp.float32).astype(
+        out_ref.dtype
+    )
+
+
+def expert_quarter(rows, w_gate, w_up, w_down):
+    count, width = rows.shape
+    units = w_gate.shape[1]
+    return pl.pallas_call(
+        expert_kernel,
+        out_shape=jax.ShapeDtypeStruct((count, width), jnp.bfloat16),
+        in_specs=[pl.BlockSpec(memory_space=pltpu.VMEM)] * 4,
+        out_specs=pl.BlockSpec(memory_space=pltpu.VMEM),
+        cost_estimate=pl.CostEstimate(
+            flops=6 * count * width * units,
+            transcendentals=0,
+            bytes_accessed=2 * (3 * width * units + 2 * count * width),
+        ),
+    )(rows, w_gate, w_up, w_down)
 
 
 def on_device(
@@ -200,15 +228,7 @@
 
     with jax.named_scope("expert_quarter"):
         rows_in = arrived.reshape(devices * MOST, D)
-        hidden = (
-            jax.nn.relu(jnp.dot(rows_in, w_gate, preferred_element_type=jnp.float32))
-            * jnp.dot(rows_in, w_up, preferred_element_type=jnp.float32)
-        ).astype(jnp.bfloat16)
-        produced = (
-            jnp.dot(hidden, w_down, preferred_element_type=jnp.float32)
-            .astype(jnp.bfloat16)
-            .reshape(devices, MOST, D)
-        )
+        produced = expert_quarter(rows_in, w_gate, w_up, w_down).reshape(devices, MOST, D)
 
     with jax.named_scope("expert_return"):
         returned = lax.all_to_all(produced, ("req", "seq"), 0, 0, tiled=True)

time: 122 us -> 120 us (0.984)
  blocking collectives: 22.9 us -> 0 us
  waiting for transfers between devices: 44 us -> 56.7 us
  starting transfers between devices: 21.3 us -> 28 us
  matrix products: 15.3 us -> 10.6 us
  Pallas kernels: 0 us -> 3.53 us
  local copies, waits for them, and re-layouts: 7.52 us -> 10.7 us
    all_to_all x1 -> x0, blocking collectives: 22.9 us -> none  [on_device(): arrived = lax.all_to_all(sent_u, ('req', 'seq'), 0, 0, tiled=True)]
    all_to_all x0 -> x1, waiting for transfers between devices: none -> 12.7 us  [on_device(): arrived = lax.all_to_all(sent_u, ('req', 'seq'), 0, 0, tiled=True)]
    all_to_all x0 -> x1, starting transfers between devices: none -> 6.75 us  [on_device(): arrived = lax.all_to_all(sent_u, ('req', 'seq'), 0, 0, tiled=True)]
    dot_general x2 -> x0, matrix products: 4.74 us -> none  [the longest x1 3.27 us: on_device(): jnp.dot(hidden, w_down, preferred_element_type=jnp.float32)]
    pallas_call x0 -> x1, Pallas kernels: none -> 3.53 us  [expert_quarter(): pl.pallas_call(expert_kernel, out_shape=jax.ShapeDtypeStruct((count, widt...]
    unnamed x16 -> x20, local copies, waits for them, and re-layouts: 0.04 us -> 3.44 us
  transfers between devices with their start and end apart: 3 -> 4, of which waited for: 3 -> 4; matrix products, arithmetic and copies ran while one was open for 2% -> 4% of each run, Pallas kernels for 0% -> 0%
where the time goes in v11:
time: 120 us
  waiting for transfers between devices  56.7 us (47%)
  starting transfers between devices  28 us (23%)
  local copies, waits for them, and re-layouts  10.7 us (9%)
  matrix products  10.6 us (9%)
  other arithmetic  9.72 us (8%)
  Pallas kernels  3.53 us (3%)
    all_to_all x1, waiting for transfers between devices, on_device(): returned = lax.all_to_all(produced, ('req', 'seq'), 0, 0, tiled=True)  15.1 us
    all_to_all x1, waiting for transfers between devices, on_device(): every_query = lax.all_to_all(sent_q, 'seq', 0, 0, tiled=True)  14.6 us
    all_to_all x1, waiting for transfers between devices, on_device(): parts = lax.all_to_all(packed, 'seq', 0, 0, tiled=True)  14.2 us
    all_to_all x1, waiting for transfers between devices, on_device(): arrived = lax.all_to_all(sent_u, ('req', 'seq'), 0, 0, tiled=True)  12.7 us
    all_to_all x1, starting transfers between devices, on_device(): every_query = lax.all_to_all(sent_q, 'seq', 0, 0, tiled=True)  12 us
    all_to_all x1, starting transfers between devices, on_device(): arrived = lax.all_to_all(sent_u, ('req', 'seq'), 0, 0, tiled=True)  6.75 us
    all_to_all x1, starting transfers between devices, on_device(): parts = lax.all_to_all(packed, 'seq', 0, 0, tiled=True)  4.78 us
    all_to_all x1, starting transfers between devices, on_device(): returned = lax.all_to_all(produced, ('req', 'seq'), 0, 0, tiled=True)  4.54 us
  transfers between devices with their start and end apart: 4, of which 4 were waited for; matrix products, arithmetic and copies ran while one was open for 4% of the time, Pallas kernels for 0%

profile of v11, /device:TPU:1, one launch (start us, length us, event | category | flops | bytes accessed | tf_op | source)
XLA Modules:
  0.0 119.7 jit_solution(13534749564808356689)
XLA Ops:
  0.0 1.4 %broadcast_add_fusion.1 = (s32[64]{0:T(128)S(1)}, s32[]{:T(128)}) fusion(s32[64]{0:T(128)} %param.15, s32[]{:T(128)S(6)} %axis_index.22), kind=kLoop, calls=%fused_computation.140 | loop fusion | flops 255 | bytes 520 | tf_op jit(solution)/shard_map/slot_attention/sub | solution.py:114
  2.8 0.8 fusion.36
  3.6 3.8 %fusion.39 = f32[4,2048]{1,0:T(4,128)S(1)} fusion(bf16[1536,2048]{1,0:T(8,128)(2,1)} %param.19, bf16[4,1,1536]{2,0,1:T(4,128)(2,1)} %param.14, f32[1536]{0:T(1024)S(1)} %convert_element_type.181, f32[4]{0:T(128)S(1)} %add_rsqrt_fusion.1), kind=kOutput, calls=%fused_computation.77 | convolution fusion | flops 25190400 | bytes 6342672 | tf_op jit(solution)/shard_map/qkv_projection/dot_general | solution.py:96
  7.8 1.0 broadcast_in_dim.66
  8.8 12.0 %all-to-all-start = ((bf16[64,48,128]{2,1,0:T(8,128)(2,1)}), bf16[64,48,128]{2,1,0:T(8,128)(2,1)S(1)}, u32[]{:S(2)}, u32[]{:S(2)}) async-start(bf16[64,48,128]{2,1,0:T(8,128)(2,1)} %broadcast_in_dim.66), calls=%async_computation | async-start | bytes 1572864 | tf_op jit(solution)/shard_map/query_exchange/all_to_all | solution.py:110
  21.1 14.6 %all-to-all-done = bf16[64,48,128]{2,1,0:T(8,128)(2,1)S(1)} async-done(((bf16[64,48,128]{2,1,0:T(8,128)(2,1)}), bf16[64,48,128]{2,1,0:T(8,128)(2,1)S(1)}, u32[]{:S(2)}, u32[]{:S(2)}) %all-to-all-start) | async-done | bytes 786464 | tf_op jit(solution)/shard_map/query_exchange/all_to_all | solution.py:110
  35.7 1.0 fusion.5
  36.7 1.7 %fusion.12 = (bf16[64,48,64]{2,1,0:T(8,128)(2,1)S(1)}, bf16[64,48]{1,0:T(8,128)(2,1)S(1)}) fusion(f32[64,48,64]{2,1,0:T(8,128)S(1)} %get-tuple-element.18, f32[64,48]{1,0:T(8,128)S(1)} %convert_add_fusion, s32[64,48]{1,0:T(8,128)S(1)} %broadcast_minimum_fusion, s32[64,64]{1,0:T(8,128)S(1)} %add_select_fusion), kind=kLoop, calls=%fused_computation.22 | loop fusion | flops 979968 | bytes 1226752 | tf_op jit(solution)/shard_map/convert.15
  39.7 1.0 pad_maximum_fusion
  40.7 4.8 %all-to-all-start.1 = ((bf16[64,56,128]{2,1,0:T(8,128)(2,1)}), bf16[64,56,128]{2,1,0:T(8,128)(2,1)S(1)}, u32[]{:S(2)}, u32[]{:S(2)}) async-start(bf16[64,56,128]{2,1,0:T(8,128)(2,1)} %pad_maximum_fusion), calls=%async_computation.1 | async-start | bytes 1835008 | tf_op jit(solution)/shard_map/partial_exchange/all_to_all | solution.py:159
  46.5 14.2 %all-to-all-done.1 = bf16[64,56,128]{2,1,0:T(8,128)(2,1)S(1)} async-done(((bf16[64,56,128]{2,1,0:T(8,128)(2,1)}), bf16[64,56,128]{2,1,0:T(8,128)(2,1)S(1)}, u32[]{:S(2)}, u32[]{:S(2)}) %all-to-all-start.1) | async-done | bytes 917536 | tf_op jit(solution)/shard_map/partial_exchange/all_to_all | solution.py:159
  62.0 3.2 %multiply_reduce_fusion.1 = (f32[4]{0:T(128)S(1)}, f32[4,1536]{1,0:T(4,128)S(1)}) fusion(bf16[4,1536]{1,0:T(4,128)(2,1)S(1)} %convert_element_type.198, bf16[1536,1536]{1,0:T(8,128)(2,1)} %param.21, bf16[4,1,1536]{2,0,1:T(4,128)(2,1)S(1)} %copy-done.3), kind=kOutput, calls=%fused_computation.71 | convolution fusion | flops 18911228 | bytes 4767760 | tf_op jit(solution)/shard_map/attention_output/dot_general | solution.py:201
  65.7 1.3 %broadcast_in_dim.120 = bf16[32,4,2,1536]{3,2,1,0:T(2,128)(2,1)} broadcast(bf16[32,2,1536]{2,1,0:T(2,128)(2,1)S(1)} %copy.71), dimensions={0,2,3} | broadcast | bytes 983040 | tf_op jit(solution)/shard_map/route/broadcast_in_dim | solution.py:222
  66.9 6.8 %all-to-all-start.2 = ((bf16[128,2,1536]{2,1,0:T(2,128)(2,1)}), bf16[128,2,1536]{2,1,0:T(2,128)(2,1)S(1)}, u32[]{:S(2)}, u32[]{:S(2)}) async-start(bf16[128,2,1536]{2,1,0:T(2,128)(2,1)} %bitcast.65), calls=%async_computation.2 | async-start | bytes 1572864 | tf_op jit(solution)/shard_map/token_dispatch/all_to_all | solution.py:227
  73.7 1.2 copy.72.gate_ref
  74.9 2.2 %copy.73.up_ref = bf16[1536,192]{1,0:T(8,128)(2,1)} copy(bf16[1536,192]{0,1:T(8,128)(2,1)} %param.25) | data formatting | bytes 1179648 | tf_op args[11]
  77.1 12.7 %all-to-all-done.2 = bf16[128,2,1536]{2,1,0:T(2,128)(2,1)S(1)} async-done(((bf16[128,2,1536]{2,1,0:T(2,128)(2,1)}), bf16[128,2,1536]{2,1,0:T(2,128)(2,1)S(1)}, u32[]{:S(2)}, u32[]{:S(2)}) %all-to-all-start.2) | async-done | bytes 786464 | tf_op jit(solution)/shard_map/token_dispatch/all_to_all | solution.py:227
  89.9 1.2 reshape.436.rows_ref
  91.0 3.5 %expert_quarter.1 = bf16[256,1536]{1,0:T(8,128)(2,1)} custom-call(bf16[256,1536]{1,0:T(8,128)(2,1)} %reshape.436.rows_ref, bf16[1536,192]{1,0:T(8,128)(2,1)} %copy.72.gate_ref, bf16[1536,192]{1,0:T(8,128)(2,1)} %copy.73.up_ref, bf16[192,1536]{1,0:T(8,128)(2,1)} %down_ref.1), custom_call_target="tpu_custom_call" | custom-call | flops 452984832 | bytes 3342336 | tf_op jit(solution)/shard_map/expert_quarter/pallas_call | solution.py:52
  94.6 2.9 %reshape.437 = bf16[128,2,1536]{2,1,0:T(2,128)(2,1)} reshape(bf16[256,1536]{1,0:T(8,128)(2,1)} %expert_quarter.1) | data formatting | bytes 1572864 | tf_op jit(solution)/shard_map/expert_quarter/reshape | solution.py:231
  97.5 4.5 %all-to-all-start.3 = ((bf16[128,2,1536]{2,1,0:T(2,128)(2,1)}), bf16[128,2,1536]{2,1,0:T(2,128)(2,1)S(1)}, u32[]{:S(2)}, u32[]{:S(2)}) async-start(bf16[128,2,1536]{2,1,0:T(2,128)(2,1)} %reshape.437), calls=%async_computation.3 | async-start | bytes 1572864 | tf_op jit(solution)/shard_map/expert_return/all_to_all | solution.py:234
  102.9 15.1 %all-to-all-done.3 = bf16[128,2,1536]{2,1,0:T(2,128)(2,1)S(1)} async-done(((bf16[128,2,1536]{2,1,0:T(2,128)(2,1)}), bf16[128,2,1536]{2,1,0:T(2,128)(2,1)S(1)}, u32[]{:S(2)}, u32[]{:S(2)}) %all-to-all-start.3) | async-done | bytes 786464 | tf_op jit(solution)/shard_map/expert_return/all_to_all | solution.py:234
  118.0 0.7 convert_reduce_fusion
  118.7 1.0 fusion.4
  (85 shorter events, 6.7 us)
Async XLA Ops:
  0.0 35.7 %copy-start = (bf16[64,64,256]{2,1,0:T(8,128)(2,1)S(1)}, bf16[64,64,256]{2,1,0:T(8,128)(2,1)}, u32[]{:S(2)}) copy-start(bf16[64,64,256]{2,1,0:T(8,128)(2,1)} %param.16) | copy-start | bytes 6291460
  7.4 13.5 %copy-start.6 = (s32[64]{0:T(128)S(1)}, s32[64]{0:T(128)}, u32[]{:S(2)}) copy-start(s32[64]{0:T(128)} %param.15) | copy-start | bytes 772
  8.8 26.9 %all-to-all-start = ((bf16[64,48,128]{2,1,0:T(8,128)(2,1)}), bf16[64,48,128]{2,1,0:T(8,128)(2,1)S(1)}, u32[]{:S(2)}, u32[]{:S(2)}) async-start(bf16[64,48,128]{2,1,0:T(8,128)(2,1)} %broadcast_in_dim.66), calls=%async_computation | async-start | bytes 1572864 | tf_op jit(solution)/shard_map/query_exchange/all_to_all | solution.py:110
  36.6 1.8 %copy-start.1 = (bf16[64,64,256]{2,1,0:T(8,128)(2,1)S(1)}, bf16[64,64,256]{2,1,0:T(8,128)(2,1)}, u32[]{:S(2)}) copy-start(bf16[64,64,256]{2,1,0:T(8,128)(2,1)} %param.17) | copy-start | bytes 6291460
  39.7 5.9 %copy-start.8 = (f32[12]{0:T(128)S(1)}, f32[12]{0:T(128)}, u32[]{:S(2)}) copy-start(f32[12]{0:T(128)} %param.20) | copy-start | bytes 148
  39.7 6.4 %copy-start.5 = (bf16[1536]{0:T(1024)(128)(2,1)S(1)}, bf16[1536]{0:T(1024)(128)(2,1)}, u32[]{:S(2)}) copy-start(bf16[1536]{0:T(1024)(128)(2,1)} %param.22) | copy-start | bytes 9220
  39.7 6.5 %copy-start.4 = (s32[128,4,4]{0,2,1:T(4,128)S(1)}, s32[128,4,4]{0,2,1:T(4,128)}, u32[]{:S(2)}) copy-start(s32[128,4,4]{0,2,1:T(4,128)} %param.27) | copy-start | bytes 24580
  40.7 21.2 %copy-start.3 = (bf16[4,1,1536]{2,0,1:T(4,128)(2,1)S(1)}, bf16[4,1,1536]{2,0,1:T(4,128)(2,1)}, u32[]{:S(2)}) copy-start(bf16[4,1,1536]{2,0,1:T(4,128)(2,1)} %param.14) | copy-start | bytes 36868
  40.7 19.9 %all-to-all-start.1 = ((bf16[64,56,128]{2,1,0:T(8,128)(2,1)}), bf16[64,56,128]{2,1,0:T(8,128)(2,1)S(1)}, u32[]{:S(2)}, u32[]{:S(2)}) async-start(bf16[64,56,128]{2,1,0:T(8,128)(2,1)} %pad_maximum_fusion), calls=%async_computation.1 | async-start | bytes 1835008 | tf_op jit(solution)/shard_map/partial_exchange/all_to_all | solution.py:159
  65.2 8.6 %copy-start.2 = (bf16[1536,192]{0,1:T(8,128)(2,1)S(1)}, bf16[1536,192]{0,1:T(8,128)(2,1)}, u32[]{:S(2)}) copy-start(bf16[1536,192]{0,1:T(8,128)(2,1)} %param.24) | copy-start | bytes 1769476
  66.9 22.9 %all-to-all-start.2 = ((bf16[128,2,1536]{2,1,0:T(2,128)(2,1)}), bf16[128,2,1536]{2,1,0:T(2,128)(2,1)S(1)}, u32[]{:S(2)}, u32[]{:S(2)}) async-start(bf16[128,2,1536]{2,1,0:T(2,128)(2,1)} %bitcast.65), calls=%async_computation.2 | async-start | bytes 1572864 | tf_op jit(solution)/shard_map/token_dispatch/all_to_all | solution.py:227
  94.6 7.4 %copy-start.7 = (bf16[1536,32]{0,1:T(8,128)(2,1)S(1)}, bf16[1536,32]{0,1:T(8,128)(2,1)}, u32[]{:S(2)}) copy-start(bf16[1536,32]{0,1:T(8,128)(2,1)} %param.23) | copy-start | bytes 294916
  97.5 20.6 %all-to-all-start.3 = ((bf16[128,2,1536]{2,1,0:T(2,128)(2,1)}), bf16[128,2,1536]{2,1,0:T(2,128)(2,1)S(1)}, u32[]{:S(2)}, u32[]{:S(2)}) async-start(bf16[128,2,1536]{2,1,0:T(2,128)(2,1)} %reshape.437), calls=%async_computation.3 | async-start | bytes 1572864 | tf_op jit(solution)/shard_map/expert_return/all_to_all | solution.py:234

commit v12 on v10

--- a/solution.py
+++ b/solution.py
@@ -199,16 +199,13 @@
         arrived = lax.all_to_all(sent_u, ("req", "seq"), 0, 0, tiled=True)
 
     with jax.named_scope("expert_quarter"):
-        rows_in = arrived.reshape(devices * MOST, D)
         hidden = (
-            jax.nn.relu(jnp.dot(rows_in, w_gate, preferred_element_type=jnp.float32))
-            * jnp.dot(rows_in, w_up, preferred_element_type=jnp.float32)
-        ).astype(jnp.bfloat16)
-        produced = (
-            jnp.dot(hidden, w_down, preferred_element_type=jnp.float32)
-            .astype(jnp.bfloat16)
-            .reshape(devices, MOST, D)
-        )
+            jax.nn.relu(jnp.einsum("sjm,mf->sjf", arrived, w_gate, preferred_element_type=jnp.float32))
+            * jnp.einsum("sjm,mf->sjf", arrived, w_up, preferred_element_type=jnp.float32)
+        ).astype(jnp.bfloat16)
+        produced = jnp.einsum(
+            "sjf,fm->sjm", hidden, w_down, preferred_element_type=jnp.float32
+        ).astype(jnp.bfloat16)
 
     with jax.named_scope("expert_return"):
         returned = lax.all_to_all(produced, ("req", "seq"), 0, 0, tiled=True)

time: 122 us -> 118 us (0.967)
  local copies, waits for them, and re-layouts: 7.52 us -> 5.25 us
    reshape x2 -> x0, local copies, waits for them, and re-layouts: 5.16 us -> none  [the longest x1 2.9 us: on_device(): produced = jnp.dot(hidden, w_down, preferred_element_type=jnp.float32).as...]
    convert_element_type x0 -> x1, local copies, waits for them, and re-layouts: none -> 2.88 us  [on_device(): produced = jnp.einsum('sjf,fm->sjm', hidden, w_down, preferred_element_ty...]
where the time goes in v12:
time: 118 us
  waiting for transfers between devices  44 us (37%)
  blocking collectives  22.4 us (19%)
  starting transfers between devices  21.3 us (18%)
  matrix products  14.8 us (13%)
  other arithmetic  9.72 us (8%)
  local copies, waits for them, and re-layouts  5.25 us (4%)
    all_to_all x1, blocking collectives, on_device(): arrived = lax.all_to_all(sent_u, ('req', 'seq'), 0, 0, tiled=True)  22.4 us
    all_to_all x1, waiting for transfers between devices, on_device(): returned = lax.all_to_all(produced, ('req', 'seq'), 0, 0, tiled=True)  15.1 us
    all_to_all x1, waiting for transfers between devices, on_device(): every_query = lax.all_to_all(sent_q, 'seq', 0, 0, tiled=True)  14.6 us
    all_to_all x1, waiting for transfers between devices, on_device(): parts = lax.all_to_all(packed, 'seq', 0, 0, tiled=True)  14.2 us
    all_to_all x1, starting transfers between devices, on_device(): every_query = lax.all_to_all(sent_q, 'seq', 0, 0, tiled=True)  12 us
    all_to_all x1, starting transfers between devices, on_device(): parts = lax.all_to_all(packed, 'seq', 0, 0, tiled=True)  4.78 us
    all_to_all x1, starting transfers between devices, on_device(): returned = lax.all_to_all(produced, ('req', 'seq'), 0, 0, tiled=True)  4.54 us
    dot_general x1, matrix products, on_device(): proj = jnp.dot(a, w_qkv, preferred_element_type=jnp.float32)  3.76 us
  transfers between devices with their start and end apart: 3, of which 3 were waited for; matrix products, arithmetic and copies ran while one was open for 2% of the time, Pallas kernels for 0%

profile of v12, /device:TPU:1, one launch (start us, length us, event | category | flops | bytes accessed | tf_op | source)
XLA Modules:
  0.0 117.9 jit_solution(8728088467761545708)
XLA Ops:
  0.0 1.4 %broadcast_add_fusion.1 = (s32[64]{0:T(128)S(1)}, s32[]{:T(128)}) fusion(s32[64]{0:T(128)} %param.15, s32[]{:T(128)S(6)} %axis_index.22), kind=kLoop, calls=%fused_computation.149 | loop fusion | flops 255 | bytes 520 | tf_op jit(solution)/shard_map/slot_attention/sub | solution.py:86
  1.5 0.6 add_convert_fusion.2
  2.1 0.7 convert_element_type.187
  2.8 0.8 fusion.44
  3.6 3.8 %fusion.47 = f32[4,2048]{1,0:T(4,128)S(1)} fusion(bf16[1536,2048]{1,0:T(8,128)(2,1)} %param.19, bf16[4,1,1536]{2,0,1:T(4,128)(2,1)} %param.14, f32[1536]{0:T(1024)S(1)} %convert_element_type.187, f32[4]{0:T(128)S(1)} %add_rsqrt_fusion.1), kind=kOutput, calls=%fused_computation.86 | convolution fusion | flops 25190400 | bytes 6342672 | tf_op jit(solution)/shard_map/qkv_projection/dot_general | solution.py:68
  7.8 1.0 broadcast_in_dim.66
  8.8 12.0 %all-to-all-start = ((bf16[64,48,128]{2,1,0:T(8,128)(2,1)}), bf16[64,48,128]{2,1,0:T(8,128)(2,1)S(1)}, u32[]{:S(2)}, u32[]{:S(2)}) async-start(bf16[64,48,128]{2,1,0:T(8,128)(2,1)} %broadcast_in_dim.66), calls=%async_computation | async-start | bytes 1572864 | tf_op jit(solution)/shard_map/query_exchange/all_to_all | solution.py:82
  21.1 14.6 %all-to-all-done = bf16[64,48,128]{2,1,0:T(8,128)(2,1)S(1)} async-done(((bf16[64,48,128]{2,1,0:T(8,128)(2,1)}), bf16[64,48,128]{2,1,0:T(8,128)(2,1)S(1)}, u32[]{:S(2)}, u32[]{:S(2)}) %all-to-all-start) | async-done | bytes 786464 | tf_op jit(solution)/shard_map/query_exchange/all_to_all | solution.py:82
  35.7 1.0 fusion.5
  36.7 1.7 %fusion.12 = (bf16[64,48,64]{2,1,0:T(8,128)(2,1)S(1)}, bf16[64,48]{1,0:T(8,128)(2,1)S(1)}) fusion(f32[64,48,64]{2,1,0:T(8,128)S(1)} %get-tuple-element.18, f32[64,48]{1,0:T(8,128)S(1)} %convert_add_fusion, s32[64,48]{1,0:T(8,128)S(1)} %broadcast_minimum_fusion, s32[64,64]{1,0:T(8,128)S(1)} %add_select_fusion), kind=kLoop, calls=%fused_computation.23 | loop fusion | flops 979968 | bytes 1226752 | tf_op jit(solution)/shard_map/convert.15
  39.7 1.0 pad_maximum_fusion
  40.7 4.8 %all-to-all-start.1 = ((bf16[64,56,128]{2,1,0:T(8,128)(2,1)}), bf16[64,56,128]{2,1,0:T(8,128)(2,1)S(1)}, u32[]{:S(2)}, u32[]{:S(2)}) async-start(bf16[64,56,128]{2,1,0:T(8,128)(2,1)} %pad_maximum_fusion), calls=%async_computation.1 | async-start | bytes 1835008 | tf_op jit(solution)/shard_map/partial_exchange/all_to_all | solution.py:131
  46.5 14.2 %all-to-all-done.1 = bf16[64,56,128]{2,1,0:T(8,128)(2,1)S(1)} async-done(((bf16[64,56,128]{2,1,0:T(8,128)(2,1)}), bf16[64,56,128]{2,1,0:T(8,128)(2,1)S(1)}, u32[]{:S(2)}, u32[]{:S(2)}) %all-to-all-start.1) | async-done | bytes 917536 | tf_op jit(solution)/shard_map/partial_exchange/all_to_all | solution.py:131
  61.1 0.5 multiply_reduce_fusion
  62.0 3.2 %multiply_reduce_fusion.1 = (f32[4]{0:T(128)S(1)}, f32[4,1536]{1,0:T(4,128)S(1)}) fusion(bf16[4,1536]{1,0:T(4,128)(2,1)S(1)} %convert_element_type.204, bf16[1536,1536]{1,0:T(8,128)(2,1)} %param.21, bf16[4,1,1536]{2,0,1:T(4,128)(2,1)S(1)} %copy-done.3), kind=kOutput, calls=%fused_computation.80 | convolution fusion | flops 18911228 | bytes 4767760 | tf_op jit(solution)/shard_map/attention_output/dot_general | solution.py:173
  65.7 0.4 broadcast_in_dim.120
  66.1 22.4 %all_to_all.20 = bf16[128,2,1536]{2,1,0:T(2,128)(2,1)S(1)} all-to-all(bf16[128,2,1536]{2,1,0:T(2,128)(2,1)S(1)} %bitcast.75), channel_id=1, replica_groups=mesh['req'=2,'seq'=64] {'req','seq'}, dimensions={0} | all-to-all | bytes 1572864 | tf_op jit(solution)/shard_map/token_dispatch/all_to_all | solution.py:199
  88.5 1.1 convolution_maximum_fusion
  89.6 3.1 %convolution_convert_fusion = bf16[128,2,1536]{2,0,1:T(8,128)(2,1)} fusion(f32[128,2,192]{0,2,1:T(8,128)} %convolution_maximum_fusion, bf16[128,2,1536]{2,1,0:T(2,128)(2,1)S(1)} %all_to_all.20, bf16[192,1536]{1,0:T(8,128)(2,1)S(1)} %copy-done.2, bf16[1536,192]{0,1:T(8,128)(2,1)} %param.25), kind=kOutput, calls=%fused_computation | convolution fusion | flops 302481408 | bytes 2949120 | tf_op jit(solution)/shard_map/expert_quarter/sjf,fm->sjm/dot_general | solution.py:206
  92.7 2.9 %copy.83 = bf16[128,2,1536]{2,1,0:T(2,128)(2,1)} copy(bf16[128,2,1536]{2,0,1:T(8,128)(2,1)} %convolution_convert_fusion) | data formatting | bytes 1572864 | tf_op jit(solution)/shard_map/expert_quarter/convert_element_type | solution.py:208
  95.6 4.5 %all-to-all-start.3 = ((bf16[128,2,1536]{2,1,0:T(2,128)(2,1)}), bf16[128,2,1536]{2,1,0:T(2,128)(2,1)S(1)}, u32[]{:S(2)}, u32[]{:S(2)}) async-start(bf16[128,2,1536]{2,1,0:T(2,128)(2,1)} %copy.83), calls=%async_computation.3 | async-start | bytes 1572864 | tf_op jit(solution)/shard_map/expert_return/all_to_all | solution.py:211
  101.0 15.1 %all-to-all-done.3 = bf16[128,2,1536]{2,1,0:T(2,128)(2,1)S(1)} async-done(((bf16[128,2,1536]{2,1,0:T(2,128)(2,1)}), bf16[128,2,1536]{2,1,0:T(2,128)(2,1)S(1)}, u32[]{:S(2)}, u32[]{:S(2)}) %all-to-all-start.3) | async-done | bytes 786464 | tf_op jit(solution)/shard_map/expert_return/all_to_all | solution.py:211
  116.2 0.7 convert_reduce_fusion
  116.9 1.0 fusion.4
  (84 shorter events, 4.9 us)
Async XLA Ops:
  0.0 35.7 %copy-start = (bf16[64,64,256]{2,1,0:T(8,128)(2,1)S(1)}, bf16[64,64,256]{2,1,0:T(8,128)(2,1)}, u32[]{:S(2)}) copy-start(bf16[64,64,256]{2,1,0:T(8,128)(2,1)} %param.16) | copy-start | bytes 6291460
  7.4 13.5 %copy-start.6 = (s32[64]{0:T(128)S(1)}, s32[64]{0:T(128)}, u32[]{:S(2)}) copy-start(s32[64]{0:T(128)} %param.15) | copy-start | bytes 772
  8.8 26.9 %all-to-all-start = ((bf16[64,48,128]{2,1,0:T(8,128)(2,1)}), bf16[64,48,128]{2,1,0:T(8,128)(2,1)S(1)}, u32[]{:S(2)}, u32[]{:S(2)}) async-start(bf16[64,48,128]{2,1,0:T(8,128)(2,1)} %broadcast_in_dim.66), calls=%async_computation | async-start | bytes 1572864 | tf_op jit(solution)/shard_map/query_exchange/all_to_all | solution.py:82
  36.6 1.8 %copy-start.1 = (bf16[64,64,256]{2,1,0:T(8,128)(2,1)S(1)}, bf16[64,64,256]{2,1,0:T(8,128)(2,1)}, u32[]{:S(2)}) copy-start(bf16[64,64,256]{2,1,0:T(8,128)(2,1)} %param.17) | copy-start | bytes 6291460
  39.7 5.9 %copy-start.9 = (f32[12]{0:T(128)S(1)}, f32[12]{0:T(128)}, u32[]{:S(2)}) copy-start(f32[12]{0:T(128)} %param.20) | copy-start | bytes 148
  39.7 6.4 %copy-start.5 = (bf16[1536]{0:T(1024)(128)(2,1)S(1)}, bf16[1536]{0:T(1024)(128)(2,1)}, u32[]{:S(2)}) copy-start(bf16[1536]{0:T(1024)(128)(2,1)} %param.22) | copy-start | bytes 9220
  39.7 6.5 %copy-start.4 = (s32[128,4,4]{0,2,1:T(4,128)S(1)}, s32[128,4,4]{0,2,1:T(4,128)}, u32[]{:S(2)}) copy-start(s32[128,4,4]{0,2,1:T(4,128)} %param.27) | copy-start | bytes 24580
  40.7 21.2 %copy-start.3 = (bf16[4,1,1536]{2,0,1:T(4,128)(2,1)S(1)}, bf16[4,1,1536]{2,0,1:T(4,128)(2,1)}, u32[]{:S(2)}) copy-start(bf16[4,1,1536]{2,0,1:T(4,128)(2,1)} %param.14) | copy-start | bytes 36868
  40.7 19.9 %all-to-all-start.1 = ((bf16[64,56,128]{2,1,0:T(8,128)(2,1)}), bf16[64,56,128]{2,1,0:T(8,128)(2,1)S(1)}, u32[]{:S(2)}, u32[]{:S(2)}) async-start(bf16[64,56,128]{2,1,0:T(8,128)(2,1)} %pad_maximum_fusion), calls=%async_computation.1 | async-start | bytes 1835008 | tf_op jit(solution)/shard_map/partial_exchange/all_to_all | solution.py:131
  65.2 23.3 %copy-start.7 = (bf16[1536,192]{0,1:T(8,128)(2,1)S(1)}, bf16[1536,192]{0,1:T(8,128)(2,1)}, u32[]{:S(2)}) copy-start(bf16[1536,192]{0,1:T(8,128)(2,1)} %param.24) | copy-start | bytes 1769476
  66.1 23.5 %copy-start.2 = (bf16[192,1536]{1,0:T(8,128)(2,1)S(1)}, bf16[192,1536]{1,0:T(8,128)(2,1)}, u32[]{:S(2)}) copy-start(bf16[192,1536]{1,0:T(8,128)(2,1)} %param.26) | copy-start | bytes 1769476
  92.7 7.4 %copy-start.8 = (bf16[1536,32]{0,1:T(8,128)(2,1)S(1)}, bf16[1536,32]{0,1:T(8,128)(2,1)}, u32[]{:S(2)}) copy-start(bf16[1536,32]{0,1:T(8,128)(2,1)} %param.23) | copy-start | bytes 294916
  95.6 20.6 %all-to-all-start.3 = ((bf16[128,2,1536]{2,1,0:T(2,128)(2,1)}), bf16[128,2,1536]{2,1,0:T(2,128)(2,1)S(1)}, u32[]{:S(2)}, u32[]{:S(2)}) async-start(bf16[128,2,1536]{2,1,0:T(2,128)(2,1)} %copy.83), calls=%async_computation.3 | async-start | bytes 1572864 | tf_op jit(solution)/shard_map/expert_return/all_to_all | solution.py:211

commit v13 on v12

--- a/solution.py
+++ b/solution.py
@@ -199,10 +199,12 @@
         arrived = lax.all_to_all(sent_u, ("req", "seq"), 0, 0, tiled=True)
 
     with jax.named_scope("expert_quarter"):
-        hidden = (
-            jax.nn.relu(jnp.einsum("sjm,mf->sjf", arrived, w_gate, preferred_element_type=jnp.float32))
-            * jnp.einsum("sjm,mf->sjf", arrived, w_up, preferred_element_type=jnp.float32)
-        ).astype(jnp.bfloat16)
+        units = w_gate.shape[1]
+        gate_up = jnp.einsum(
+            "sjm,mf->sjf", arrived, jnp.concatenate([w_gate, w_up], axis=1),
+            preferred_element_type=jnp.float32,
+        )
+        hidden = (jax.nn.relu(gate_up[..., :units]) * gate_up[..., units:]).astype(jnp.bfloat16)
         produced = jnp.einsum(
             "sjf,fm->sjm", hidden, w_down, preferred_element_type=jnp.float32
         ).astype(jnp.bfloat16)

time: 118 us -> 117 us (level)
  blocking collectives: 22.4 us -> 0 us
  waiting for transfers between devices: 44 us -> 56.7 us
  starting transfers between devices: 21.3 us -> 28 us
  local copies, waits for them, and re-layouts: 5.25 us -> 8.33 us
  matrix products: 14.8 us -> 13 us
    all_to_all x1 -> x0, blocking collectives: 22.4 us -> none  [on_device(): arrived = lax.all_to_all(sent_u, ('req', 'seq'), 0, 0, tiled=True)]
    all_to_all x0 -> x1, waiting for transfers between devices: none -> 12.7 us  [on_device(): arrived = lax.all_to_all(sent_u, ('req', 'seq'), 0, 0, tiled=True)]
    all_to_all x0 -> x1, starting transfers between devices: none -> 6.75 us  [on_device(): arrived = lax.all_to_all(sent_u, ('req', 'seq'), 0, 0, tiled=True)]
    unnamed x20 -> x22, local copies, waits for them, and re-layouts: 0.05 us -> 3.45 us
    dot_general x1, matrix products: 3.14 us -> 0.42 us  [on_device(): jnp.einsum('sjf,fm->sjm', hidden, w_down, preferred_element_type=jnp.floa...]
    convert_element_type x1, local copies, waits for them, and re-layouts: 2.88 us -> 1.69 us  [on_device(): produced = jnp.einsum('sjf,fm->sjm', hidden, w_down, preferred_element_ty...]
  transfers between devices with their start and end apart: 3 -> 4, of which waited for: 3 -> 4; matrix products, arithmetic and copies ran while one was open for 2% -> 5% of each run, Pallas kernels for 0% -> 0%
where the time goes in v13:
time: 117 us; the launch traced here: 116 us
  waiting for transfers between devices  56.7 us (48%)
  starting transfers between devices  28 us (24%)
  matrix products  13 us (11%)
  other arithmetic  9.72 us (8%)
  local copies, waits for them, and re-layouts  8.33 us (7%)
    all_to_all x1, waiting for transfers between devices, on_device(): returned = lax.all_to_all(produced, ('req', 'seq'), 0, 0, tiled=True)  15.1 us
    all_to_all x1, waiting for transfers between devices, on_device(): every_query = lax.all_to_all(sent_q, 'seq', 0, 0, tiled=True)  14.6 us
    all_to_all x1, waiting for transfers between devices, on_device(): parts = lax.all_to_all(packed, 'seq', 0, 0, tiled=True)  14.2 us
    all_to_all x1, waiting for transfers between devices, on_device(): arrived = lax.all_to_all(sent_u, ('req', 'seq'), 0, 0, tiled=True)  12.7 us
    all_to_all x1, starting transfers between devices, on_device(): every_query = lax.all_to_all(sent_q, 'seq', 0, 0, tiled=True)  12 us
    all_to_all x1, starting transfers between devices, on_device(): arrived = lax.all_to_all(sent_u, ('req', 'seq'), 0, 0, tiled=True)  6.75 us
    all_to_all x1, starting transfers between devices, on_device(): parts = lax.all_to_all(packed, 'seq', 0, 0, tiled=True)  4.78 us
    all_to_all x1, starting transfers between devices, on_device(): returned = lax.all_to_all(produced, ('req', 'seq'), 0, 0, tiled=True)  4.54 us
  transfers between devices with their start and end apart: 4, of which 4 were waited for; matrix products, arithmetic and copies ran while one was open for 5% of the time, Pallas kernels for 0%

profile of v13, /device:TPU:1, one launch (start us, length us, event | category | flops | bytes accessed | tf_op | source)
XLA Modules:
  0.0 116.3 jit_solution(452344499230113604)
XLA Ops:
  0.0 1.4 %broadcast_add_fusion.1 = (s32[64]{0:T(128)S(1)}, s32[]{:T(128)}) fusion(s32[64]{0:T(128)} %param.15, s32[]{:T(128)S(6)} %axis_index.22), kind=kLoop, calls=%fused_computation.151 | loop fusion | flops 255 | bytes 520 | tf_op jit(solution)/shard_map/slot_attention/sub | solution.py:86
  2.1 0.7 convert_element_type.187
  2.8 0.8 fusion.44
  3.6 3.8 %fusion.47 = f32[4,2048]{1,0:T(4,128)S(1)} fusion(bf16[1536,2048]{1,0:T(8,128)(2,1)} %param.19, bf16[4,1,1536]{2,0,1:T(4,128)(2,1)} %param.14, f32[1536]{0:T(1024)S(1)} %convert_element_type.187, f32[4]{0:T(128)S(1)} %add_rsqrt_fusion.1), kind=kOutput, calls=%fused_computation.88 | convolution fusion | flops 25190400 | bytes 6342672 | tf_op jit(solution)/shard_map/qkv_projection/dot_general | solution.py:68
  7.8 1.0 broadcast_in_dim.66
  8.8 12.0 %all-to-all-start = ((bf16[64,48,128]{2,1,0:T(8,128)(2,1)}), bf16[64,48,128]{2,1,0:T(8,128)(2,1)S(1)}, u32[]{:S(2)}, u32[]{:S(2)}) async-start(bf16[64,48,128]{2,1,0:T(8,128)(2,1)} %broadcast_in_dim.66), calls=%async_computation | async-start | bytes 1572864 | tf_op jit(solution)/shard_map/query_exchange/all_to_all | solution.py:82
  21.1 14.6 %all-to-all-done = bf16[64,48,128]{2,1,0:T(8,128)(2,1)S(1)} async-done(((bf16[64,48,128]{2,1,0:T(8,128)(2,1)}), bf16[64,48,128]{2,1,0:T(8,128)(2,1)S(1)}, u32[]{:S(2)}, u32[]{:S(2)}) %all-to-all-start) | async-done | bytes 786464 | tf_op jit(solution)/shard_map/query_exchange/all_to_all | solution.py:82
  35.7 1.0 fusion.5
  36.7 1.7 %fusion.12 = (bf16[64,48,64]{2,1,0:T(8,128)(2,1)S(1)}, bf16[64,48]{1,0:T(8,128)(2,1)S(1)}) fusion(f32[64,48,64]{2,1,0:T(8,128)S(1)} %get-tuple-element.18, f32[64,48]{1,0:T(8,128)S(1)} %convert_add_fusion, s32[64,48]{1,0:T(8,128)S(1)} %broadcast_minimum_fusion, s32[64,64]{1,0:T(8,128)S(1)} %add_select_fusion), kind=kLoop, calls=%fused_computation.23 | loop fusion | flops 979968 | bytes 1226752 | tf_op jit(solution)/shard_map/convert.15
  39.7 1.0 pad_maximum_fusion
  40.7 4.8 %all-to-all-start.1 = ((bf16[64,56,128]{2,1,0:T(8,128)(2,1)}), bf16[64,56,128]{2,1,0:T(8,128)(2,1)S(1)}, u32[]{:S(2)}, u32[]{:S(2)}) async-start(bf16[64,56,128]{2,1,0:T(8,128)(2,1)} %pad_maximum_fusion), calls=%async_computation.1 | async-start | bytes 1835008 | tf_op jit(solution)/shard_map/partial_exchange/all_to_all | solution.py:131
  46.5 14.2 %all-to-all-done.1 = bf16[64,56,128]{2,1,0:T(8,128)(2,1)S(1)} async-done(((bf16[64,56,128]{2,1,0:T(8,128)(2,1)}), bf16[64,56,128]{2,1,0:T(8,128)(2,1)S(1)}, u32[]{:S(2)}, u32[]{:S(2)}) %all-to-all-start.1) | async-done | bytes 917536 | tf_op jit(solution)/shard_map/partial_exchange/all_to_all | solution.py:131
  62.0 3.2 %multiply_reduce_fusion.1 = (f32[4]{0:T(128)S(1)}, f32[4,1536]{1,0:T(4,128)S(1)}) fusion(bf16[4,1536]{1,0:T(4,128)(2,1)S(1)} %convert_element_type.204, bf16[1536,1536]{1,0:T(8,128)(2,1)} %param.21, bf16[4,1,1536]{2,0,1:T(4,128)(2,1)S(1)} %copy-done.4), kind=kOutput, calls=%fused_computation.82 | convolution fusion | flops 18911228 | bytes 4767760 | tf_op jit(solution)/shard_map/attention_output/dot_general | solution.py:173
  65.7 1.3 %broadcast_in_dim.120 = bf16[32,4,2,1536]{3,2,1,0:T(2,128)(2,1)} broadcast(bf16[32,2,1536]{2,1,0:T(2,128)(2,1)S(1)} %copy.93), dimensions={0,2,3} | broadcast | bytes 983040 | tf_op jit(solution)/shard_map/route/broadcast_in_dim | solution.py:194
  66.9 6.8 %all-to-all-start.2 = ((bf16[128,2,1536]{2,1,0:T(2,128)(2,1)}), bf16[128,2,1536]{2,1,0:T(2,128)(2,1)S(1)}, u32[]{:S(2)}, u32[]{:S(2)}) async-start(bf16[128,2,1536]{2,1,0:T(2,128)(2,1)} %bitcast.18), calls=%async_computation.2 | async-start | bytes 1572864 | tf_op jit(solution)/shard_map/token_dispatch/all_to_all | solution.py:199
  73.7 1.2 %copy.94 = bf16[1536,192]{1,0:T(8,128)(2,1)} copy(bf16[1536,192]{0,1:T(8,128)(2,1)S(1)} %copy-done.3) | data formatting | bytes 1179648 | tf_op args[10]
  74.9 2.2 %copy.95 = bf16[1536,192]{1,0:T(8,128)(2,1)} copy(bf16[1536,192]{0,1:T(8,128)(2,1)} %param.25) | data formatting | bytes 1179648 | tf_op args[11]
  77.1 12.7 %all-to-all-done.2 = bf16[128,2,1536]{2,1,0:T(2,128)(2,1)S(1)} async-done(((bf16[128,2,1536]{2,1,0:T(2,128)(2,1)}), bf16[128,2,1536]{2,1,0:T(2,128)(2,1)S(1)}, u32[]{:S(2)}, u32[]{:S(2)}) %all-to-all-start.2) | async-done | bytes 786464 | tf_op jit(solution)/shard_map/token_dispatch/all_to_all | solution.py:199
  89.9 2.0 %fusion.13 = f32[128,2,384]{2,0,1:T(8,128)S(1)} fusion(bf16[1536,192]{1,0:T(8,128)(2,1)} %copy.95, bf16[1536,192]{1,0:T(8,128)(2,1)} %copy.94, bf16[128,2,1536]{2,1,0:T(2,128)(2,1)S(1)} %all-to-all-done.2), kind=kOutput, calls=%fused_computation.25 | convolution fusion | flops 304349184 | bytes 2359296 | tf_op jit(solution)/shard_map/expert_quarter/sjm,mf->sjf/dot_general | solution.py:203
  92.3 1.7 %copy.98 = bf16[128,2,1536]{2,1,0:T(2,128)(2,1)} copy(bf16[128,2,1536]{2,0,1:T(8,128)(2,1)S(1)} %convolution_convert_fusion) | data formatting | bytes 1572864 | tf_op jit(solution)/shard_map/expert_quarter/convert_element_type | solution.py:210
  94.0 4.5 %all-to-all-start.3 = ((bf16[128,2,1536]{2,1,0:T(2,128)(2,1)}), bf16[128,2,1536]{2,1,0:T(2,128)(2,1)S(1)}, u32[]{:S(2)}, u32[]{:S(2)}) async-start(bf16[128,2,1536]{2,1,0:T(2,128)(2,1)} %copy.98), calls=%async_computation.3 | async-start | bytes 1572864 | tf_op jit(solution)/shard_map/expert_return/all_to_all | solution.py:213
  99.4 15.1 %all-to-all-done.3 = bf16[128,2,1536]{2,1,0:T(2,128)(2,1)S(1)} async-done(((bf16[128,2,1536]{2,1,0:T(2,128)(2,1)}), bf16[128,2,1536]{2,1,0:T(2,128)(2,1)S(1)}, u32[]{:S(2)}, u32[]{:S(2)}) %all-to-all-start.3) | async-done | bytes 786464 | tf_op jit(solution)/shard_map/expert_return/all_to_all | solution.py:213
  114.6 0.7 convert_reduce_fusion
  115.3 1.0 fusion.4
  (87 shorter events, 6.4 us)
Async XLA Ops:
  0.0 35.7 %copy-start = (bf16[64,64,256]{2,1,0:T(8,128)(2,1)S(1)}, bf16[64,64,256]{2,1,0:T(8,128)(2,1)}, u32[]{:S(2)}) copy-start(bf16[64,64,256]{2,1,0:T(8,128)(2,1)} %param.16) | copy-start | bytes 6291460
  7.4 13.5 %copy-start.7 = (s32[64]{0:T(128)S(1)}, s32[64]{0:T(128)}, u32[]{:S(2)}) copy-start(s32[64]{0:T(128)} %param.15) | copy-start | bytes 772
  8.8 26.9 %all-to-all-start = ((bf16[64,48,128]{2,1,0:T(8,128)(2,1)}), bf16[64,48,128]{2,1,0:T(8,128)(2,1)S(1)}, u32[]{:S(2)}, u32[]{:S(2)}) async-start(bf16[64,48,128]{2,1,0:T(8,128)(2,1)} %broadcast_in_dim.66), calls=%async_computation | async-start | bytes 1572864 | tf_op jit(solution)/shard_map/query_exchange/all_to_all | solution.py:82
  36.6 1.8 %copy-start.1 = (bf16[64,64,256]{2,1,0:T(8,128)(2,1)S(1)}, bf16[64,64,256]{2,1,0:T(8,128)(2,1)}, u32[]{:S(2)}) copy-start(bf16[64,64,256]{2,1,0:T(8,128)(2,1)} %param.17) | copy-start | bytes 6291460
  39.7 5.9 %copy-start.9 = (f32[12]{0:T(128)S(1)}, f32[12]{0:T(128)}, u32[]{:S(2)}) copy-start(f32[12]{0:T(128)} %param.20) | copy-start | bytes 148
  39.7 6.4 %copy-start.6 = (bf16[1536]{0:T(1024)(128)(2,1)S(1)}, bf16[1536]{0:T(1024)(128)(2,1)}, u32[]{:S(2)}) copy-start(bf16[1536]{0:T(1024)(128)(2,1)} %param.22) | copy-start | bytes 9220
  39.7 6.5 %copy-start.5 = (s32[128,4,4]{0,2,1:T(4,128)S(1)}, s32[128,4,4]{0,2,1:T(4,128)}, u32[]{:S(2)}) copy-start(s32[128,4,4]{0,2,1:T(4,128)} %param.27) | copy-start | bytes 24580
  40.7 21.2 %copy-start.4 = (bf16[4,1,1536]{2,0,1:T(4,128)(2,1)S(1)}, bf16[4,1,1536]{2,0,1:T(4,128)(2,1)}, u32[]{:S(2)}) copy-start(bf16[4,1,1536]{2,0,1:T(4,128)(2,1)} %param.14) | copy-start | bytes 36868
  40.7 19.9 %all-to-all-start.1 = ((bf16[64,56,128]{2,1,0:T(8,128)(2,1)}), bf16[64,56,128]{2,1,0:T(8,128)(2,1)S(1)}, u32[]{:S(2)}, u32[]{:S(2)}) async-start(bf16[64,56,128]{2,1,0:T(8,128)(2,1)} %pad_maximum_fusion), calls=%async_computation.1 | async-start | bytes 1835008 | tf_op jit(solution)/shard_map/partial_exchange/all_to_all | solution.py:131
  65.2 8.6 %copy-start.3 = (bf16[1536,192]{0,1:T(8,128)(2,1)S(1)}, bf16[1536,192]{0,1:T(8,128)(2,1)}, u32[]{:S(2)}) copy-start(bf16[1536,192]{0,1:T(8,128)(2,1)} %param.24) | copy-start | bytes 1769476
  66.9 22.9 %all-to-all-start.2 = ((bf16[128,2,1536]{2,1,0:T(2,128)(2,1)}), bf16[128,2,1536]{2,1,0:T(2,128)(2,1)S(1)}, u32[]{:S(2)}, u32[]{:S(2)}) async-start(bf16[128,2,1536]{2,1,0:T(2,128)(2,1)} %bitcast.18), calls=%async_computation.2 | async-start | bytes 1572864 | tf_op jit(solution)/shard_map/token_dispatch/all_to_all | solution.py:199
  77.1 14.8 %copy-start.2 = (bf16[192,1536]{1,0:T(8,128)(2,1)S(1)}, bf16[192,1536]{1,0:T(8,128)(2,1)}, u32[]{:S(2)}) copy-start(bf16[192,1536]{1,0:T(8,128)(2,1)} %param.26) | copy-start | bytes 1769476
  92.3 6.2 %copy-start.8 = (bf16[1536,32]{0,1:T(8,128)(2,1)S(1)}, bf16[1536,32]{0,1:T(8,128)(2,1)}, u32[]{:S(2)}) copy-start(bf16[1536,32]{0,1:T(8,128)(2,1)} %param.23) | copy-start | bytes 294916
  94.0 20.6 %all-to-all-start.3 = ((bf16[128,2,1536]{2,1,0:T(2,128)(2,1)}), bf16[128,2,1536]{2,1,0:T(2,128)(2,1)S(1)}, u32[]{:S(2)}, u32[]{:S(2)}) async-start(bf16[128,2,1536]{2,1,0:T(2,128)(2,1)} %copy.98), calls=%async_computation.3 | async-start | bytes 1572864 | tf_op jit(solution)/shard_map/expert_return/all_to_all | solution.py:213

commit v14 on v13

--- a/solution.py
+++ b/solution.py
@@ -213,11 +213,12 @@
         returned = lax.all_to_all(produced, ("req", "seq"), 0, 0, tiled=True)
 
     with jax.named_scope("expert_sum"):
-        by_expert = jnp.sum(returned.astype(jnp.float32).reshape(E, per_device, MOST, D), axis=1)
-        mix = (weight_te[:, :, None] * select).reshape(STEPS, E * MOST)
+        mix = jnp.broadcast_to(
+            (weight_te[:, :, None] * select)[:, :, None, :], (STEPS, E, per_device, MOST)
+        ).reshape(STEPS, devices * MOST)
         moe = jnp.dot(
-            mix, by_expert.reshape(E * MOST, D), precision=lax.Precision.HIGHEST,
-            preferred_element_type=jnp.float32,
+            mix, returned.reshape(devices * MOST, D).astype(jnp.float32),
+            precision=lax.Precision.HIGHEST, preferred_element_type=jnp.float32,
         )
         out = (h.astype(jnp.float32) + moe).astype(jnp.bfloat16)
     return out[:, None, :]

time: 117 us -> 119 us (1.017)
  matrix products: 13 us -> 15.2 us
  local copies, waits for them, and re-layouts: 8.33 us -> 9.64 us
    dot_general x1, matrix products: 0.96 us -> 2.21 us  [on_device(): jnp.dot(mix, returned.reshape(devices * MOST, D).astype(jnp.float32), pre...]
    unnamed x22 -> x20, local copies, waits for them, and re-layouts: 3.45 us -> 3.44 us
where the time goes in v14:
time: 119 us; the launch traced here: 118 us
  waiting for transfers between devices  55.7 us (47%)
  starting transfers between devices  28 us (24%)
  matrix products  15.2 us (13%)
  local copies, waits for them, and re-layouts  9.64 us (8%)
  other arithmetic  8.99 us (8%)
    all_to_all x1, waiting for transfers between devices, on_device(): returned = lax.all_to_all(produced, ('req', 'seq'), 0, 0, tiled=True)  15.2 us
    all_to_all x1, waiting for transfers between devices, on_device(): every_query = lax.all_to_all(sent_q, 'seq', 0, 0, tiled=True)  14.6 us
    all_to_all x1, waiting for transfers between devices, on_device(): parts = lax.all_to_all(packed, 'seq', 0, 0, tiled=True)  14.2 us
    all_to_all x1, starting transfers between devices, on_device(): every_query = lax.all_to_all(sent_q, 'seq', 0, 0, tiled=True)  12 us
    all_to_all x1, waiting for transfers between devices, on_device(): arrived = lax.all_to_all(sent_u, ('req', 'seq'), 0, 0, tiled=True)  11.7 us
    all_to_all x1, starting transfers between devices, on_device(): arrived = lax.all_to_all(sent_u, ('req', 'seq'), 0, 0, tiled=True)  6.75 us
    all_to_all x1, starting transfers between devices, on_device(): parts = lax.all_to_all(packed, 'seq', 0, 0, tiled=True)  4.78 us
    all_to_all x1, starting transfers between devices, on_device(): returned = lax.all_to_all(produced, ('req', 'seq'), 0, 0, tiled=True)  4.54 us
  transfers between devices with their start and end apart: 4, of which 4 were waited for; matrix products, arithmetic and copies ran while one was open for 5% of the time, Pallas kernels for 0%

profile of v14, /device:TPU:1, one launch (start us, length us, event | category | flops | bytes accessed | tf_op | source)
XLA Modules:
  0.0 118.0 jit_solution(12882080784189335179)
XLA Ops:
  0.0 1.4 %broadcast_add_fusion.1 = (s32[64]{0:T(128)S(1)}, s32[]{:T(128)}) fusion(s32[64]{0:T(128)} %param.15, s32[]{:T(128)S(6)} %axis_index.22), kind=kLoop, calls=%fused_computation.144 | loop fusion | flops 255 | bytes 520 | tf_op jit(solution)/shard_map/slot_attention/sub | solution.py:86
  2.8 0.8 fusion.42
  3.6 3.8 %fusion.45 = f32[4,2048]{1,0:T(4,128)S(1)} fusion(bf16[1536,2048]{1,0:T(8,128)(2,1)} %param.19, bf16[4,1,1536]{2,0,1:T(4,128)(2,1)} %param.14, f32[1536]{0:T(1024)S(1)} %convert_element_type.187, f32[4]{0:T(128)S(1)} %add_rsqrt_fusion.1), kind=kOutput, calls=%fused_computation.85 | convolution fusion | flops 25190400 | bytes 6342672 | tf_op jit(solution)/shard_map/qkv_projection/dot_general | solution.py:68
  7.8 1.0 broadcast_in_dim.68
  8.8 12.0 %all-to-all-start = ((bf16[64,48,128]{2,1,0:T(8,128)(2,1)}), bf16[64,48,128]{2,1,0:T(8,128)(2,1)S(1)}, u32[]{:S(2)}, u32[]{:S(2)}) async-start(bf16[64,48,128]{2,1,0:T(8,128)(2,1)} %broadcast_in_dim.68), calls=%async_computation | async-start | bytes 1572864 | tf_op jit(solution)/shard_map/query_exchange/all_to_all | solution.py:82
  21.1 14.6 %all-to-all-done = bf16[64,48,128]{2,1,0:T(8,128)(2,1)S(1)} async-done(((bf16[64,48,128]{2,1,0:T(8,128)(2,1)}), bf16[64,48,128]{2,1,0:T(8,128)(2,1)S(1)}, u32[]{:S(2)}, u32[]{:S(2)}) %all-to-all-start) | async-done | bytes 786464 | tf_op jit(solution)/shard_map/query_exchange/all_to_all | solution.py:82
  35.7 1.0 fusion.4
  36.7 1.7 %fusion.11 = (bf16[64,48,64]{2,1,0:T(8,128)(2,1)S(1)}, bf16[64,48]{1,0:T(8,128)(2,1)S(1)}) fusion(f32[64,48,64]{2,1,0:T(8,128)S(1)} %get-tuple-element.18, f32[64,48]{1,0:T(8,128)S(1)} %convert_add_fusion, s32[64,48]{1,0:T(8,128)S(1)} %broadcast_minimum_fusion, s32[64,64]{1,0:T(8,128)S(1)} %add_select_fusion), kind=kLoop, calls=%fused_computation.21 | loop fusion | flops 979968 | bytes 1226752 | tf_op jit(solution)/shard_map/convert.14
  39.7 1.0 pad_maximum_fusion
  40.7 4.8 %all-to-all-start.1 = ((bf16[64,56,128]{2,1,0:T(8,128)(2,1)}), bf16[64,56,128]{2,1,0:T(8,128)(2,1)S(1)}, u32[]{:S(2)}, u32[]{:S(2)}) async-start(bf16[64,56,128]{2,1,0:T(8,128)(2,1)} %pad_maximum_fusion), calls=%async_computation.1 | async-start | bytes 1835008 | tf_op jit(solution)/shard_map/partial_exchange/all_to_all | solution.py:131
  46.5 14.2 %all-to-all-done.1 = bf16[64,56,128]{2,1,0:T(8,128)(2,1)S(1)} async-done(((bf16[64,56,128]{2,1,0:T(8,128)(2,1)}), bf16[64,56,128]{2,1,0:T(8,128)(2,1)S(1)}, u32[]{:S(2)}, u32[]{:S(2)}) %all-to-all-start.1) | async-done | bytes 917536 | tf_op jit(solution)/shard_map/partial_exchange/all_to_all | solution.py:131
  62.0 3.2 %multiply_reduce_fusion.1 = (f32[4]{0:T(128)S(1)}, f32[4,1536]{1,0:T(4,128)S(1)}) fusion(bf16[4,1536]{1,0:T(4,128)(2,1)S(1)} %convert_element_type.204, bf16[1536,1536]{1,0:T(8,128)(2,1)} %param.21, bf16[4,1,1536]{2,0,1:T(4,128)(2,1)S(1)} %copy-done.4), kind=kOutput, calls=%fused_computation.79 | convolution fusion | flops 18911228 | bytes 4767760 | tf_op jit(solution)/shard_map/attention_output/dot_general | solution.py:173
  65.7 1.3 %broadcast_in_dim.127 = bf16[32,4,2,1536]{3,2,1,0:T(2,128)(2,1)} broadcast(bf16[32,2,1536]{2,1,0:T(2,128)(2,1)S(1)} %copy.81), dimensions={0,2,3} | broadcast | bytes 983040 | tf_op jit(solution)/shard_map/route/broadcast_in_dim | solution.py:194
  66.9 6.8 %all-to-all-start.2 = ((bf16[128,2,1536]{2,1,0:T(2,128)(2,1)}), bf16[128,2,1536]{2,1,0:T(2,128)(2,1)S(1)}, u32[]{:S(2)}, u32[]{:S(2)}) async-start(bf16[128,2,1536]{2,1,0:T(2,128)(2,1)} %bitcast.19), calls=%async_computation.2 | async-start | bytes 1572864 | tf_op jit(solution)/shard_map/token_dispatch/all_to_all | solution.py:199
  73.7 1.2 copy.82
  74.9 2.2 %copy.83 = bf16[1536,192]{1,0:T(8,128)(2,1)} copy(bf16[1536,192]{0,1:T(8,128)(2,1)} %param.25) | data formatting | bytes 1179648 | tf_op args[11]
  77.1 1.1 fusion.76
  78.2 11.7 %all-to-all-done.2 = bf16[128,2,1536]{2,1,0:T(2,128)(2,1)S(1)} async-done(((bf16[128,2,1536]{2,1,0:T(2,128)(2,1)}), bf16[128,2,1536]{2,1,0:T(2,128)(2,1)S(1)}, u32[]{:S(2)}, u32[]{:S(2)}) %all-to-all-start.2) | async-done | bytes 786464 | tf_op jit(solution)/shard_map/token_dispatch/all_to_all | solution.py:199
  89.9 2.0 %fusion.12 = f32[128,2,384]{2,0,1:T(8,128)S(1)} fusion(bf16[1536,192]{1,0:T(8,128)(2,1)} %copy.83, bf16[1536,192]{1,0:T(8,128)(2,1)} %copy.82, bf16[128,2,1536]{2,1,0:T(2,128)(2,1)S(1)} %all-to-all-done.2), kind=kOutput, calls=%fused_computation.23 | convolution fusion | flops 304349184 | bytes 2359296 | tf_op jit(solution)/shard_map/expert_quarter/sjm,mf->sjf/dot_general | solution.py:203
  92.3 1.7 %copy.86 = bf16[128,2,1536]{2,1,0:T(2,128)(2,1)} copy(bf16[128,2,1536]{2,0,1:T(8,128)(2,1)S(1)} %convolution_convert_fusion) | data formatting | bytes 1572864 | tf_op jit(solution)/shard_map/expert_quarter/convert_element_type | solution.py:210
  94.0 4.5 %all-to-all-start.3 = ((bf16[128,2,1536]{2,1,0:T(2,128)(2,1)}), bf16[128,2,1536]{2,1,0:T(2,128)(2,1)S(1)}, u32[]{:S(2)}, u32[]{:S(2)}) async-start(bf16[128,2,1536]{2,1,0:T(2,128)(2,1)} %copy.86), calls=%async_computation.3 | async-start | bytes 1572864 | tf_op jit(solution)/shard_map/expert_return/all_to_all | solution.py:213
  99.3 15.2 %all-to-all-done.3 = bf16[128,2,1536]{2,1,0:T(2,128)(2,1)S(1)} async-done(((bf16[128,2,1536]{2,1,0:T(2,128)(2,1)}), bf16[128,2,1536]{2,1,0:T(2,128)(2,1)S(1)}, u32[]{:S(2)}, u32[]{:S(2)}) %all-to-all-start.3) | async-done | bytes 786464 | tf_op jit(solution)/shard_map/expert_return/all_to_all | solution.py:213
  114.6 1.2 reshape.434
  115.8 2.2 %fusion.3 = bf16[4,1,1536]{2,0,1:T(4,128)(2,1)} fusion(f32[4,1536]{1,0:T(4,128)S(1)} %get-tuple-element.22, f32[4,256]{0,1:T(8,128)S(1)} %bitcast.63, bf16[256,1536]{1,0:T(8,128)(2,1)} %reshape.434), kind=kOutput, calls=%fused_computation.7 | convolution fusion | flops 18886656 | bytes 827392 | tf_op jit(solution)/shard_map/expert_sum/dot_general | solution.py:219
  (88 shorter events, 7.1 us)
Async XLA Ops:
  0.0 35.7 %copy-start = (bf16[64,64,256]{2,1,0:T(8,128)(2,1)S(1)}, bf16[64,64,256]{2,1,0:T(8,128)(2,1)}, u32[]{:S(2)}) copy-start(bf16[64,64,256]{2,1,0:T(8,128)(2,1)} %param.16) | copy-start | bytes 6291460
  7.4 13.5 %copy-start.7 = (s32[64]{0:T(128)S(1)}, s32[64]{0:T(128)}, u32[]{:S(2)}) copy-start(s32[64]{0:T(128)} %param.15) | copy-start | bytes 772
  8.8 26.9 %all-to-all-start = ((bf16[64,48,128]{2,1,0:T(8,128)(2,1)}), bf16[64,48,128]{2,1,0:T(8,128)(2,1)S(1)}, u32[]{:S(2)}, u32[]{:S(2)}) async-start(bf16[64,48,128]{2,1,0:T(8,128)(2,1)} %broadcast_in_dim.68), calls=%async_computation | async-start | bytes 1572864 | tf_op jit(solution)/shard_map/query_exchange/all_to_all | solution.py:82
  36.6 1.8 %copy-start.1 = (bf16[64,64,256]{2,1,0:T(8,128)(2,1)S(1)}, bf16[64,64,256]{2,1,0:T(8,128)(2,1)}, u32[]{:S(2)}) copy-start(bf16[64,64,256]{2,1,0:T(8,128)(2,1)} %param.17) | copy-start | bytes 6291460
  39.7 5.9 %copy-start.8 = (f32[12]{0:T(128)S(1)}, f32[12]{0:T(128)}, u32[]{:S(2)}) copy-start(f32[12]{0:T(128)} %param.20) | copy-start | bytes 148
  39.7 6.4 %copy-start.5 = (s32[128,4,4]{0,2,1:T(4,128)S(1)}, s32[128,4,4]{0,2,1:T(4,128)}, u32[]{:S(2)}) copy-start(s32[128,4,4]{0,2,1:T(4,128)} %param.27) | copy-start | bytes 24580
  39.7 6.7 %copy-start.6 = (bf16[1536]{0:T(1024)(128)(2,1)S(1)}, bf16[1536]{0:T(1024)(128)(2,1)}, u32[]{:S(2)}) copy-start(bf16[1536]{0:T(1024)(128)(2,1)} %param.22) | copy-start | bytes 9220
  40.7 21.2 %copy-start.4 = (bf16[4,1,1536]{2,0,1:T(4,128)(2,1)S(1)}, bf16[4,1,1536]{2,0,1:T(4,128)(2,1)}, u32[]{:S(2)}) copy-start(bf16[4,1,1536]{2,0,1:T(4,128)(2,1)} %param.14) | copy-start | bytes 36868
  40.7 19.9 %all-to-all-start.1 = ((bf16[64,56,128]{2,1,0:T(8,128)(2,1)}), bf16[64,56,128]{2,1,0:T(8,128)(2,1)S(1)}, u32[]{:S(2)}, u32[]{:S(2)}) async-start(bf16[64,56,128]{2,1,0:T(8,128)(2,1)} %pad_maximum_fusion), calls=%async_computation.1 | async-start | bytes 1835008 | tf_op jit(solution)/shard_map/partial_exchange/all_to_all | solution.py:131
  65.2 8.6 %copy-start.3 = (bf16[1536,192]{0,1:T(8,128)(2,1)S(1)}, bf16[1536,192]{0,1:T(8,128)(2,1)}, u32[]{:S(2)}) copy-start(bf16[1536,192]{0,1:T(8,128)(2,1)} %param.24) | copy-start | bytes 1769476
  66.9 22.9 %all-to-all-start.2 = ((bf16[128,2,1536]{2,1,0:T(2,128)(2,1)}), bf16[128,2,1536]{2,1,0:T(2,128)(2,1)S(1)}, u32[]{:S(2)}, u32[]{:S(2)}) async-start(bf16[128,2,1536]{2,1,0:T(2,128)(2,1)} %bitcast.19), calls=%async_computation.2 | async-start | bytes 1572864 | tf_op jit(solution)/shard_map/token_dispatch/all_to_all | solution.py:199
  78.2 13.7 %copy-start.2 = (bf16[192,1536]{1,0:T(8,128)(2,1)S(1)}, bf16[192,1536]{1,0:T(8,128)(2,1)}, u32[]{:S(2)}) copy-start(bf16[192,1536]{1,0:T(8,128)(2,1)} %param.26) | copy-start | bytes 1769476
  94.0 20.6 %all-to-all-start.3 = ((bf16[128,2,1536]{2,1,0:T(2,128)(2,1)}), bf16[128,2,1536]{2,1,0:T(2,128)(2,1)S(1)}, u32[]{:S(2)}, u32[]{:S(2)}) async-start(bf16[128,2,1536]{2,1,0:T(2,128)(2,1)} %copy.86), calls=%async_computation.3 | async-start | bytes 1572864 | tf_op jit(solution)/shard_map/expert_return/all_to_all | solution.py:213

commit v15 on v13

--- a/solution.py
+++ b/solution.py
@@ -200,9 +200,9 @@
 
     with jax.named_scope("expert_quarter"):
         units = w_gate.shape[1]
+        joined = lax.optimization_barrier(jnp.concatenate([w_gate, w_up], axis=1))
         gate_up = jnp.einsum(
-            "sjm,mf->sjf", arrived, jnp.concatenate([w_gate, w_up], axis=1),
-            preferred_element_type=jnp.float32,
+            "sjm,mf->sjf", arrived, joined, preferred_element_type=jnp.float32
         )
         hidden = (jax.nn.relu(gate_up[..., :units]) * gate_up[..., units:]).astype(jnp.bfloat16)
         produced = jnp.einsum(

time: 117 us -> 117 us (level)
  local copies, waits for them, and re-layouts: 8.33 us -> 4.95 us
  waiting for transfers between devices: 56.7 us -> 58.5 us
  other arithmetic: 9.72 us -> 11 us
    unnamed x22 -> x18, local copies, waits for them, and re-layouts: 3.45 us -> 0.05 us
    all_to_all x1, waiting for transfers between devices: 12.7 us -> 14.5 us  [on_device(): arrived = lax.all_to_all(sent_u, ('req', 'seq'), 0, 0, tiled=True)]
    concatenate x0 -> x1, other arithmetic: none -> 1.32 us  [on_device(): joined = lax.optimization_barrier(jnp.concatenate([w_gate, w_up], axis=1))]
  transfers between devices with their start and end apart: 4 -> 4, of which waited for: 4 -> 4; matrix products, arithmetic and copies ran while one was open for 5% -> 3% of each run, Pallas kernels for 0% -> 0%
where the time goes in v15:
time: 117 us
  waiting for transfers between devices  58.5 us (50%)
  starting transfers between devices  29 us (25%)
  matrix products  12.8 us (11%)
  other arithmetic  11 us (9%)
  local copies, waits for them, and re-layouts  4.95 us (4%)
    all_to_all x1, waiting for transfers between devices, on_device(): returned = lax.all_to_all(produced, ('req', 'seq'), 0, 0, tiled=True)  15.1 us
    all_to_all x1, waiting for transfers between devices, on_device(): every_query = lax.all_to_all(sent_q, 'seq', 0, 0, tiled=True)  14.6 us
    all_to_all x1, waiting for transfers between devices, on_device(): arrived = lax.all_to_all(sent_u, ('req', 'seq'), 0, 0, tiled=True)  14.5 us
    all_to_all x1, waiting for transfers between devices, on_device(): parts = lax.all_to_all(packed, 'seq', 0, 0, tiled=True)  14.2 us
    all_to_all x1, starting transfers between devices, on_device(): every_query = lax.all_to_all(sent_q, 'seq', 0, 0, tiled=True)  12 us
    all_to_all x1, starting transfers between devices, on_device(): arrived = lax.all_to_all(sent_u, ('req', 'seq'), 0, 0, tiled=True)  7.75 us
    all_to_all x1, starting transfers between devices, on_device(): parts = lax.all_to_all(packed, 'seq', 0, 0, tiled=True)  4.78 us
    all_to_all x1, starting transfers between devices, on_device(): returned = lax.all_to_all(produced, ('req', 'seq'), 0, 0, tiled=True)  4.54 us
  transfers between devices with their start and end apart: 4, of which 4 were waited for; matrix products, arithmetic and copies ran while one was open for 3% of the time, Pallas kernels for 0%

profile of v15, /device:TPU:1, one launch (start us, length us, event | category | flops | bytes accessed | tf_op | source)
XLA Modules:
  0.0 116.7 jit_solution(1550212058038154666)
XLA Ops:
  0.0 1.4 %broadcast_add_fusion.1 = (s32[64]{0:T(128)S(1)}, s32[]{:T(128)}) fusion(s32[64]{0:T(128)} %param.15, s32[]{:T(128)S(6)} %axis_index.22), kind=kLoop, calls=%fused_computation.150 | loop fusion | flops 255 | bytes 520 | tf_op jit(solution)/shard_map/slot_attention/sub | solution.py:86
  1.5 0.6 add_convert_fusion.2
  2.1 0.7 convert_element_type.187
  2.8 0.8 fusion.43
  3.6 3.8 %fusion.46 = f32[4,2048]{1,0:T(4,128)S(1)} fusion(bf16[1536,2048]{1,0:T(8,128)(2,1)} %param.19, bf16[4,1,1536]{2,0,1:T(4,128)(2,1)} %param.14, f32[1536]{0:T(1024)S(1)} %convert_element_type.187, f32[4]{0:T(128)S(1)} %add_rsqrt_fusion.1), kind=kOutput, calls=%fused_computation.87 | convolution fusion | flops 25190400 | bytes 6342672 | tf_op jit(solution)/shard_map/qkv_projection/dot_general | solution.py:68
  7.8 1.0 broadcast_in_dim.66
  8.8 12.0 %all-to-all-start = ((bf16[64,48,128]{2,1,0:T(8,128)(2,1)}), bf16[64,48,128]{2,1,0:T(8,128)(2,1)S(1)}, u32[]{:S(2)}, u32[]{:S(2)}) async-start(bf16[64,48,128]{2,1,0:T(8,128)(2,1)} %broadcast_in_dim.66), calls=%async_computation | async-start | bytes 1572864 | tf_op jit(solution)/shard_map/query_exchange/all_to_all | solution.py:82
  21.1 14.6 %all-to-all-done = bf16[64,48,128]{2,1,0:T(8,128)(2,1)S(1)} async-done(((bf16[64,48,128]{2,1,0:T(8,128)(2,1)}), bf16[64,48,128]{2,1,0:T(8,128)(2,1)S(1)}, u32[]{:S(2)}, u32[]{:S(2)}) %all-to-all-start) | async-done | bytes 786464 | tf_op jit(solution)/shard_map/query_exchange/all_to_all | solution.py:82
  35.7 1.0 fusion.5
  36.7 1.7 %fusion.12 = (bf16[64,48,64]{2,1,0:T(8,128)(2,1)S(1)}, bf16[64,48]{1,0:T(8,128)(2,1)S(1)}) fusion(f32[64,48,64]{2,1,0:T(8,128)S(1)} %get-tuple-element.18, f32[64,48]{1,0:T(8,128)S(1)} %convert_add_fusion, s32[64,48]{1,0:T(8,128)S(1)} %broadcast_minimum_fusion, s32[64,64]{1,0:T(8,128)S(1)} %add_select_fusion), kind=kLoop, calls=%fused_computation.23 | loop fusion | flops 979968 | bytes 1226752 | tf_op jit(solution)/shard_map/convert.15
  39.7 1.0 pad_maximum_fusion.1
  40.7 4.8 %all-to-all-start.1 = ((bf16[64,56,128]{2,1,0:T(8,128)(2,1)}), bf16[64,56,128]{2,1,0:T(8,128)(2,1)S(1)}, u32[]{:S(2)}, u32[]{:S(2)}) async-start(bf16[64,56,128]{2,1,0:T(8,128)(2,1)} %pad_maximum_fusion.1), calls=%async_computation.1 | async-start | bytes 1835008 | tf_op jit(solution)/shard_map/partial_exchange/all_to_all | solution.py:131
  46.5 14.2 %all-to-all-done.1 = bf16[64,56,128]{2,1,0:T(8,128)(2,1)S(1)} async-done(((bf16[64,56,128]{2,1,0:T(8,128)(2,1)}), bf16[64,56,128]{2,1,0:T(8,128)(2,1)S(1)}, u32[]{:S(2)}, u32[]{:S(2)}) %all-to-all-start.1) | async-done | bytes 917536 | tf_op jit(solution)/shard_map/partial_exchange/all_to_all | solution.py:131
  62.0 3.2 %multiply_reduce_fusion.1 = (f32[4]{0:T(128)S(1)}, f32[4,1536]{1,0:T(4,128)S(1)}) fusion(bf16[4,1536]{1,0:T(4,128)(2,1)S(1)} %convert_element_type.204, bf16[1536,1536]{1,0:T(8,128)(2,1)} %param.21, bf16[4,1,1536]{2,0,1:T(4,128)(2,1)S(1)} %copy-done.3), kind=kOutput, calls=%fused_computation.81 | convolution fusion | flops 18911228 | bytes 4767760 | tf_op jit(solution)/shard_map/attention_output/dot_general | solution.py:173
  65.7 1.3 %broadcast_in_dim.120 = bf16[32,4,2,1536]{3,2,1,0:T(2,128)(2,1)} broadcast(bf16[32,2,1536]{2,1,0:T(2,128)(2,1)S(1)} %copy.88), dimensions={0,2,3} | broadcast | bytes 983040 | tf_op jit(solution)/shard_map/route/broadcast_in_dim | solution.py:194
  67.0 7.7 %all-to-all-start.2 = ((bf16[128,2,1536]{2,1,0:T(2,128)(2,1)}), bf16[128,2,1536]{2,1,0:T(2,128)(2,1)}, u32[]{:S(2)}, u32[]{:S(2)}) async-start(bf16[128,2,1536]{2,1,0:T(2,128)(2,1)} %bitcast.18), calls=%async_computation.2 | async-start | bytes 1572864 | tf_op jit(solution)/shard_map/token_dispatch/all_to_all | solution.py:199
  74.7 1.3 %pad_maximum_fusion = bf16[1536,384]{0,1:T(8,128)(2,1)S(1)} fusion(bf16[1536,192]{0,1:T(8,128)(2,1)} %param.25, bf16[1536,192]{0,1:T(8,128)(2,1)} %param.24), kind=kLoop, calls=%fused_computation.24 | loop fusion | flops 2359296 | bytes 2359296 | tf_op jit(solution)/shard_map/expert_quarter/concatenate | solution.py:203
  76.0 14.5 %all-to-all-done.2 = bf16[128,2,1536]{2,1,0:T(2,128)(2,1)} async-done(((bf16[128,2,1536]{2,1,0:T(2,128)(2,1)}), bf16[128,2,1536]{2,1,0:T(2,128)(2,1)}, u32[]{:S(2)}, u32[]{:S(2)}) %all-to-all-start.2) | async-done | bytes 786464 | tf_op jit(solution)/shard_map/token_dispatch/all_to_all | solution.py:199
  90.6 1.8 %fusion.13 = f32[128,2,384]{2,0,1:T(8,128)S(1)} fusion(bf16[1536,384]{0,1:T(8,128)(2,1)S(1)} %pad_maximum_fusion, bf16[128,2,1536]{2,1,0:T(2,128)(2,1)} %all-to-all-done.2), kind=kOutput, calls=%fused_computation.25 | convolution fusion | flops 301989888 | bytes 2359296 | tf_op jit(solution)/shard_map/expert_quarter/sjm,mf->sjf/dot_general | solution.py:204
  92.8 1.7 %copy.92 = bf16[128,2,1536]{2,1,0:T(2,128)(2,1)} copy(bf16[128,2,1536]{2,0,1:T(8,128)(2,1)S(1)} %convolution_convert_fusion) | data formatting | bytes 1572864 | tf_op jit(solution)/shard_map/expert_quarter/convert_element_type | solution.py:210
  94.5 4.5 %all-to-all-start.3 = ((bf16[128,2,1536]{2,1,0:T(2,128)(2,1)}), bf16[128,2,1536]{2,1,0:T(2,128)(2,1)S(1)}, u32[]{:S(2)}, u32[]{:S(2)}) async-start(bf16[128,2,1536]{2,1,0:T(2,128)(2,1)} %copy.92), calls=%async_computation.3 | async-start | bytes 1572864 | tf_op jit(solution)/shard_map/expert_return/all_to_all | solution.py:213
  99.9 15.1 %all-to-all-done.3 = bf16[128,2,1536]{2,1,0:T(2,128)(2,1)S(1)} async-done(((bf16[128,2,1536]{2,1,0:T(2,128)(2,1)}), bf16[128,2,1536]{2,1,0:T(2,128)(2,1)S(1)}, u32[]{:S(2)}, u32[]{:S(2)}) %all-to-all-start.3) | async-done | bytes 786464 | tf_op jit(solution)/shard_map/expert_return/all_to_all | solution.py:213
  115.0 0.7 convert_reduce_fusion
  115.8 1.0 fusion.4
  (84 shorter events, 5.8 us)
Async XLA Ops:
  0.0 35.7 %copy-start = (bf16[64,64,256]{2,1,0:T(8,128)(2,1)S(1)}, bf16[64,64,256]{2,1,0:T(8,128)(2,1)}, u32[]{:S(2)}) copy-start(bf16[64,64,256]{2,1,0:T(8,128)(2,1)} %param.16) | copy-start | bytes 6291460
  7.4 13.5 %copy-start.6 = (s32[64]{0:T(128)S(1)}, s32[64]{0:T(128)}, u32[]{:S(2)}) copy-start(s32[64]{0:T(128)} %param.15) | copy-start | bytes 772
  8.8 26.9 %all-to-all-start = ((bf16[64,48,128]{2,1,0:T(8,128)(2,1)}), bf16[64,48,128]{2,1,0:T(8,128)(2,1)S(1)}, u32[]{:S(2)}, u32[]{:S(2)}) async-start(bf16[64,48,128]{2,1,0:T(8,128)(2,1)} %broadcast_in_dim.66), calls=%async_computation | async-start | bytes 1572864 | tf_op jit(solution)/shard_map/query_exchange/all_to_all | solution.py:82
  36.6 1.8 %copy-start.1 = (bf16[64,64,256]{2,1,0:T(8,128)(2,1)S(1)}, bf16[64,64,256]{2,1,0:T(8,128)(2,1)}, u32[]{:S(2)}) copy-start(bf16[64,64,256]{2,1,0:T(8,128)(2,1)} %param.17) | copy-start | bytes 6291460
  39.7 5.9 %copy-start.8 = (f32[12]{0:T(128)S(1)}, f32[12]{0:T(128)}, u32[]{:S(2)}) copy-start(f32[12]{0:T(128)} %param.20) | copy-start | bytes 148
  39.7 6.4 %copy-start.5 = (bf16[1536]{0:T(1024)(128)(2,1)S(1)}, bf16[1536]{0:T(1024)(128)(2,1)}, u32[]{:S(2)}) copy-start(bf16[1536]{0:T(1024)(128)(2,1)} %param.22) | copy-start | bytes 9220
  39.7 6.5 %copy-start.4 = (s32[128,4,4]{0,2,1:T(4,128)S(1)}, s32[128,4,4]{0,2,1:T(4,128)}, u32[]{:S(2)}) copy-start(s32[128,4,4]{0,2,1:T(4,128)} %param.27) | copy-start | bytes 24580
  40.7 21.2 %copy-start.3 = (bf16[4,1,1536]{2,0,1:T(4,128)(2,1)S(1)}, bf16[4,1,1536]{2,0,1:T(4,128)(2,1)}, u32[]{:S(2)}) copy-start(bf16[4,1,1536]{2,0,1:T(4,128)(2,1)} %param.14) | copy-start | bytes 36868
  40.7 19.9 %all-to-all-start.1 = ((bf16[64,56,128]{2,1,0:T(8,128)(2,1)}), bf16[64,56,128]{2,1,0:T(8,128)(2,1)S(1)}, u32[]{:S(2)}, u32[]{:S(2)}) async-start(bf16[64,56,128]{2,1,0:T(8,128)(2,1)} %pad_maximum_fusion.1), calls=%async_computation.1 | async-start | bytes 1835008 | tf_op jit(solution)/shard_map/partial_exchange/all_to_all | solution.py:131
  67.0 23.6 %all-to-all-start.2 = ((bf16[128,2,1536]{2,1,0:T(2,128)(2,1)}), bf16[128,2,1536]{2,1,0:T(2,128)(2,1)}, u32[]{:S(2)}, u32[]{:S(2)}) async-start(bf16[128,2,1536]{2,1,0:T(2,128)(2,1)} %bitcast.18), calls=%async_computation.2 | async-start | bytes 1572864 | tf_op jit(solution)/shard_map/token_dispatch/all_to_all | solution.py:199
  90.6 1.8 %copy-start.2 = (bf16[192,1536]{1,0:T(8,128)(2,1)S(1)}, bf16[192,1536]{1,0:T(8,128)(2,1)}, u32[]{:S(2)}) copy-start(bf16[192,1536]{1,0:T(8,128)(2,1)} %param.26) | copy-start | bytes 1769476
  92.8 6.2 %copy-start.7 = (bf16[1536,32]{0,1:T(8,128)(2,1)S(1)}, bf16[1536,32]{0,1:T(8,128)(2,1)}, u32[]{:S(2)}) copy-start(bf16[1536,32]{0,1:T(8,128)(2,1)} %param.23) | copy-start | bytes 294916
  94.5 20.6 %all-to-all-start.3 = ((bf16[128,2,1536]{2,1,0:T(2,128)(2,1)}), bf16[128,2,1536]{2,1,0:T(2,128)(2,1)S(1)}, u32[]{:S(2)}, u32[]{:S(2)}) async-start(bf16[128,2,1536]{2,1,0:T(2,128)(2,1)} %copy.92), calls=%async_computation.3 | async-start | bytes 1572864 | tf_op jit(solution)/shard_map/expert_return/all_to_all | solution.py:213

commit v16 on v10

--- a/solution.py
+++ b/solution.py
@@ -199,11 +199,12 @@
         arrived = lax.all_to_all(sent_u, ("req", "seq"), 0, 0, tiled=True)
 
     with jax.named_scope("expert_quarter"):
-        rows_in = arrived.reshape(devices * MOST, D)
-        hidden = (
-            jax.nn.relu(jnp.dot(rows_in, w_gate, preferred_element_type=jnp.float32))
-            * jnp.dot(rows_in, w_up, preferred_element_type=jnp.float32)
-        ).astype(jnp.bfloat16)
+        units = w_gate.shape[1]
+        gate_up = jnp.dot(
+            arrived.reshape(devices * MOST, D), jnp.concatenate([w_gate, w_up], axis=1),
+            preferred_element_type=jnp.float32,
+        )
+        hidden = (jax.nn.relu(gate_up[..., :units]) * gate_up[..., units:]).astype(jnp.bfloat16)
         produced = (
             jnp.dot(hidden, w_down, preferred_element_type=jnp.float32)
             .astype(jnp.bfloat16)

time: 122 us -> 116 us (0.951)
  local copies, waits for them, and re-layouts: 7.52 us -> 4.7 us
  matrix products: 15.3 us -> 13.1 us
    dot_general x1, matrix products: 3.27 us -> 0.42 us  [on_device(): jnp.dot(hidden, w_down, preferred_element_type=jnp.float32)]
    reshape x1, local copies, waits for them, and re-layouts: 2.9 us -> 1.17 us  [on_device(): produced = jnp.dot(hidden, w_down, preferred_element_type=jnp.float32).as...]
where the time goes in v16:
time: 116 us
  waiting for transfers between devices  44 us (38%)
  blocking collectives  22.4 us (19%)
  starting transfers between devices  21.3 us (18%)
  matrix products  13.1 us (11%)
  other arithmetic  9.72 us (8%)
  local copies, waits for them, and re-layouts  4.7 us (4%)
    all_to_all x1, blocking collectives, on_device(): arrived = lax.all_to_all(sent_u, ('req', 'seq'), 0, 0, tiled=True)  22.4 us
    all_to_all x1, waiting for transfers between devices, on_device(): returned = lax.all_to_all(produced, ('req', 'seq'), 0, 0, tiled=True)  15.1 us
    all_to_all x1, waiting for transfers between devices, on_device(): every_query = lax.all_to_all(sent_q, 'seq', 0, 0, tiled=True)  14.6 us
    all_to_all x1, waiting for transfers between devices, on_device(): parts = lax.all_to_all(packed, 'seq', 0, 0, tiled=True)  14.2 us
    all_to_all x1, starting transfers between devices, on_device(): every_query = lax.all_to_all(sent_q, 'seq', 0, 0, tiled=True)  12 us
    all_to_all x1, starting transfers between devices, on_device(): parts = lax.all_to_all(packed, 'seq', 0, 0, tiled=True)  4.78 us
    all_to_all x1, starting transfers between devices, on_device(): returned = lax.all_to_all(produced, ('req', 'seq'), 0, 0, tiled=True)  4.53 us
    dot_general x1, matrix products, on_device(): proj = jnp.dot(a, w_qkv, preferred_element_type=jnp.float32)  3.76 us
  transfers between devices with their start and end apart: 3, of which 3 were waited for; matrix products, arithmetic and copies ran while one was open for 2% of the time, Pallas kernels for 0%

profile of v16, /device:TPU:1, one launch (start us, length us, event | category | flops | bytes accessed | tf_op | source)
XLA Modules:
  0.0 115.7 jit_solution(14381038506240520416)
XLA Ops:
  0.0 1.4 %broadcast_add_fusion.1 = (s32[64]{0:T(128)S(1)}, s32[]{:T(128)}) fusion(s32[64]{0:T(128)} %param.15, s32[]{:T(128)S(6)} %axis_index.22), kind=kLoop, calls=%fused_computation.149 | loop fusion | flops 255 | bytes 520 | tf_op jit(solution)/shard_map/slot_attention/sub | solution.py:86
  1.5 0.6 add_convert_fusion.2
  2.1 0.7 convert_element_type.187
  2.8 0.8 fusion.43
  3.6 3.8 %fusion.46 = f32[4,2048]{1,0:T(4,128)S(1)} fusion(bf16[1536,2048]{1,0:T(8,128)(2,1)} %param.19, bf16[4,1,1536]{2,0,1:T(4,128)(2,1)} %param.14, f32[1536]{0:T(1024)S(1)} %convert_element_type.187, f32[4]{0:T(128)S(1)} %add_rsqrt_fusion.1), kind=kOutput, calls=%fused_computation.86 | convolution fusion | flops 25190400 | bytes 6342672 | tf_op jit(solution)/shard_map/qkv_projection/dot_general | solution.py:68
  7.8 1.0 broadcast_in_dim.66
  8.8 12.0 %all-to-all-start = ((bf16[64,48,128]{2,1,0:T(8,128)(2,1)}), bf16[64,48,128]{2,1,0:T(8,128)(2,1)S(1)}, u32[]{:S(2)}, u32[]{:S(2)}) async-start(bf16[64,48,128]{2,1,0:T(8,128)(2,1)} %broadcast_in_dim.66), calls=%async_computation | async-start | bytes 1572864 | tf_op jit(solution)/shard_map/query_exchange/all_to_all | solution.py:82
  21.1 14.6 %all-to-all-done = bf16[64,48,128]{2,1,0:T(8,128)(2,1)S(1)} async-done(((bf16[64,48,128]{2,1,0:T(8,128)(2,1)}), bf16[64,48,128]{2,1,0:T(8,128)(2,1)S(1)}, u32[]{:S(2)}, u32[]{:S(2)}) %all-to-all-start) | async-done | bytes 786464 | tf_op jit(solution)/shard_map/query_exchange/all_to_all | solution.py:82
  35.7 1.0 fusion.5
  36.7 1.7 %fusion.12 = (bf16[64,48,64]{2,1,0:T(8,128)(2,1)S(1)}, bf16[64,48]{1,0:T(8,128)(2,1)S(1)}) fusion(f32[64,48,64]{2,1,0:T(8,128)S(1)} %get-tuple-element.18, f32[64,48]{1,0:T(8,128)S(1)} %convert_add_fusion, s32[64,48]{1,0:T(8,128)S(1)} %broadcast_minimum_fusion, s32[64,64]{1,0:T(8,128)S(1)} %add_select_fusion), kind=kLoop, calls=%fused_computation.23 | loop fusion | flops 979968 | bytes 1226752 | tf_op jit(solution)/shard_map/convert.15
  39.7 1.0 pad_maximum_fusion
  40.7 4.8 %all-to-all-start.1 = ((bf16[64,56,128]{2,1,0:T(8,128)(2,1)}), bf16[64,56,128]{2,1,0:T(8,128)(2,1)S(1)}, u32[]{:S(2)}, u32[]{:S(2)}) async-start(bf16[64,56,128]{2,1,0:T(8,128)(2,1)} %pad_maximum_fusion), calls=%async_computation.1 | async-start | bytes 1835008 | tf_op jit(solution)/shard_map/partial_exchange/all_to_all | solution.py:131
  46.5 14.2 %all-to-all-done.1 = bf16[64,56,128]{2,1,0:T(8,128)(2,1)S(1)} async-done(((bf16[64,56,128]{2,1,0:T(8,128)(2,1)}), bf16[64,56,128]{2,1,0:T(8,128)(2,1)S(1)}, u32[]{:S(2)}, u32[]{:S(2)}) %all-to-all-start.1) | async-done | bytes 917536 | tf_op jit(solution)/shard_map/partial_exchange/all_to_all | solution.py:131
  61.1 0.5 multiply_reduce_fusion
  62.0 3.2 %multiply_reduce_fusion.1 = (f32[4]{0:T(128)S(1)}, f32[4,1536]{1,0:T(4,128)S(1)}) fusion(bf16[4,1536]{1,0:T(4,128)(2,1)S(1)} %convert_element_type.204, bf16[1536,1536]{1,0:T(8,128)(2,1)} %param.21, bf16[4,1,1536]{2,0,1:T(4,128)(2,1)S(1)} %copy-done.3), kind=kOutput, calls=%fused_computation.80 | convolution fusion | flops 18911228 | bytes 4767760 | tf_op jit(solution)/shard_map/attention_output/dot_general | solution.py:173
  66.1 22.4 %all_to_all.20 = bf16[128,2,1536]{2,1,0:T(2,128)(2,1)S(1)} all-to-all(bf16[128,2,1536]{2,1,0:T(2,128)(2,1)S(1)} %bitcast.67), channel_id=1, replica_groups=mesh['req'=2,'seq'=64] {'req','seq'}, dimensions={0} | all-to-all | bytes 1572864 | tf_op jit(solution)/shard_map/token_dispatch/all_to_all | solution.py:199
  88.5 1.2 %reshape.436 = bf16[256,1536]{1,0:T(8,128)(2,1)} reshape(bf16[128,2,1536]{2,1,0:T(2,128)(2,1)S(1)} %all_to_all.20) | data formatting | bytes 1572864 | tf_op jit(solution)/shard_map/expert_quarter/reshape | solution.py:204
  89.7 2.1 %fusion.13 = f32[256,384]{1,0:T(8,128)S(1)} fusion(bf16[256,1536]{1,0:T(8,128)(2,1)} %reshape.436, bf16[1536,192]{0,1:T(8,128)(2,1)} %param.25, bf16[1536,192]{0,1:T(8,128)(2,1)} %param.24), kind=kOutput, calls=%fused_computation.24 | convolution fusion | flops 304349184 | bytes 2359296 | tf_op jit(solution)/shard_map/expert_quarter/dot_general | solution.py:203
  91.8 0.4 convolution_convert_fusion
  92.2 1.2 %reshape.437 = bf16[128,2,1536]{2,1,0:T(2,128)(2,1)} reshape(bf16[256,1536]{1,0:T(8,128)(2,1)S(1)} %convolution_convert_fusion) | data formatting | bytes 1572864 | tf_op jit(solution)/shard_map/expert_quarter/reshape | solution.py:211
  93.4 4.5 %all-to-all-start.3 = ((bf16[128,2,1536]{2,1,0:T(2,128)(2,1)}), bf16[128,2,1536]{2,1,0:T(2,128)(2,1)S(1)}, u32[]{:S(2)}, u32[]{:S(2)}) async-start(bf16[128,2,1536]{2,1,0:T(2,128)(2,1)} %reshape.437), calls=%async_computation.3 | async-start | bytes 1572864 | tf_op jit(solution)/shard_map/expert_return/all_to_all | solution.py:215
  98.8 15.1 %all-to-all-done.3 = bf16[128,2,1536]{2,1,0:T(2,128)(2,1)S(1)} async-done(((bf16[128,2,1536]{2,1,0:T(2,128)(2,1)}), bf16[128,2,1536]{2,1,0:T(2,128)(2,1)S(1)}, u32[]{:S(2)}, u32[]{:S(2)}) %all-to-all-start.3) | async-done | bytes 786464 | tf_op jit(solution)/shard_map/expert_return/all_to_all | solution.py:215
  114.0 0.7 convert_reduce_fusion
  114.7 1.0 fusion.4
  (83 shorter events, 5.3 us)
Async XLA Ops:
  0.0 35.7 %copy-start = (bf16[64,64,256]{2,1,0:T(8,128)(2,1)S(1)}, bf16[64,64,256]{2,1,0:T(8,128)(2,1)}, u32[]{:S(2)}) copy-start(bf16[64,64,256]{2,1,0:T(8,128)(2,1)} %param.16) | copy-start | bytes 6291460
  7.4 13.5 %copy-start.6 = (s32[64]{0:T(128)S(1)}, s32[64]{0:T(128)}, u32[]{:S(2)}) copy-start(s32[64]{0:T(128)} %param.15) | copy-start | bytes 772
  8.8 26.9 %all-to-all-start = ((bf16[64,48,128]{2,1,0:T(8,128)(2,1)}), bf16[64,48,128]{2,1,0:T(8,128)(2,1)S(1)}, u32[]{:S(2)}, u32[]{:S(2)}) async-start(bf16[64,48,128]{2,1,0:T(8,128)(2,1)} %broadcast_in_dim.66), calls=%async_computation | async-start | bytes 1572864 | tf_op jit(solution)/shard_map/query_exchange/all_to_all | solution.py:82
  36.6 1.8 %copy-start.1 = (bf16[64,64,256]{2,1,0:T(8,128)(2,1)S(1)}, bf16[64,64,256]{2,1,0:T(8,128)(2,1)}, u32[]{:S(2)}) copy-start(bf16[64,64,256]{2,1,0:T(8,128)(2,1)} %param.17) | copy-start | bytes 6291460
  39.7 5.9 %copy-start.8 = (f32[12]{0:T(128)S(1)}, f32[12]{0:T(128)}, u32[]{:S(2)}) copy-start(f32[12]{0:T(128)} %param.20) | copy-start | bytes 148
  39.7 6.4 %copy-start.5 = (bf16[1536]{0:T(1024)(128)(2,1)S(1)}, bf16[1536]{0:T(1024)(128)(2,1)}, u32[]{:S(2)}) copy-start(bf16[1536]{0:T(1024)(128)(2,1)} %param.22) | copy-start | bytes 9220
  39.7 6.5 %copy-start.4 = (s32[128,4,4]{0,2,1:T(4,128)S(1)}, s32[128,4,4]{0,2,1:T(4,128)}, u32[]{:S(2)}) copy-start(s32[128,4,4]{0,2,1:T(4,128)} %param.27) | copy-start | bytes 24580
  40.7 21.2 %copy-start.3 = (bf16[4,1,1536]{2,0,1:T(4,128)(2,1)S(1)}, bf16[4,1,1536]{2,0,1:T(4,128)(2,1)}, u32[]{:S(2)}) copy-start(bf16[4,1,1536]{2,0,1:T(4,128)(2,1)} %param.14) | copy-start | bytes 36868
  40.7 19.9 %all-to-all-start.1 = ((bf16[64,56,128]{2,1,0:T(8,128)(2,1)}), bf16[64,56,128]{2,1,0:T(8,128)(2,1)S(1)}, u32[]{:S(2)}, u32[]{:S(2)}) async-start(bf16[64,56,128]{2,1,0:T(8,128)(2,1)} %pad_maximum_fusion), calls=%async_computation.1 | async-start | bytes 1835008 | tf_op jit(solution)/shard_map/partial_exchange/all_to_all | solution.py:131
  89.7 2.1 %copy-start.2 = (bf16[192,1536]{1,0:T(8,128)(2,1)S(1)}, bf16[192,1536]{1,0:T(8,128)(2,1)}, u32[]{:S(2)}) copy-start(bf16[192,1536]{1,0:T(8,128)(2,1)} %param.26) | copy-start | bytes 1769476
  92.2 5.7 %copy-start.7 = (bf16[1536,32]{0,1:T(8,128)(2,1)S(1)}, bf16[1536,32]{0,1:T(8,128)(2,1)}, u32[]{:S(2)}) copy-start(bf16[1536,32]{0,1:T(8,128)(2,1)} %param.23) | copy-start | bytes 294916
  93.4 20.5 %all-to-all-start.3 = ((bf16[128,2,1536]{2,1,0:T(2,128)(2,1)}), bf16[128,2,1536]{2,1,0:T(2,128)(2,1)S(1)}, u32[]{:S(2)}, u32[]{:S(2)}) async-start(bf16[128,2,1536]{2,1,0:T(2,128)(2,1)} %reshape.437), calls=%async_computation.3 | async-start | bytes 1572864 | tf_op jit(solution)/shard_map/expert_return/all_to_all | solution.py:215
